TPU v7x, 128 devices: a whole 4x4x4 slice. The times are simulated.
128 devices in a mesh: seq: 16 (over z_lo, y, core), head: 8 (over z_hi, x).
Axes of the slice: x: 4, y: 4, z: 4 (z_hi: 2, z_lo: 2; z = z_hi * 2 + z_lo), core: 2. Of those that a mesh axis runs over, the one named last changes fastest.
Arguments:
- inputs: bfloat16 [16384, 5376], P(('seq', 'head')), may hold values from -18 to 18
- queries: bfloat16 [16384, 4096], P('seq', 'head'), may hold values from -12 to 12
- key_rows: bfloat16 [16384, 2048], P('seq', 'head'), may hold values from -12 to 12
- values: bfloat16 [16384, 2048], P('seq', 'head'), may hold values from -6 to 6
- out_grad: bfloat16 [16384, 4096], P('seq', 'head'), may hold values from -6 to 6
- band_start: int32 [16384], P('seq'), may hold values from 0 to 16383, as said below
- owners: int32 [8, 6], replicated, may hold values from 0 to 15, as said below
Outputs:
- left_stat: float32 [16, 8, 1024, 1024], P('seq', 'head')
- right_stat: float32 [16, 8, 1024, 1024], P('seq', 'head')
Inputs may be any that keep to these rules, and one draw needn't show every extreme that they name: band_start[i] lies between i - 1023 and i, and never decreases with i. `owners`: the 6 entries of a row differ.
All inputs are finite; a program needn't handle non-finite values.
Results may differ from a plain program's by a relative error of at most 0.015.
Values may be sent and summed in bfloat16 or wider, within the bound.
No kernel may reach another device: no remote copies, remote signals or barrier semaphores. Data moves between devices by JAX's collectives and lax.ppermute only.
A program may use at most 128 MiB of HBM per device.

v0:
```python
import jax
import jax.numpy as jnp
from jax import lax
from jax.sharding import PartitionSpec as P

D = 5376
HD = 128
KV_DEV = 2
QPK = 2
WINDOW = 1024
BLOCK = 1024
NBLK = 6


score_scale = 168.0 ** (-0.5)
rotary_frequency_base = 10000.0
neg_large = -1e30


def shifted(value, axis, steps):
    count = lax.axis_size(axis)
    initial, last = (max(0, -steps), min(count, count - steps))
    return lax.ppermute(value, axis, [(source, source + steps) for source in range(initial, last)])


def rope_tables(positions, head_size):
    half_size = head_size // 2
    frequency = jnp.power(
        rotary_frequency_base, -2.0 * jnp.arange(half_size, dtype=jnp.float32) / head_size
    )
    angles = positions.astype(jnp.float32)[:, None] * frequency[None, :]
    cosine_table = jnp.concatenate([jnp.cos(angles), jnp.cos(angles)], 1)
    sine_table = jnp.concatenate([jnp.sin(angles), jnp.sin(angles)], 1)
    return (cosine_table, sine_table)


def unrotate(gradient, cosine_table, sine_table):
    half_size = gradient.shape[-1] // 2
    scaled = gradient * sine_table
    turned = jnp.concatenate([-scaled[..., half_size:], scaled[..., :half_size]], -1)
    return gradient * cosine_table - turned


def arrange_features(rows, seq_count):
    full_blocks = D // BLOCK
    piece = BLOCK // seq_count
    tail_piece = (D - full_blocks * BLOCK) // seq_count
    count = rows.shape[0]
    main = rows[:, : full_blocks * BLOCK].reshape(count, full_blocks, seq_count, piece)
    main = main.transpose(0, 2, 1, 3).reshape(count, seq_count, full_blocks * piece)
    tail = rows[:, full_blocks * BLOCK :].reshape(count, seq_count, tail_piece)
    return jnp.concatenate([main, tail], 2).reshape(count, D)


def owned_block(arranged, owner_row, block_pick, seq_count):
    full_blocks = D // BLOCK
    piece = BLOCK // seq_count
    tail_piece = (D - full_blocks * BLOCK) // seq_count
    columns = arranged.shape[1]
    mine = lax.psum_scatter(arranged, "seq", scatter_dimension=0, tiled=True)
    mine = jnp.concatenate(
        [mine, jnp.zeros((NBLK * piece - mine.shape[0], columns), mine.dtype)], 0
    ).reshape(NBLK, piece, columns)
    destinations = jnp.arange(seq_count, dtype=jnp.int32)
    dest_block = jnp.sum(
        jnp.where(
            owner_row[None, :] == destinations[:, None],
            jnp.arange(NBLK, dtype=jnp.int32)[None, :],
            0,
        ),
        1,
    )
    send = jnp.take(mine, dest_block, axis=0)
    received = lax.all_to_all(send, "seq", 0, 0, tiled=False)
    main_block = received.reshape(BLOCK, columns)
    tail_block = jnp.concatenate(
        [
            received[:, :tail_piece].reshape(tail_piece * seq_count, columns),
            jnp.zeros((BLOCK - tail_piece * seq_count, columns), received.dtype),
        ],
        0,
    )
    return jnp.where(block_pick == full_blocks, tail_block, main_block)

def per_device(inputs, queries, key_rows, values, out_grad, band_start, owners):
    tok_rows = queries.shape[0]
    seq_count = lax.axis_size("seq")
    seq_index = lax.axis_index("seq")
    group_index = lax.axis_index("head")
    tokens_all = tok_rows * seq_count
    earlier_keys, earlier_values = shifted((key_rows, values), "seq", 1)
    gathered_key_rows = jnp.concatenate([earlier_keys, key_rows], 0).reshape(
        2 * tok_rows, KV_DEV, HD
    )
    value_all = jnp.concatenate([earlier_values, values], 0).reshape(2 * tok_rows, KV_DEV, HD)
    query_heads = queries.reshape(tok_rows, KV_DEV, QPK, HD)
    out_heads = out_grad.reshape(tok_rows, KV_DEV, QPK, HD)
    block_rows = min(512, tok_rows)
    span_rows = block_rows + WINDOW
    block_count = tok_rows // block_rows

    def one_block(block_index, state_pair):
        grad_query, grad_keys, grad_values = state_pair
        offset = block_index * block_rows
        query_part = lax.dynamic_slice_in_dim(query_heads, offset, block_rows, 0)
        out_part = lax.dynamic_slice_in_dim(out_heads, offset, block_rows, 0)
        key_start = tok_rows + offset - WINDOW
        key_part = lax.dynamic_slice_in_dim(gathered_key_rows, key_start, span_rows, 0)
        value_part = lax.dynamic_slice_in_dim(value_all, key_start, span_rows, 0)
        band_part = lax.dynamic_slice_in_dim(band_start, offset, block_rows, 0)
        query_pos = seq_index * tok_rows + offset + jnp.arange(block_rows, dtype=jnp.int32)
        key_pos = seq_index * tok_rows + offset - WINDOW + jnp.arange(span_rows, dtype=jnp.int32)
        allowed = (key_pos[None, :] >= band_part[:, None]) & (
            key_pos[None, :] <= query_pos[:, None]
        )
        attention_logits = (
            jnp.einsum("qgrh,kgh->grqk", query_part, key_part, preferred_element_type=jnp.float32)
            * score_scale
        )
        masked = jnp.where(allowed, attention_logits, neg_large)
        row_top = jnp.max(masked, -1, keepdims=True)
        exponent = jnp.where(allowed, jnp.exp(masked - row_top), 0.0)
        attend = exponent / jnp.sum(exponent, -1, keepdims=True)
        attend_low = attend.astype(jnp.bfloat16)
        grad_attend = jnp.einsum(
            "qgrh,kgh->grqk", out_part, value_part, preferred_element_type=jnp.float32
        )
        row_dot = jnp.sum(attend * grad_attend, -1, keepdims=True)
        grad_score = (attend * (grad_attend - row_dot) * score_scale).astype(jnp.bfloat16)
        query_term = jnp.einsum(
            "grqk,kgh->qgrh", grad_score, key_part, preferred_element_type=jnp.float32
        )
        key_term = jnp.einsum(
            "grqk,qgrh->kgh", grad_score, query_part, preferred_element_type=jnp.float32
        )
        value_term = jnp.einsum(
            "grqk,qgrh->kgh", attend_low, out_part, preferred_element_type=jnp.float32
        )
        grad_query = lax.dynamic_update_slice_in_dim(grad_query, query_term, offset, 0)
        grad_keys = lax.dynamic_update_slice_in_dim(
            grad_keys,
            lax.dynamic_slice_in_dim(grad_keys, key_start, span_rows, 0) + key_term,
            key_start,
            0,
        )
        grad_values = lax.dynamic_update_slice_in_dim(
            grad_values,
            lax.dynamic_slice_in_dim(grad_values, key_start, span_rows, 0) + value_term,
            key_start,
            0,
        )
        return (grad_query, grad_keys, grad_values)

    start_state = (
        jnp.zeros((tok_rows, KV_DEV, QPK, HD), jnp.float32),
        jnp.zeros((2 * tok_rows, KV_DEV, HD), jnp.float32),
        jnp.zeros((2 * tok_rows, KV_DEV, HD), jnp.float32),
    )
    grad_query, grad_keys, grad_values = lax.fori_loop(0, block_count, one_block, start_state)
    rim_keys, rim_values = (
        shifted(grad_keys[:tok_rows].astype(jnp.bfloat16), "seq", -1).astype(jnp.float32),
        shifted(grad_values[:tok_rows].astype(jnp.bfloat16), "seq", -1).astype(jnp.float32),
    )
    own_keys = grad_keys[tok_rows:] + rim_keys
    own_values = grad_values[tok_rows:] + rim_values
    positions = seq_index * tok_rows + jnp.arange(tok_rows, dtype=jnp.int32)
    cosine_table, sine_table = rope_tables(positions, HD)
    query_pre = unrotate(
        grad_query.reshape(tok_rows, KV_DEV * QPK, HD),
        cosine_table[:, None, :],
        sine_table[:, None, :],
    )
    key_pre = unrotate(own_keys, cosine_table[:, None, :], sine_table[:, None, :])
    column_grads = jnp.concatenate(
        [
            query_pre.reshape(tok_rows, KV_DEV * QPK * HD),
            key_pre.reshape(tok_rows, KV_DEV * HD),
            own_values.reshape(tok_rows, KV_DEV * HD),
        ],
        1,
    ).astype(jnp.bfloat16)
    column_count = column_grads.shape[1]
    partial_sum = lax.dot_general(
        lax.all_gather(arrange_features(inputs, seq_count), "head", axis=0, tiled=True),
        column_grads,
        (((0,), (0,)), ((), ())),
        preferred_element_type=jnp.float32,
    )
    owner_row = lax.dynamic_index_in_dim(owners, group_index, 0, keepdims=False)
    is_mine = owner_row == seq_index
    block_pick = jnp.sum(jnp.where(is_mine, jnp.arange(NBLK, dtype=jnp.int32), 0))
    block_part = owned_block(partial_sum.astype(jnp.bfloat16), owner_row, block_pick, seq_count)
    def gram_pair(part_rows):
        left_value = (
            lax.dot_general(
                part_rows, part_rows, (((1,), (1,)), ((), ())), preferred_element_type=jnp.float32
            )
            / tokens_all
        )
        right_value = (
            lax.dot_general(
                part_rows, part_rows, (((0,), (0,)), ((), ())), preferred_element_type=jnp.float32
            )
            / tokens_all
        )
        return (left_value, right_value)

    def nothing(part_rows):
        return (
            jnp.zeros((BLOCK, BLOCK), jnp.float32),
            jnp.zeros((column_count, column_count), jnp.float32),
        )

    left_stat, right_stat = lax.cond(jnp.any(is_mine), gram_pair, nothing, block_part)
    return (left_stat[None, None], right_stat[None, None])


def solution(mesh):
    in_specs = (
        P(("seq", "head"), None),
        P("seq", "head"),
        P("seq", "head"),
        P("seq", "head"),
        P("seq", "head"),
        P("seq"),
        P(),
    )
    out_specs = (P("seq", "head", None, None), P("seq", "head", None, None))
    return jax.shard_map(
        per_device, mesh=mesh, in_specs=in_specs, out_specs=out_specs, check_vma=False
    )
```

profile of v0, /device:TPU:0, one launch (start us, length us, event | category | flops | bytes accessed | tf_op | source)
XLA Modules:
  0.0 346.7 jit_solution(16453392193887728162)
XLA Ops:
  7.2 1.3 slice-done
  8.5 1.4 copy.73
  9.9 1.4 copy.45
  11.5 1.2 pad_maximum_fusion.1
  12.9 2.1 collective-permute-start
  15.0 1.2 copy.50
  16.3 3.6 %collective-permute-start.1 = (bf16[1024,256]{0,1:T(8,128)(2,1)S(1)}, bf16[1024,256]{0,1:T(8,128)(2,1)S(1)}, u32[]{:S(2)}, u32[]{:S(2)}) collective-permute-start(bf16[1024,256]{0,1:T(8,128)(2,1)S(1)} %copy.50), channel_id=1, source_target_pairs={{0,8},{8,16},{16,24},{24,32},{32,40},{40,48},{48,56},{56,64},{64,7... | collective-permute-start | bytes 1572872 | tf_op jit(solution)/shard_map/ppermute | solution.py:23
  19.9 1.0 multiply_cosine_fusion
  20.9 1.3 copy.49
  22.2 2.3 copy.52
  24.5 0.8 pad_maximum_fusion.5
  25.4 0.9 pad_maximum_fusion.4
  26.2 2.2 pad_maximum_fusion.2
  28.5 1.6 broadcast.113
  30.1 1.6 broadcast.113.clone
  31.7 1.6 broadcast_in_dim.120
  33.3 138.9 %while.22 = (s32[]{:T(128)}, f32[1024,2,2,128]{0,3,2,1:T(8,128)}, f32[2048,2,128]{0,2,1:T(8,128)}, f32[2048,2,128]{0,2,1:T(8,128)}, bf16[2048,2,128]{0,2,1:T(8,1...) while((s32[]{:T(128)}, f32[1024,2,2,128]{0,3,2,1:T(8,128)}, ...), condition=%wide.region_6.7_spmd, body=%wide.region_2.6_spmd.sunk | while | flops 4095748608 | bytes 186194320 | solution.py:159
  34.0 11.7 %fusion.114 = (f32[2,2,512]{2,1,0:T(2,128)S(1)}, f32[2,2,512,1536]{2,3,1,0:T(8,128)}) fusion(pred[512,1536]{0,1:T(8,128)(4,1)S(1)} %compare_and_fusion.3, bf16[2048,2,128]{0,2,1:T(8,128)(2,1)} %get-tuple-element.532, s32[]{:T(128)S(6)} %select_n.140, bf16[1024,2,2,128]{0,3,2,1:T(8,128)(2,1)} %get-tuple-element.535, s32[]{:T(128)S(6)} %select_n.139), kind=kOutput, calls=%fused_computation.104.clone.1 | convolution fusion | flops 821036544 | bytes 15474696 | tf_op jit(solution)/shard_map/while/body/eval_jaxpr/sub | solution.py:122
  45.8 7.6 %fusion.113 = f32[2,1536,512,2]{2,1,3,0:T(8,128)} fusion(bf16[2048,2,128]{0,2,1:T(8,128)(2,1)S(1)} %get-tuple-element.536, s32[]{:T(128)S(6)} %select_n.140, bf16[1024,2,2,128]{0,3,2,1:T(8,128)(2,1)} %get-tuple-element.537, s32[]{:T(128)S(6)} %select_n.139), kind=kOutput, calls=%fused_computation.34.clone.1 | convolution fusion | flops 805306368 | bytes 13893640 | tf_op jit(solution)/shard_map/while/body/eval_jaxpr/qgrh,kgh->grqk/dot_general | solution.py:125
  53.3 20.2 %fusion.116 = f32[2048,2,128]{0,2,1:T(8,128)S(1)} fusion(f32[2048,2,128]{0,2,1:T(8,128)S(1)} %copy-done.3, s32[]{:T(128)S(6)} %select_n.140, f32[2,1536,512,2]{2,1,3,0:T(8,128)} %fusion.113, bf16[1024,2,2,128]{0,3,2,1:T(8,128)(2,1)} %get-tuple-element.535, s32[]{:T(128)S(6)} %select_n.139, f32[2,2,512,1536]{2,3,1,0:T(8,128)} %get-tuple-element.494, ...), kind=kOutput, calls=%fused_computation.26.clone.1 | convolution fusion | flops 827723264 | bytes 54018056 | tf_op jit(solution)/shard_map/while/body/eval_jaxpr/grqk,qgrh->kgh/dot_general | solution.py:133
  73.5 1.3 copy-done.4
  74.9 8.9 %fusion.117 = f32[2048,2,128]{0,2,1:T(8,128)} fusion(f32[2048,2,128]{0,2,1:T(8,128)} %get-tuple-element.515, s32[]{:T(128)S(6)} %select_n.140, bf16[1024,2,2,128]{0,3,2,1:T(8,128)(2,1)} %get-tuple-element.537, s32[]{:T(128)S(6)} %select_n.139, f32[2,2,512,1536]{2,3,1,0:T(8,128)} %get-tuple-element.494, f32[2,2,512]{2,1,0:T(2,128)S(1)} %get-tuple-element.495), kind=kOutput, calls=%fused_computation.23.clone.1 | convolution fusion | flops 811991040 | bytes 16261128 | tf_op jit(solution)/shard_map/while/body/eval_jaxpr/grqk,qgrh->kgh/dot_general | solution.py:136
  83.8 17.6 %fusion.115 = f32[1024,2,2,128]{0,3,2,1:T(8,128)S(1)} fusion(f32[1024,2,2,128]{0,3,2,1:T(8,128)S(1)} %copy-done, s32[]{:T(128)S(6)} %select_n.139, f32[2,1536,512,2]{2,1,3,0:T(8,128)} %fusion.113, bf16[2048,2,128]{0,2,1:T(8,128)(2,1)} %get-tuple-element.532, s32[]{:T(128)S(6)} %select_n.140, f32[2,2,512,1536]{2,3,1,0:T(8,128)} %get-tuple-element.494, ...), kind=kOutput, calls=%fused_computation.28.clone.1 | convolution fusion | flops 827330048 | bytes 52183048 | tf_op jit(solution)/shard_map/while/body/eval_jaxpr/grqk,kgh->qgrh/dot_general | solution.py:130
  101.4 1.3 copy-done.1
  103.5 11.7 %fusion.114 = (f32[2,2,512]{2,1,0:T(2,128)S(1)}, f32[2,2,512,1536]{2,3,1,0:T(8,128)}) fusion(pred[512,1536]{0,1:T(8,128)(4,1)S(1)} %compare_and_fusion.3, bf16[2048,2,128]{0,2,1:T(8,128)(2,1)} %get-tuple-element.532, s32[]{:T(128)S(6)} %select_n.140, bf16[1024,2,2,128]{0,3,2,1:T(8,128)(2,1)} %get-tuple-element.535, s32[]{:T(128)S(6)} %select_n.139), kind=kOutput, calls=%fused_computation.104.clone.1 | convolution fusion | flops 821036544 | bytes 15474696 | tf_op jit(solution)/shard_map/while/body/eval_jaxpr/sub | solution.py:122
  115.2 7.6 %fusion.113 = f32[2,1536,512,2]{2,1,3,0:T(8,128)} fusion(bf16[2048,2,128]{0,2,1:T(8,128)(2,1)S(1)} %get-tuple-element.536, s32[]{:T(128)S(6)} %select_n.140, bf16[1024,2,2,128]{0,3,2,1:T(8,128)(2,1)} %get-tuple-element.537, s32[]{:T(128)S(6)} %select_n.139), kind=kOutput, calls=%fused_computation.34.clone.1 | convolution fusion | flops 805306368 | bytes 13893640 | tf_op jit(solution)/shard_map/while/body/eval_jaxpr/qgrh,kgh->grqk/dot_general | solution.py:125
  122.8 20.1 %fusion.116 = f32[2048,2,128]{0,2,1:T(8,128)S(1)} fusion(f32[2048,2,128]{0,2,1:T(8,128)S(1)} %copy-done.3, s32[]{:T(128)S(6)} %select_n.140, f32[2,1536,512,2]{2,1,3,0:T(8,128)} %fusion.113, bf16[1024,2,2,128]{0,3,2,1:T(8,128)(2,1)} %get-tuple-element.535, s32[]{:T(128)S(6)} %select_n.139, f32[2,2,512,1536]{2,3,1,0:T(8,128)} %get-tuple-element.494, ...), kind=kOutput, calls=%fused_computation.26.clone.1 | convolution fusion | flops 827723264 | bytes 54018056 | tf_op jit(solution)/shard_map/while/body/eval_jaxpr/grqk,qgrh->kgh/dot_general | solution.py:133
  142.9 1.3 copy-done.4
  144.2 8.9 %fusion.117 = f32[2048,2,128]{0,2,1:T(8,128)} fusion(f32[2048,2,128]{0,2,1:T(8,128)} %get-tuple-element.515, s32[]{:T(128)S(6)} %select_n.140, bf16[1024,2,2,128]{0,3,2,1:T(8,128)(2,1)} %get-tuple-element.537, s32[]{:T(128)S(6)} %select_n.139, f32[2,2,512,1536]{2,3,1,0:T(8,128)} %get-tuple-element.494, f32[2,2,512]{2,1,0:T(2,128)S(1)} %get-tuple-element.495), kind=kOutput, calls=%fused_computation.23.clone.1 | convolution fusion | flops 811991040 | bytes 16261128 | tf_op jit(solution)/shard_map/while/body/eval_jaxpr/grqk,qgrh->kgh/dot_general | solution.py:136
  153.1 17.7 %fusion.115 = f32[1024,2,2,128]{0,3,2,1:T(8,128)S(1)} fusion(f32[1024,2,2,128]{0,3,2,1:T(8,128)S(1)} %copy-done, s32[]{:T(128)S(6)} %select_n.139, f32[2,1536,512,2]{2,1,3,0:T(8,128)} %fusion.113, bf16[2048,2,128]{0,2,1:T(8,128)(2,1)} %get-tuple-element.532, s32[]{:T(128)S(6)} %select_n.140, f32[2,2,512,1536]{2,3,1,0:T(8,128)} %get-tuple-element.494, ...), kind=kOutput, calls=%fused_computation.28.clone.1 | convolution fusion | flops 827330048 | bytes 52183048 | tf_op jit(solution)/shard_map/while/body/eval_jaxpr/grqk,kgh->qgrh/dot_general | solution.py:130
  170.8 1.3 copy-done.1
  172.1 1.4 slice.65
  173.6 1.3 collective-permute-start.2
  174.9 1.3 slice.64
  176.2 1.3 collective-permute-start.3
  177.5 1.4 bitcast_multiply_fusion.16
  179.5 0.8 copy-done.8
  180.9 0.9 copy-done.5
  183.4 19.6 %convolution_convert_fusion = bf16[5376,1024]{1,0:T(8,128)(2,1)} fusion(bf16[1024,5376]{0,1:T(8,128)(2,1)} %all-gather.2.cloned.1.call-done, bf16[1024,256]{0,1:T(8,128)(2,1)S(1)} %bitcast.174, bf16[1024,256]{0,1:T(8,128)(2,1)S(1)} %bitcast.173, bf16[1024,512]{0,1:T(8,128)(2,1)S(1)} %fusion.72), kind=kOutput, calls=%fused_computation.63 | convolution fusion | flops 11286085632 | bytes 24117248 | tf_op jit(solution)/shard_map/dot_general | solution.py:183
  203.0 1.3 fusion.77
  204.4 89.4 %reduce-scatter.2.cloned.1.call-done = bf16[336,1024]{1,0:T(8,128)(2,1)} async-done(((bf16[5376,1024]{1,0:T(8,128)(2,1)}), bf16[336,1024]{1,0:T(8,128)(2,1)}) %reduce-scatter.2.cloned.1.call-update) | async-done | bytes 688144 | tf_op jit(solution)/shard_map/reduce_scatter | solution.py:60
  293.9 1.2 concatenate.42
  295.7 1.6 broadcast_select_fusion
  297.3 3.7 %all-to-all-start = ((bf16[16,64,1024]{2,1,0:T(8,128)(2,1)}), bf16[16,64,1024]{2,1,0:T(8,128)(2,1)S(1)}, u32[]{:S(2)}, u32[]{:S(2)}) async-start(bf16[16,64,1024]{2,1,0:T(8,128)(2,1)} %broadcast_select_fusion), calls=%async_computation.1 | async-start | bytes 4194304 | tf_op jit(solution)/shard_map/all_to_all | solution.py:74
  301.7 27.3 %all-to-all-done = bf16[16,64,1024]{2,1,0:T(8,128)(2,1)S(1)} async-done(((bf16[16,64,1024]{2,1,0:T(8,128)(2,1)}), bf16[16,64,1024]{2,1,0:T(8,128)(2,1)S(1)}, u32[]{:S(2)}, u32[]{:S(2)}) %all-to-all-start) | async-done | bytes 2097184 | tf_op jit(solution)/shard_map/all_to_all | solution.py:74
  329.0 10.9 %conditional.1 = (f32[1,1,1024,1024]{3,2,1,0:T(8,128)}, f32[1,1,1024,1024]{3,2,1,0:T(8,128)}) conditional(s32[]{:T(128)} %convert_element_type.50, () %tuple.53, (pred[6]{0:T(512)(128)(4,1)S(1)}, s32[6]{0:T(128)S(1)}, bf16[16,64,1024]{2,1,0:T(8,128)(2,1)S(1)}) %tuple.55), branch_computations={%region_8.9_spmd, %region_9.11_spmd} | conditional | flops 4298113024 | bytes 18350140 | solution.py:214
  331.1 4.4 %multiply_bitcast_fusion = f32[1,1,1024,1024]{3,2,1,0:T(8,128)} fusion(bf16[1024,1024]{1,0:T(8,128)(2,1)S(1)} %bitcast_select_fusion.4), kind=kOutput, calls=%fused_computation.59 | convolution fusion | flops 2148532224 | bytes 6291456 | tf_op jit(solution)/shard_map/cond/branch_1_fun/dot_general | solution.py:201
  335.5 4.4 %multiply_bitcast_fusion.1 = f32[1,1,1024,1024]{3,2,1,0:T(8,128)} fusion(bf16[1024,1024]{1,0:T(8,128)(2,1)S(1)} %bitcast_select_fusion.4), kind=kOutput, calls=%fused_computation.60 | convolution fusion | flops 2148532224 | bytes 6291456 | tf_op jit(solution)/shard_map/cond/branch_1_fun/dot_general | solution.py:195
  (67 shorter events, 6.9 us)
Async XLA Ops:
  7.2 1.3 slice-start
  7.2 176.2 %all-gather.2.cloned.1.call-start = ((), (), s32[]{:S(2)}) async-start(), calls=%async_computation.2 | async-start | bytes 12386304 | tf_op jit(solution)/shard_map/all_gather | solution.py:184
  7.2 4.1 %slice-start.1 = ((bf16[128,5376]{1,0:T(8,128)(2,1)}), bf16[128,256]{1,0:T(8,128)(2,1)S(1)}, s32[]{:S(2)}) async-start(bf16[128,5376]{1,0:T(8,128)(2,1)} %param.11), calls=%async_computation.5 | async-start | bytes 131072 | tf_op jit(solution)/shard_map/slice | solution.py:51
  11.3 1.4 copy-start.10
  11.5 9.4 %copy-start.9 = (bf16[1024,512]{1,0:T(8,128)(2,1)S(1)}, bf16[1024,512]{1,0:T(8,128)(2,1)}, u32[]{:S(2)}) copy-start(bf16[1024,512]{1,0:T(8,128)(2,1)} %param.12) | copy-start | bytes 3145732
  12.7 281.2 %reduce-scatter.2.cloned.1.call-start = ((), (), s32[]{:S(2)}) async-start(), calls=%async_computation.3 | async-start | bytes 11698176 | tf_op jit(solution)/shard_map/reduce_scatter | solution.py:60
  12.9 13.3 %collective-permute-start = (bf16[1024,256]{0,1:T(8,128)(2,1)S(1)}, bf16[1024,256]{0,1:T(8,128)(2,1)}, u32[]{:S(2)}, u32[]{:S(2)}) collective-permute-start(bf16[1024,256]{0,1:T(8,128)(2,1)S(1)} %copy.47), channel_id=1, source_target_pairs={{0,8},{8,16},{16,24},{24,32},{32,40},{40,48},{48,56},{56,64},{64,7... | collective-permute-start | bytes 1572872 | tf_op jit(solution)/shard_map/ppermute | solution.py:23
  16.3 12.1 %collective-permute-start.1 = (bf16[1024,256]{0,1:T(8,128)(2,1)S(1)}, bf16[1024,256]{0,1:T(8,128)(2,1)S(1)}, u32[]{:S(2)}, u32[]{:S(2)}) collective-permute-start(bf16[1024,256]{0,1:T(8,128)(2,1)S(1)} %copy.50), channel_id=1, source_target_pairs={{0,8},{8,16},{16,24},{24,32},{32,40},{40,48},{48,56},{56,64},{64,7... | collective-permute-start | bytes 1572872 | tf_op jit(solution)/shard_map/ppermute | solution.py:23
  28.5 4.8 %copy-start.11 = (s32[1024]{0:T(1024)S(1)}, s32[1024]{0:T(1024)}, u32[]{:S(2)}) copy-start(s32[1024]{0:T(1024)} %param.16) | copy-start | bytes 12292
  45.8 7.6 %copy-start.3 = (f32[2048,2,128]{0,2,1:T(8,128)S(1)}, f32[2048,2,128]{0,2,1:T(8,128)}, u32[]{:S(2)}) copy-start(f32[2048,2,128]{0,2,1:T(8,128)} %get-tuple-element.514) | copy-start | bytes 6291460 | tf_op jit(solution)/shard_map/while
  73.5 1.3 copy-start.4
  74.9 8.9 %copy-start = (f32[1024,2,2,128]{0,3,2,1:T(8,128)S(1)}, f32[1024,2,2,128]{0,3,2,1:T(8,128)}, u32[]{:S(2)}) copy-start(f32[1024,2,2,128]{0,3,2,1:T(8,128)} %get-tuple-element.513) | copy-start | bytes 6291460 | tf_op jit(solution)/shard_map/while
  101.4 1.3 copy-start.1
  115.2 7.6 %copy-start.3 = (f32[2048,2,128]{0,2,1:T(8,128)S(1)}, f32[2048,2,128]{0,2,1:T(8,128)}, u32[]{:S(2)}) copy-start(f32[2048,2,128]{0,2,1:T(8,128)} %get-tuple-element.514) | copy-start | bytes 6291460 | tf_op jit(solution)/shard_map/while
  142.9 1.3 copy-start.4
  144.2 8.9 %copy-start = (f32[1024,2,2,128]{0,3,2,1:T(8,128)S(1)}, f32[1024,2,2,128]{0,3,2,1:T(8,128)}, u32[]{:S(2)}) copy-start(f32[1024,2,2,128]{0,3,2,1:T(8,128)} %get-tuple-element.513) | copy-start | bytes 6291460 | tf_op jit(solution)/shard_map/while
  170.8 1.3 copy-start.1
  172.1 5.3 %copy-start.2 = (f32[1024,2,2,128]{0,3,2,1:T(8,128)S(1)}, f32[1024,2,2,128]{0,3,2,1:T(8,128)}, u32[]{:S(2)}) copy-start(f32[1024,2,2,128]{0,3,2,1:T(8,128)} %get-tuple-element.375) | copy-start | bytes 6291460
  173.6 7.3 %collective-permute-start.2 = (bf16[1024,2,128]{0,2,1:T(8,128)(2,1)S(1)}, bf16[1024,2,128]{0,2,1:T(8,128)(2,1)S(1)}, u32[]{:S(2)}, u32[]{:S(2)}) collective-permute-start(bf16[1024,2,128]{0,2,1:T(8,128)(2,1)S(1)} %slice.65), channel_id=1, source_target_pairs={{8,0},{16,8},{24,16},{32,24},{40,32},{48,40},{56,48},{64,56},{72,6... | collective-permute-start | bytes 1572872 | tf_op jit(solution)/shard_map/ppermute | solution.py:23
  176.2 6.1 %collective-permute-start.3 = (bf16[1024,2,128]{0,2,1:T(8,128)(2,1)S(1)}, bf16[1024,2,128]{0,2,1:T(8,128)(2,1)S(1)}, u32[]{:S(2)}, u32[]{:S(2)}) collective-permute-start(bf16[1024,2,128]{0,2,1:T(8,128)(2,1)S(1)} %slice.64), channel_id=1, source_target_pairs={{8,0},{16,8},{24,16},{32,24},{40,32},{48,40},{56,48},{64,56},{72,6... | collective-permute-start | bytes 1572872 | tf_op jit(solution)/shard_map/ppermute | solution.py:23
  179.2 1.0 copy-start.8
  180.2 1.6 copy-start.5
  180.2 1.7 copy-start.7
  180.9 1.9 copy-start.6
  297.3 31.7 %all-to-all-start = ((bf16[16,64,1024]{2,1,0:T(8,128)(2,1)}), bf16[16,64,1024]{2,1,0:T(8,128)(2,1)S(1)}, u32[]{:S(2)}, u32[]{:S(2)}) async-start(bf16[16,64,1024]{2,1,0:T(8,128)(2,1)} %broadcast_select_fusion), calls=%async_computation.1 | async-start | bytes 4194304 | tf_op jit(solution)/shard_map/all_to_all | solution.py:74
Sparse Core Ops, SparseCore 0:
  12.8 148.7 all-gather.1
  203.1 90.7 reduce-scatter.1
where the time goes:
time: 348 us; the launch traced here: 347 us
  matrix products  160 us (46%)
  waiting for transfers between devices  117 us (34%)
  local copies, waits for them, and re-layouts  26.4 us (8%)
  other arithmetic  15.3 us (4%)
  between operations  15 us (4%)
  starting transfers between devices  12 us (3%)
    reduce_scatter x1, waiting for transfers between devices, owned_block(): mine = lax.psum_scatter(arranged, 'seq', scatter_dimension=0, tiled=True)  89.4 us
    dot_general x2, matrix products, one_block(): jnp.einsum('grqk,qgrh->kgh', grad_score, query_part, preferred_element_ty...  40.4 us
    dot_general x2, matrix products, one_block(): jnp.einsum('grqk,kgh->qgrh', grad_score, key_part, preferred_element_type...  35.3 us
    all_to_all x1, waiting for transfers between devices, owned_block(): received = lax.all_to_all(send, 'seq', 0, 0, tiled=False)  27.3 us
    sub x2, matrix products, one_block(): exponent = jnp.where(allowed, jnp.exp(masked - row_top), 0.0)  23.4 us
    dot_general x1, matrix products, per_device(): lax.dot_general(lax.all_gather(arrange_features(inputs, seq_count), 'head...  19.6 us
    dot_general x2, matrix products, one_block(): jnp.einsum('grqk,qgrh->kgh', attend_low, out_part, preferred_element_type...  17.8 us
    dot_general x2, matrix products, one_block(): jnp.einsum('qgrh,kgh->grqk', out_part, value_part, preferred_element_type...  15.1 us
  transfers between devices with their start and end apart: 7, of which 2 were waited for; matrix products, arithmetic and copies ran while one was open for 45% of the time, Pallas kernels for 0%

commit v1 on v0

--- a/solution.py
+++ b/solution.py
@@ -2,6 +2,8 @@
 import jax.numpy as jnp
 from jax import lax
 from jax.sharding import PartitionSpec as P
+from jax.experimental import pallas as pl
+from jax.experimental.pallas import tpu as pltpu
 
 D = 5376
 HD = 128
@@ -15,6 +17,65 @@
 score_scale = 168.0 ** (-0.5)
 rotary_frequency_base = 10000.0
 neg_large = -1e30
+QBLK = 256
+
+
+def attention_kernel(band_ref, q_ref, do_ref, k_ref, v_ref, dq_ref, dk_ref, dv_ref):
+    tok_rows = q_ref.shape[0]
+    span = QBLK + WINDOW
+    dk_ref[...] = jnp.zeros(dk_ref.shape, jnp.float32)
+    dv_ref[...] = jnp.zeros(dv_ref.shape, jnp.float32)
+    def one_block(qb, carry):
+        q0 = pl.multiple_of(qb * QBLK, QBLK)
+        band = band_ref[pl.ds(q0, QBLK), :]
+        band = jnp.concatenate([band, band], 0)
+        col = lax.broadcasted_iota(jnp.int32, (QPK * QBLK, span), 1)
+        row = lax.broadcasted_iota(jnp.int32, (QPK * QBLK, span), 0) % QBLK
+        allowed = (col + q0 >= band) & (col <= row + WINDOW)
+        for g in range(KV_DEV):
+            base = g * QPK * HD
+            qs = jnp.concatenate(
+                [q_ref[pl.ds(q0, QBLK), base + r * HD:base + (r + 1) * HD] for r in range(QPK)], 0)
+            dos = jnp.concatenate(
+                [do_ref[pl.ds(q0, QBLK), base + r * HD:base + (r + 1) * HD] for r in range(QPK)], 0)
+            keys = k_ref[pl.ds(q0, span), g * HD:(g + 1) * HD]
+            vals = v_ref[pl.ds(q0, span), g * HD:(g + 1) * HD]
+            logits = lax.dot_general(qs, keys, (((1,), (1,)), ((), ())),
+                                     preferred_element_type=jnp.float32) * score_scale
+            masked = jnp.where(allowed, logits, neg_large)
+            top = jnp.max(masked, -1, keepdims=True)
+            expo = jnp.where(allowed, jnp.exp(masked - top), 0.0)
+            attend = expo / jnp.sum(expo, -1, keepdims=True)
+            grad_attend = lax.dot_general(dos, vals, (((1,), (1,)), ((), ())),
+                                          preferred_element_type=jnp.float32)
+            row_dot = jnp.sum(attend * grad_attend, -1, keepdims=True)
+            grad_score = (attend * (grad_attend - row_dot) * score_scale).astype(jnp.bfloat16)
+            dqs = jnp.dot(grad_score, keys, preferred_element_type=jnp.float32)
+            for r in range(QPK):
+                dq_ref[pl.ds(q0, QBLK), base + r * HD:base + (r + 1) * HD] = dqs[r * QBLK:(r + 1) * QBLK]
+            dk_ref[pl.ds(q0, span), g * HD:(g + 1) * HD] += lax.dot_general(
+                grad_score, qs, (((0,), (0,)), ((), ())), preferred_element_type=jnp.float32)
+            dv_ref[pl.ds(q0, span), g * HD:(g + 1) * HD] += lax.dot_general(
+                attend.astype(jnp.bfloat16), dos, (((0,), (0,)), ((), ())),
+                preferred_element_type=jnp.float32)
+        return carry
+
+    lax.fori_loop(0, tok_rows // QBLK, one_block, 0)
+
+
+def attention_backward(band_rel, queries, out_grad, key_all, value_all):
+    tok_rows = queries.shape[0]
+    vmem = pl.BlockSpec(memory_space=pltpu.VMEM)
+    return pl.pallas_call(
+        attention_kernel,
+        out_shape=(
+            jax.ShapeDtypeStruct(queries.shape, jnp.float32),
+            jax.ShapeDtypeStruct(key_all.shape, jnp.float32),
+            jax.ShapeDtypeStruct(value_all.shape, jnp.float32),
+        ),
+        in_specs=[vmem] * 5,
+        out_specs=(vmem, vmem, vmem),
+    )(band_rel.reshape(tok_rows, 1), queries, out_grad, key_all, value_all)
 
 
 def shifted(value, axis, steps):
@@ -89,74 +150,14 @@
     group_index = lax.axis_index("head")
     tokens_all = tok_rows * seq_count
     earlier_keys, earlier_values = shifted((key_rows, values), "seq", 1)
-    gathered_key_rows = jnp.concatenate([earlier_keys, key_rows], 0).reshape(
-        2 * tok_rows, KV_DEV, HD
-    )
-    value_all = jnp.concatenate([earlier_values, values], 0).reshape(2 * tok_rows, KV_DEV, HD)
-    query_heads = queries.reshape(tok_rows, KV_DEV, QPK, HD)
-    out_heads = out_grad.reshape(tok_rows, KV_DEV, QPK, HD)
-    block_rows = min(512, tok_rows)
-    span_rows = block_rows + WINDOW
-    block_count = tok_rows // block_rows
-
-    def one_block(block_index, state_pair):
-        grad_query, grad_keys, grad_values = state_pair
-        offset = block_index * block_rows
-        query_part = lax.dynamic_slice_in_dim(query_heads, offset, block_rows, 0)
-        out_part = lax.dynamic_slice_in_dim(out_heads, offset, block_rows, 0)
-        key_start = tok_rows + offset - WINDOW
-        key_part = lax.dynamic_slice_in_dim(gathered_key_rows, key_start, span_rows, 0)
-        value_part = lax.dynamic_slice_in_dim(value_all, key_start, span_rows, 0)
-        band_part = lax.dynamic_slice_in_dim(band_start, offset, block_rows, 0)
-        query_pos = seq_index * tok_rows + offset + jnp.arange(block_rows, dtype=jnp.int32)
-        key_pos = seq_index * tok_rows + offset - WINDOW + jnp.arange(span_rows, dtype=jnp.int32)
-        allowed = (key_pos[None, :] >= band_part[:, None]) & (
-            key_pos[None, :] <= query_pos[:, None]
-        )
-        attention_logits = (
-            jnp.einsum("qgrh,kgh->grqk", query_part, key_part, preferred_element_type=jnp.float32)
-            * score_scale
-        )
-        masked = jnp.where(allowed, attention_logits, neg_large)
-        row_top = jnp.max(masked, -1, keepdims=True)
-        exponent = jnp.where(allowed, jnp.exp(masked - row_top), 0.0)
-        attend = exponent / jnp.sum(exponent, -1, keepdims=True)
-        attend_low = attend.astype(jnp.bfloat16)
-        grad_attend = jnp.einsum(
-            "qgrh,kgh->grqk", out_part, value_part, preferred_element_type=jnp.float32
-        )
-        row_dot = jnp.sum(attend * grad_attend, -1, keepdims=True)
-        grad_score = (attend * (grad_attend - row_dot) * score_scale).astype(jnp.bfloat16)
-        query_term = jnp.einsum(
-            "grqk,kgh->qgrh", grad_score, key_part, preferred_element_type=jnp.float32
-        )
-        key_term = jnp.einsum(
-            "grqk,qgrh->kgh", grad_score, query_part, preferred_element_type=jnp.float32
-        )
-        value_term = jnp.einsum(
-            "grqk,qgrh->kgh", attend_low, out_part, preferred_element_type=jnp.float32
-        )
-        grad_query = lax.dynamic_update_slice_in_dim(grad_query, query_term, offset, 0)
-        grad_keys = lax.dynamic_update_slice_in_dim(
-            grad_keys,
-            lax.dynamic_slice_in_dim(grad_keys, key_start, span_rows, 0) + key_term,
-            key_start,
-            0,
-        )
-        grad_values = lax.dynamic_update_slice_in_dim(
-            grad_values,
-            lax.dynamic_slice_in_dim(grad_values, key_start, span_rows, 0) + value_term,
-            key_start,
-            0,
-        )
-        return (grad_query, grad_keys, grad_values)
-
-    start_state = (
-        jnp.zeros((tok_rows, KV_DEV, QPK, HD), jnp.float32),
-        jnp.zeros((2 * tok_rows, KV_DEV, HD), jnp.float32),
-        jnp.zeros((2 * tok_rows, KV_DEV, HD), jnp.float32),
-    )
-    grad_query, grad_keys, grad_values = lax.fori_loop(0, block_count, one_block, start_state)
+    key_all = jnp.concatenate([earlier_keys, key_rows], 0)
+    value_all = jnp.concatenate([earlier_values, values], 0)
+    band_rel = band_start - (seq_index * tok_rows - WINDOW)
+    grad_query, grad_keys, grad_values = attention_backward(
+        band_rel, queries, out_grad, key_all, value_all
+    )
+    grad_keys = grad_keys.reshape(2 * tok_rows, KV_DEV, HD)
+    grad_values = grad_values.reshape(2 * tok_rows, KV_DEV, HD)
     rim_keys, rim_values = (
         shifted(grad_keys[:tok_rows].astype(jnp.bfloat16), "seq", -1).astype(jnp.float32),
         shifted(grad_values[:tok_rows].astype(jnp.bfloat16), "seq", -1).astype(jnp.float32),

time: 348 us -> 324 us (0.931)
  matrix products: 160 us -> 27.2 us
  waiting for transfers between devices: 117 us -> 192 us
  Pallas kernels: 0 us -> 27.8 us
  other arithmetic: 15.3 us -> 23.3 us
    dot_general x8 -> x0, matrix products: 109 us -> none  [the longest x2 40.4 us: one_block(): jnp.einsum('grqk,qgrh->kgh', grad_score, query_part, preferred_element_ty...]
    all_gather x1, waiting for transfers between devices: 0.02 us -> 76.5 us  [per_device(): lax.all_gather(arrange_features(inputs, seq_count), 'head', axis=0, tiled...]
    pallas_call x0 -> x1, Pallas kernels: none -> 27.8 us  [attention_backward(): pl.pallas_call(attention_kernel, out_shape=(jax.ShapeDtypeStruct(queries....]
    sub x2 -> x0, matrix products: 23.4 us -> none  [one_block(): exponent = jnp.where(allowed, jnp.exp(masked - row_top), 0.0)]
    slice x0 -> x4, local copies, waits for them, and re-layouts: none -> 7.97 us  [the longest x2 4.19 us: per_device(): own_keys = grad_keys[tok_rows:] + rim_keys]
    unnamed x22, local copies, waits for them, and re-layouts: 8.95 us -> 1.75 us
    while x16 -> x0, local copies, waits for them, and re-layouts: 5.26 us -> none
    convert_element_type x0 -> x2, local copies, waits for them, and re-layouts: none -> 3.98 us  [the longest x1 2 us: per_device(): grad_keys[:tok_rows].astype(jnp.bfloat16)]
  transfers between devices with their start and end apart: 7 -> 7, of which waited for: 2 -> 3; matrix products, arithmetic and copies ran while one was open for 45% -> 12% of each run, Pallas kernels for 0% -> 9%
where the time goes in v1:
time: 324 us; the launch traced here: 322 us
  waiting for transfers between devices  192 us (59%)
  Pallas kernels  27.8 us (9%)
  matrix products  27.2 us (8%)
  local copies, waits for them, and re-layouts  24.3 us (8%)
  other arithmetic  23.3 us (7%)
  between operations  15 us (5%)
  starting transfers between devices  12.2 us (4%)
    reduce_scatter x1, waiting for transfers between devices, owned_block(): mine = lax.psum_scatter(arranged, 'seq', scatter_dimension=0, tiled=True)  87.9 us
    all_gather x1, waiting for transfers between devices, per_device(): lax.all_gather(arrange_features(inputs, seq_count), 'head', axis=0, tiled...  76.5 us
    pallas_call x1, Pallas kernels, attention_backward(): pl.pallas_call(attention_kernel, out_shape=(jax.ShapeDtypeStruct(queries....  27.8 us
    all_to_all x1, waiting for transfers between devices, owned_block(): received = lax.all_to_all(send, 'seq', 0, 0, tiled=False)  27.3 us
    dot_general x1, matrix products, per_device(): lax.dot_general(lax.all_gather(arrange_features(inputs, seq_count), 'head...  18.4 us
    ppermute x4, starting transfers between devices, shifted(): lax.ppermute(value, axis, [(source, source + steps) for source in range(i...  8.39 us
  transfers between devices with their start and end apart: 7, of which 3 were waited for; matrix products, arithmetic and copies ran while one was open for 12% of the time, Pallas kernels for 9%

profile of v1, /device:TPU:0, one launch (start us, length us, event | category | flops | bytes accessed | tf_op | source)
XLA Modules:
  0.0 322.3 jit_solution(3648776417685427418)
XLA Ops:
  7.2 1.3 slice-done
  8.5 1.4 copy.21
  9.9 1.4 copy.18
  11.3 0.1 copy.22
  11.5 1.2 pad_maximum_fusion.1
  12.7 1.3 collective-permute-start
  14.1 4.3 %collective-permute-start.1 = (bf16[1024,256]{1,0:T(8,128)(2,1)S(1)}, bf16[1024,256]{1,0:T(8,128)(2,1)S(1)}, u32[]{:S(2)}, u32[]{:S(2)}) collective-permute-start(bf16[1024,256]{1,0:T(8,128)(2,1)S(1)} %copy-done.7), channel_id=1, source_target_pairs={{0,8},{8,16},{16,24},{24,32},{32,40},{40,48},{48,56},{56,64},{64,7... | collective-permute-start | bytes 1572872 | tf_op jit(solution)/shard_map/ppermute | solution.py:84
  18.5 1.0 copy.20.band_ref
  19.5 1.9 multiply_cosine_fusion
  21.4 1.3 pad_maximum_fusion.4
  22.7 1.1 pad_maximum_fusion.2.k_ref
  23.8 1.0 pad_maximum_fusion.3.v_ref
  24.8 27.8 %shard_map.90 = (f32[1024,512]{1,0:T(8,128)}, f32[2048,256]{1,0:T(8,128)}, f32[2048,256]{1,0:T(8,128)}) custom-call(s32[1024,1]{1,0:T(8,128)} %copy.20.band_ref, bf16[1024,512]{1,0:T(8,128)(2,1)} %q_ref.1, bf16[1024,512]{1,0:T(8,128)(2,1)} %do_ref.1, bf16[2048,256]{1,0:T(8,128)(2,1)} %pad_maximum_fusion.2.k_ref, bf16[2048,256]{1,0:T(8,128)(2,1)} %pad_maximum_fusion.3.v_ref), custom_call_target="tpu_custom_call" | custom-call | tf_op jit(solution)/shard_map/pallas_call | solution.py:69
  52.7 2.5 slice.48
  55.1 2.1 slice.69
  57.2 1.0 slice.53
  58.2 0.9 slice.68
  59.1 1.7 slice.49
  60.8 2.0 convert_element_type.30
  62.8 1.3 collective-permute-start.2
  64.1 1.7 reshape.87
  65.9 2.7 slice.54
  68.6 2.0 convert_element_type.32
  70.6 1.5 collective-permute-start.3
  72.0 2.3 broadcast_multiply_fusion
  74.3 1.2 slice_negate_fusion
  75.5 1.1 pad_maximum_fusion
  76.7 0.4 mul.59
  77.1 1.6 fusion
  78.7 1.8 fusion.7
  80.4 1.1 slice_negate_fusion.1
  81.6 2.7 fusion.6
  84.5 0.5 add_convert_fusion
  85.1 76.5 %all-gather.2.cloned.1.call-done = bf16[1024,5376]{0,1:T(8,128)(2,1)} async-done(((bf16[128,5376]{0,1:T(8,128)(2,1)}), bf16[1024,5376]{0,1:T(8,128)(2,1)}) %all-gather.2.cloned.1.call-update) | async-done | bytes 11010064 | tf_op jit(solution)/shard_map/all_gather | solution.py:185
  161.6 18.4 %convolution_convert_fusion = bf16[5376,1024]{1,0:T(8,128)(2,1)} fusion(bf16[1024,5376]{0,1:T(8,128)(2,1)} %all-gather.2.cloned.1.call-done, bf16[1024,256]{1,0:T(8,128)(2,1)S(1)} %bitcast.55, bf16[1024,256]{1,0:T(8,128)(2,1)S(1)} %bitcast.54, bf16[1024,512]{1,0:T(8,128)(2,1)S(1)} %copy-done.5), kind=kOutput, calls=%fused_computation.5 | convolution fusion | flops 11286085632 | bytes 24117248 | tf_op jit(solution)/shard_map/dot_general | solution.py:184
  180.1 1.3 fusion.10
  181.4 0.1 select_reduce_fusion.1
  181.5 87.9 %reduce-scatter.2.cloned.1.call-done = bf16[336,1024]{1,0:T(8,128)(2,1)} async-done(((bf16[5376,1024]{1,0:T(8,128)(2,1)}), bf16[336,1024]{1,0:T(8,128)(2,1)}) %reduce-scatter.2.cloned.1.call-update) | async-done | bytes 688144 | tf_op jit(solution)/shard_map/reduce_scatter | solution.py:121
  269.4 1.2 concatenate.42
  270.6 0.7 gather_fusion
  271.3 1.6 broadcast_select_fusion
  272.8 3.7 %all-to-all-start = ((bf16[16,64,1024]{2,1,0:T(8,128)(2,1)}), bf16[16,64,1024]{2,1,0:T(8,128)(2,1)S(1)}, u32[]{:S(2)}, u32[]{:S(2)}) async-start(bf16[16,64,1024]{2,1,0:T(8,128)(2,1)} %broadcast_select_fusion), calls=%async_computation.1 | async-start | bytes 4194304 | tf_op jit(solution)/shard_map/all_to_all | solution.py:135
  277.2 27.3 %all-to-all-done = bf16[16,64,1024]{2,1,0:T(8,128)(2,1)S(1)} async-done(((bf16[16,64,1024]{2,1,0:T(8,128)(2,1)}), bf16[16,64,1024]{2,1,0:T(8,128)(2,1)S(1)}, u32[]{:S(2)}, u32[]{:S(2)}) %all-to-all-start) | async-done | bytes 2097184 | tf_op jit(solution)/shard_map/all_to_all | solution.py:135
  304.5 10.9 %conditional.1 = (f32[1,1,1024,1024]{3,2,1,0:T(8,128)}, f32[1,1,1024,1024]{3,2,1,0:T(8,128)}) conditional(s32[]{:T(128)} %convert_element_type.28, () %tuple.20, (pred[6]{0:T(512)(128)(4,1)S(1)}, s32[6]{0:T(128)S(1)}, bf16[16,64,1024]{2,1,0:T(8,128)(2,1)S(1)}) %tuple.21), branch_computations={%region_3.4_spmd, %region_4.6_spmd} | conditional | flops 4298113024 | bytes 18350140 | solution.py:215
  304.6 0.6 select_reduce_fusion
  305.9 0.7 bitcast_select_fusion
  306.6 4.4 %multiply_bitcast_fusion = f32[1,1,1024,1024]{3,2,1,0:T(8,128)} fusion(bf16[1024,1024]{1,0:T(8,128)(2,1)S(1)} %bitcast_select_fusion), kind=kOutput, calls=%fused_computation.1 | convolution fusion | flops 2148532224 | bytes 6291456 | tf_op jit(solution)/shard_map/cond/branch_1_fun/dot_general | solution.py:202
  311.0 4.4 %multiply_bitcast_fusion.1 = f32[1,1,1024,1024]{3,2,1,0:T(8,128)} fusion(bf16[1024,1024]{1,0:T(8,128)(2,1)S(1)} %bitcast_select_fusion), kind=kOutput, calls=%fused_computation.2 | convolution fusion | flops 2148532224 | bytes 6291456 | tf_op jit(solution)/shard_map/cond/branch_1_fun/dot_general | solution.py:196
  (39 shorter events, 0.4 us)
Async XLA Ops:
  7.2 1.3 slice-start
  7.2 154.4 %all-gather.2.cloned.1.call-start = ((), (), s32[]{:S(2)}) async-start(), calls=%async_computation.2 | async-start | bytes 12386304 | tf_op jit(solution)/shard_map/all_gather | solution.py:185
  8.5 2.8 slice-start.1
  11.5 1.3 copy-start.6
  11.5 2.6 copy-start.7
  11.5 7.0 %copy-start.8 = (s32[1024]{0:T(1024)S(1)}, s32[1024]{0:T(1024)}, u32[]{:S(2)}) copy-start(s32[1024]{0:T(1024)} %param.14) | copy-start | bytes 12292
  12.7 256.7 %reduce-scatter.2.cloned.1.call-start = ((), (), s32[]{:S(2)}) async-start(), calls=%async_computation.3 | async-start | bytes 11698176 | tf_op jit(solution)/shard_map/reduce_scatter | solution.py:121
  12.7 10.0 %collective-permute-start = (bf16[1024,256]{1,0:T(8,128)(2,1)S(1)}, bf16[1024,256]{1,0:T(8,128)(2,1)S(1)}, u32[]{:S(2)}, u32[]{:S(2)}) collective-permute-start(bf16[1024,256]{1,0:T(8,128)(2,1)S(1)} %copy-done.6), channel_id=1, source_target_pairs={{0,8},{8,16},{16,24},{24,32},{32,40},{40,48},{48,56},{56,64},{64,7... | collective-permute-start | bytes 1572872 | tf_op jit(solution)/shard_map/ppermute | solution.py:84
  14.1 9.7 %collective-permute-start.1 = (bf16[1024,256]{1,0:T(8,128)(2,1)S(1)}, bf16[1024,256]{1,0:T(8,128)(2,1)S(1)}, u32[]{:S(2)}, u32[]{:S(2)}) collective-permute-start(bf16[1024,256]{1,0:T(8,128)(2,1)S(1)} %copy-done.7), channel_id=1, source_target_pairs={{0,8},{8,16},{16,24},{24,32},{32,40},{40,48},{48,56},{56,64},{64,7... | collective-permute-start | bytes 1572872 | tf_op jit(solution)/shard_map/ppermute | solution.py:84
  52.6 4.5 %copy-start.4 = (f32[2048,256]{1,0:T(8,128)S(1)}, f32[2048,256]{1,0:T(8,128)}, u32[]{:S(2)}) copy-start(f32[2048,256]{1,0:T(8,128)} %get-tuple-element.33) | copy-start | bytes 6291460
  58.2 5.9 %copy-start = (f32[1024,512]{1,0:T(8,128)S(1)}, f32[1024,512]{1,0:T(8,128)}, u32[]{:S(2)}) copy-start(f32[1024,512]{1,0:T(8,128)} %get-tuple-element.31) | copy-start | bytes 6291460
  62.8 15.8 %collective-permute-start.2 = (bf16[1024,2,128]{2,1,0:T(2,128)(2,1)}, bf16[1024,2,128]{2,1,0:T(2,128)(2,1)}, u32[]{:S(2)}, u32[]{:S(2)}) collective-permute-start(bf16[1024,2,128]{2,1,0:T(2,128)(2,1)} %convert_element_type.30), channel_id=1, source_target_pairs={{8,0},{16,8},{24,16},{32,24},{40,32},{48,40},{56,48},{64,56},{72,6... | collective-permute-start | bytes 1572872 | tf_op jit(solution)/shard_map/ppermute | solution.py:84
  70.6 13.9 %collective-permute-start.3 = (bf16[1024,2,128]{2,1,0:T(2,128)(2,1)}, bf16[1024,2,128]{2,1,0:T(2,128)(2,1)S(1)}, u32[]{:S(2)}, u32[]{:S(2)}) collective-permute-start(bf16[1024,2,128]{2,1,0:T(2,128)(2,1)} %convert_element_type.32), channel_id=1, source_target_pairs={{8,0},{16,8},{24,16},{32,24},{40,32},{48,40},{56,48},{64,56},{72,6... | collective-permute-start | bytes 1572872 | tf_op jit(solution)/shard_map/ppermute | solution.py:84
  75.5 1.2 copy-start.1
  77.1 1.6 copy-start.2
  81.6 2.8 copy-start.3
  84.3 77.3 %copy-start.5 = (bf16[1024,512]{1,0:T(8,128)(2,1)S(1)}, bf16[1024,512]{1,0:T(8,128)(2,1)}, u32[]{:S(2)}) copy-start(bf16[1024,512]{1,0:T(8,128)(2,1)} %fusion) | copy-start | bytes 3145732
  272.8 31.7 %all-to-all-start = ((bf16[16,64,1024]{2,1,0:T(8,128)(2,1)}), bf16[16,64,1024]{2,1,0:T(8,128)(2,1)S(1)}, u32[]{:S(2)}, u32[]{:S(2)}) async-start(bf16[16,64,1024]{2,1,0:T(8,128)(2,1)} %broadcast_select_fusion), calls=%async_computation.1 | async-start | bytes 4194304 | tf_op jit(solution)/shard_map/all_to_all | solution.py:135
Sparse Core Ops, SparseCore 0:
  12.8 148.7 all-gather.1
  180.2 89.1 reduce-scatter.1

commit v2 on v1

--- a/solution.py
+++ b/solution.py
@@ -113,12 +113,11 @@
     return jnp.concatenate([main, tail], 2).reshape(count, D)
 
 
-def owned_block(arranged, owner_row, block_pick, seq_count):
+def owned_block(mine, owner_row, block_pick, seq_count):
     full_blocks = D // BLOCK
     piece = BLOCK // seq_count
     tail_piece = (D - full_blocks * BLOCK) // seq_count
-    columns = arranged.shape[1]
-    mine = lax.psum_scatter(arranged, "seq", scatter_dimension=0, tiled=True)
+    columns = mine.shape[1]
     mine = jnp.concatenate(
         [mine, jnp.zeros((NBLK * piece - mine.shape[0], columns), mine.dtype)], 0
     ).reshape(NBLK, piece, columns)
@@ -181,16 +180,22 @@
         1,
     ).astype(jnp.bfloat16)
     column_count = column_grads.shape[1]
-    partial_sum = lax.dot_general(
-        lax.all_gather(arrange_features(inputs, seq_count), "head", axis=0, tiled=True),
-        column_grads,
-        (((0,), (0,)), ((), ())),
-        preferred_element_type=jnp.float32,
-    )
+    arranged = arrange_features(inputs, seq_count).reshape(inputs.shape[0], seq_count, -1)
+    half = arranged.shape[2] // 2
+    pieces = []
+    for part in (arranged[:, :, :half], arranged[:, :, half:]):
+        gathered = lax.all_gather(part.reshape(inputs.shape[0], -1), "head", axis=0, tiled=True)
+        partial = lax.dot_general(
+            gathered, column_grads, (((0,), (0,)), ((), ())), preferred_element_type=jnp.float32
+        )
+        pieces.append(
+            lax.psum_scatter(partial.astype(jnp.bfloat16), "seq", scatter_dimension=0, tiled=True)
+        )
+    mine = jnp.concatenate(pieces, 0)
     owner_row = lax.dynamic_index_in_dim(owners, group_index, 0, keepdims=False)
     is_mine = owner_row == seq_index
     block_pick = jnp.sum(jnp.where(is_mine, jnp.arange(NBLK, dtype=jnp.int32), 0))
-    block_part = owned_block(partial_sum.astype(jnp.bfloat16), owner_row, block_pick, seq_count)
+    block_part = owned_block(mine, owner_row, block_pick, seq_count)
     def gram_pair(part_rows):
         left_value = (
             lax.dot_general(

time: 324 us -> 404 us (1.25)
  waiting for transfers between devices: 192 us -> 261 us
  local copies, waits for them, and re-layouts: 24.3 us -> 31.6 us
    reduce_scatter x1 -> x2, waiting for transfers between devices: 87.9 us -> 130 us  [per_device(): lax.psum_scatter(partial.astype(jnp.bfloat16), 'seq', scatter_dimension=0...]
    all_gather x1 -> x2, waiting for transfers between devices: 76.5 us -> 104 us  [per_device(): lax.all_gather(part.reshape(inputs.shape[0], -1), 'head', axis=0, tiled=T...]
    unnamed x22 -> x23, local copies, waits for them, and re-layouts: 1.75 us -> 10 us
    dot_general x1 -> x2, matrix products: 18.4 us -> 21.3 us  [per_device(): lax.dot_general(gathered, column_grads, (((0,), (0,)), ((), ())), preferr...]
  transfers between devices with their start and end apart: 7 -> 9, of which waited for: 3 -> 5; matrix products, arithmetic and copies ran while one was open for 12% -> 17% of each run, Pallas kernels for 9% -> 7%
where the time goes in v2:
time: 404 us; the launch traced here: 403 us
  waiting for transfers between devices  261 us (65%)
  local copies, waits for them, and re-layouts  31.6 us (8%)
  matrix products  30.1 us (7%)
  Pallas kernels  27.3 us (7%)
  other arithmetic  24.5 us (6%)
  between operations  14.7 us (4%)
  starting transfers between devices  12.5 us (3%)
    reduce_scatter x2, waiting for transfers between devices, per_device(): lax.psum_scatter(partial.astype(jnp.bfloat16), 'seq', scatter_dimension=0...  130 us
    all_gather x2, waiting for transfers between devices, per_device(): lax.all_gather(part.reshape(inputs.shape[0], -1), 'head', axis=0, tiled=T...  104 us
    pallas_call x1, Pallas kernels, attention_backward(): pl.pallas_call(attention_kernel, out_shape=(jax.ShapeDtypeStruct(queries....  27.3 us
    all_to_all x1, waiting for transfers between devices, owned_block(): received = lax.all_to_all(send, 'seq', 0, 0, tiled=False)  27.3 us
    dot_general x2, matrix products, per_device(): lax.dot_general(gathered, column_grads, (((0,), (0,)), ((), ())), preferr...  21.3 us
    unnamed x23, local copies, waits for them, and re-layouts  10 us
    ppermute x4, starting transfers between devices, shifted(): lax.ppermute(value, axis, [(source, source + steps) for source in range(i...  8.39 us
  transfers between devices with their start and end apart: 9, of which 5 were waited for; matrix products, arithmetic and copies ran while one was open for 17% of the time, Pallas kernels for 7%

profile of v2, /device:TPU:0, one launch (start us, length us, event | category | flops | bytes accessed | tf_op | source)
XLA Modules:
  0.0 402.8 jit_solution(672505702649409900)
XLA Ops:
  7.2 1.3 slice-done
  8.5 1.4 copy.38
  9.9 1.4 copy.29
  11.5 1.2 fusion.8
  12.8 0.7 all-gather.5.cloned.1.call-update
  13.5 1.3 collective-permute-start
  14.9 4.3 %collective-permute-start.1 = (bf16[1024,256]{1,0:T(8,128)(2,1)S(1)}, bf16[1024,256]{1,0:T(8,128)(2,1)S(1)}, u32[]{:S(2)}, u32[]{:S(2)}) collective-permute-start(bf16[1024,256]{1,0:T(8,128)(2,1)S(1)} %copy-done.7), channel_id=1, source_target_pairs={{0,8},{8,16},{16,24},{24,32},{32,40},{40,48},{48,56},{56,64},{64,7... | collective-permute-start | bytes 1572872 | tf_op jit(solution)/shard_map/ppermute | solution.py:84
  19.2 1.1 copy.27.band_ref
  20.3 1.9 multiply_cosine_fusion
  22.2 1.4 pad_maximum_fusion.7
  23.6 1.0 pad_maximum_fusion.2.k_ref
  24.6 1.1 pad_maximum_fusion.3.v_ref
  25.7 27.3 %shard_map.90 = (f32[1024,512]{1,0:T(8,128)}, f32[2048,256]{1,0:T(8,128)}, f32[2048,256]{1,0:T(8,128)}) custom-call(s32[1024,1]{1,0:T(8,128)} %copy.27.band_ref, bf16[1024,512]{1,0:T(8,128)(2,1)} %q_ref.1, bf16[1024,512]{1,0:T(8,128)(2,1)} %do_ref.1, bf16[2048,256]{1,0:T(8,128)(2,1)} %pad_maximum_fusion.2.k_ref, bf16[2048,256]{1,0:T(8,128)(2,1)} %pad_maximum_fusion.3.v_ref), custom_call_target="tpu_custom_call" | custom-call | tf_op jit(solution)/shard_map/pallas_call | solution.py:69
  53.0 2.5 slice.52
  55.5 2.2 slice.78
  57.6 1.0 slice.57
  58.7 0.8 slice.77
  59.5 1.8 slice.53
  61.3 2.0 convert_element_type.36
  63.3 1.3 collective-permute-start.2
  64.6 1.7 reshape.86
  66.3 2.7 slice.58
  69.0 2.0 convert_element_type.38
  71.0 1.5 collective-permute-start.3
  72.5 2.2 broadcast_multiply_fusion
  74.7 1.2 slice_negate_fusion
  75.9 1.1 pad_maximum_fusion
  77.4 1.6 fusion.1
  79.0 1.8 fusion.3
  80.8 1.1 slice_negate_fusion.1
  82.0 2.7 fusion.2
  85.5 20.8 %all-gather.3.cloned.1.call-done = bf16[1024,2688]{0,1:T(8,128)(2,1)} async-done(((bf16[128,2688]{0,1:T(8,128)(2,1)}), bf16[1024,2688]{0,1:T(8,128)(2,1)}) %all-gather.3.cloned.1.call-update) | async-done | bytes 5505040 | tf_op jit(solution)/shard_map/all_gather | solution.py:187
  106.3 10.9 %fusion = bf16[2688,1024]{0,1:T(8,128)(2,1)} fusion(bf16[1024,2688]{0,1:T(8,128)(2,1)} %all-gather.3.cloned.1.call-done, bf16[1024,256]{1,0:T(8,128)(2,1)S(1)} %bitcast.63, bf16[1024,256]{1,0:T(8,128)(2,1)S(1)} %bitcast.61, bf16[1024,512]{1,0:T(8,128)(2,1)S(1)} %copy-done.5), kind=kOutput, calls=%fused_computation.7 | convolution fusion | flops 5646188544 | bytes 13107200 | tf_op jit(solution)/shard_map/dot_general | solution.py:188
  117.2 8.3 %copy.34 = bf16[2688,1024]{1,0:T(8,128)(2,1)} copy(bf16[2688,1024]{0,1:T(8,128)(2,1)} %fusion) | data formatting | bytes 11010048
  125.7 82.7 %all-gather.5.cloned.1.call-done = bf16[1024,2688]{0,1:T(8,128)(2,1)} async-done(((bf16[128,2688]{0,1:T(8,128)(2,1)}), bf16[1024,2688]{0,1:T(8,128)(2,1)}) %all-gather.5.cloned.1.call-update) | async-done | bytes 5505040 | tf_op jit(solution)/shard_map/all_gather | solution.py:187
  208.4 10.4 %convolution_convert_fusion = bf16[2688,1024]{1,0:T(8,128)(2,1)} fusion(bf16[1024,2688]{0,1:T(8,128)(2,1)} %all-gather.5.cloned.1.call-done, bf16[1024,256]{1,0:T(8,128)(2,1)S(1)} %bitcast.64, bf16[1024,256]{1,0:T(8,128)(2,1)S(1)} %bitcast.62, bf16[1024,512]{1,0:T(8,128)(2,1)S(1)} %copy-done.5), kind=kOutput, calls=%fused_computation.5 | convolution fusion | flops 5646188544 | bytes 13107200 | tf_op jit(solution)/shard_map/dot_general | solution.py:188
  218.9 1.3 fusion.7
  220.4 59.1 %reduce-scatter.7.cloned.1.call-done = bf16[168,1024]{1,0:T(8,128)(2,1)} async-done(((bf16[2688,1024]{1,0:T(8,128)(2,1)}), bf16[168,1024]{1,0:T(8,128)(2,1)}) %reduce-scatter.7.cloned.1.call-update) | async-done | bytes 344080 | tf_op jit(solution)/shard_map/reduce_scatter | solution.py:192
  279.5 70.7 %reduce-scatter.9.cloned.1.call-done = bf16[168,1024]{1,0:T(8,128)(2,1)} async-done(((bf16[2688,1024]{1,0:T(8,128)(2,1)}), bf16[168,1024]{1,0:T(8,128)(2,1)}) %reduce-scatter.9.cloned.1.call-update) | async-done | bytes 344080 | tf_op jit(solution)/shard_map/reduce_scatter | solution.py:192
  350.2 1.3 maximum_maximum_fusion
  351.5 0.7 gather_fusion
  352.1 1.6 broadcast_select_fusion
  353.7 3.7 all-to-all-start
  358.1 27.3 %all-to-all-done = bf16[16,64,1024]{2,1,0:T(8,128)(2,1)S(1)} async-done(((bf16[16,64,1024]{2,1,0:T(8,128)(2,1)}), bf16[16,64,1024]{2,1,0:T(8,128)(2,1)S(1)}, u32[]{:S(2)}, u32[]{:S(2)}) %all-to-all-start) | async-done | bytes 2097184 | tf_op jit(solution)/shard_map/all_to_all | solution.py:134
  385.4 10.9 %conditional.1 = (f32[1,1,1024,1024]{3,2,1,0:T(8,128)}, f32[1,1,1024,1024]{3,2,1,0:T(8,128)}) conditional(s32[]{:T(128)} %convert_element_type.34, () %tuple.20, (pred[6]{0:T(512)(128)(4,1)S(1)}, s32[6]{0:T(128)S(1)}, bf16[16,64,1024]{2,1,0:T(8,128)(2,1)S(1)}) %tuple.21), branch_computations={%region_4.5_spmd, %region_5.7_spmd} | conditional | flops 4298113024 | bytes 18350140 | solution.py:220
  386.7 0.7 bitcast_select_fusion
  387.5 4.4 %multiply_bitcast_fusion = f32[1,1,1024,1024]{3,2,1,0:T(8,128)} fusion(bf16[1024,1024]{1,0:T(8,128)(2,1)S(1)} %bitcast_select_fusion), kind=kOutput, calls=%fused_computation.1 | convolution fusion | flops 2148532224 | bytes 6291456 | tf_op jit(solution)/shard_map/cond/branch_1_fun/dot_general | solution.py:207
  391.9 4.4 %multiply_bitcast_fusion.1 = f32[1,1,1024,1024]{3,2,1,0:T(8,128)} fusion(bf16[1024,1024]{1,0:T(8,128)(2,1)S(1)} %bitcast_select_fusion), kind=kOutput, calls=%fused_computation.2 | convolution fusion | flops 2148532224 | bytes 6291456 | tf_op jit(solution)/shard_map/cond/branch_1_fun/dot_general | solution.py:201
  (49 shorter events, 2.6 us)
Async XLA Ops:
  7.2 1.3 slice-start
  7.2 99.1 %all-gather.3.cloned.1.call-start = ((), (), s32[]{:S(2)}) async-start(), calls=%async_computation.3 | async-start | bytes 6193152 | tf_op jit(solution)/shard_map/all_gather | solution.py:187
  8.5 2.8 slice-start.1
  11.5 2.0 copy-start.6
  11.5 3.4 copy-start.7
  11.5 7.7 %copy-start.8 = (s32[1024]{0:T(1024)S(1)}, s32[1024]{0:T(1024)}, u32[]{:S(2)}) copy-start(s32[1024]{0:T(1024)} %param.14) | copy-start | bytes 12292
  12.7 195.7 %all-gather.5.cloned.1.call-start = ((), (), s32[]{:S(2)}) async-start(), calls=%async_computation.4 | async-start | bytes 6193152 | tf_op jit(solution)/shard_map/all_gather | solution.py:187
  13.5 266.0 %reduce-scatter.7.cloned.1.call-start = ((), (), s32[]{:S(2)}) async-start(), calls=%async_computation.5 | async-start | bytes 5849088 | tf_op jit(solution)/shard_map/reduce_scatter | solution.py:192
  13.5 10.1 %collective-permute-start = (bf16[1024,256]{1,0:T(8,128)(2,1)S(1)}, bf16[1024,256]{1,0:T(8,128)(2,1)S(1)}, u32[]{:S(2)}, u32[]{:S(2)}) collective-permute-start(bf16[1024,256]{1,0:T(8,128)(2,1)S(1)} %copy-done.6), channel_id=1, source_target_pairs={{0,8},{8,16},{16,24},{24,32},{32,40},{40,48},{48,56},{56,64},{64,7... | collective-permute-start | bytes 1572872 | tf_op jit(solution)/shard_map/ppermute | solution.py:84
  14.9 9.8 %collective-permute-start.1 = (bf16[1024,256]{1,0:T(8,128)(2,1)S(1)}, bf16[1024,256]{1,0:T(8,128)(2,1)S(1)}, u32[]{:S(2)}, u32[]{:S(2)}) collective-permute-start(bf16[1024,256]{1,0:T(8,128)(2,1)S(1)} %copy-done.7), channel_id=1, source_target_pairs={{0,8},{8,16},{16,24},{24,32},{32,40},{40,48},{48,56},{56,64},{64,7... | collective-permute-start | bytes 1572872 | tf_op jit(solution)/shard_map/ppermute | solution.py:84
  53.0 4.6 %copy-start.4 = (f32[2048,256]{1,0:T(8,128)S(1)}, f32[2048,256]{1,0:T(8,128)}, u32[]{:S(2)}) copy-start(f32[2048,256]{1,0:T(8,128)} %get-tuple-element.33) | copy-start | bytes 6291460
  58.7 5.9 %copy-start = (f32[1024,512]{1,0:T(8,128)S(1)}, f32[1024,512]{1,0:T(8,128)}, u32[]{:S(2)}) copy-start(f32[1024,512]{1,0:T(8,128)} %get-tuple-element.31) | copy-start | bytes 6291460
  63.3 15.7 %collective-permute-start.2 = (bf16[1024,2,128]{2,1,0:T(2,128)(2,1)}, bf16[1024,2,128]{2,1,0:T(2,128)(2,1)}, u32[]{:S(2)}, u32[]{:S(2)}) collective-permute-start(bf16[1024,2,128]{2,1,0:T(2,128)(2,1)} %convert_element_type.36), channel_id=1, source_target_pairs={{8,0},{16,8},{24,16},{32,24},{40,32},{48,40},{56,48},{64,56},{72,6... | collective-permute-start | bytes 1572872 | tf_op jit(solution)/shard_map/ppermute | solution.py:84
  71.0 13.8 %collective-permute-start.3 = (bf16[1024,2,128]{2,1,0:T(2,128)(2,1)}, bf16[1024,2,128]{2,1,0:T(2,128)(2,1)S(1)}, u32[]{:S(2)}, u32[]{:S(2)}) collective-permute-start(bf16[1024,2,128]{2,1,0:T(2,128)(2,1)} %convert_element_type.38), channel_id=1, source_target_pairs={{8,0},{16,8},{24,16},{32,24},{40,32},{48,40},{56,48},{64,56},{72,6... | collective-permute-start | bytes 1572872 | tf_op jit(solution)/shard_map/ppermute | solution.py:84
  75.9 1.2 copy-start.1
  77.4 1.6 copy-start.2
  82.0 2.8 copy-start.3
  84.7 21.6 %copy-start.5 = (bf16[1024,512]{1,0:T(8,128)(2,1)S(1)}, bf16[1024,512]{1,0:T(8,128)(2,1)}, u32[]{:S(2)}) copy-start(bf16[1024,512]{1,0:T(8,128)(2,1)} %fusion.1) | copy-start | bytes 3145732
  125.4 224.7 %reduce-scatter.9.cloned.1.call-start = ((), (), s32[]{:S(2)}) async-start(), calls=%async_computation.6 | async-start | bytes 5849088 | tf_op jit(solution)/shard_map/reduce_scatter | solution.py:192
  353.7 31.7 %all-to-all-start = ((bf16[16,64,1024]{2,1,0:T(8,128)(2,1)}), bf16[16,64,1024]{2,1,0:T(8,128)(2,1)S(1)}, u32[]{:S(2)}, u32[]{:S(2)}) async-start(bf16[16,64,1024]{2,1,0:T(8,128)(2,1)} %broadcast_select_fusion), calls=%async_computation | async-start | bytes 4194304 | tf_op jit(solution)/shard_map/all_to_all | solution.py:134
Sparse Core Ops, SparseCore 0:
  12.8 93.3 all-gather.2
  108.4 99.9 all-gather.4
  210.8 68.5 reduce-scatter.6
  281.7 68.4 reduce-scatter.8

commit v3 on v1

--- a/solution.py
+++ b/solution.py
@@ -118,7 +118,17 @@
     piece = BLOCK // seq_count
     tail_piece = (D - full_blocks * BLOCK) // seq_count
     columns = arranged.shape[1]
-    mine = lax.psum_scatter(arranged, "seq", scatter_dimension=0, tiled=True)
+    core = lax.axis_index("seq") % 2
+    paired = arranged.reshape(seq_count // 2, 2, -1, columns)
+    kept = lax.dynamic_index_in_dim(paired, core, 1, keepdims=False)
+    given = lax.dynamic_index_in_dim(paired, 1 - core, 1, keepdims=False)
+    taken = lax.ppermute(given, "seq", [(src, src ^ 1) for src in range(seq_count)])
+    summed = (kept.astype(jnp.float32) + taken.astype(jnp.float32)).astype(jnp.bfloat16)
+    groups = [list(range(parity, seq_count, 2)) for parity in range(2)]
+    mine = lax.psum_scatter(
+        summed.reshape(-1, columns), "seq", scatter_dimension=0, tiled=True,
+        axis_index_groups=groups,
+    )
     mine = jnp.concatenate(
         [mine, jnp.zeros((NBLK * piece - mine.shape[0], columns), mine.dtype)], 0
     ).reshape(NBLK, piece, columns)

time: 324 us -> 331 us (1.022)
  other arithmetic: 23.3 us -> 32.9 us
  local copies, waits for them, and re-layouts: 24.3 us -> 30.3 us
  waiting for transfers between devices: 192 us -> 187 us
  matrix products: 27.2 us -> 23.2 us
    reduce_scatter x1, waiting for transfers between devices: 87.9 us -> 73.8 us  [owned_block(): lax.psum_scatter(summed.reshape(-1, columns), 'seq', scatter_dimension=0,...]
    convert_element_type x0 -> x1, other arithmetic: none -> 9.67 us  [owned_block(): (kept.astype(jnp.float32) + taken.astype(jnp.float32)).astype(jnp.bfloat16)]
    ppermute x0 -> x1, waiting for transfers between devices: none -> 9.37 us  [owned_block(): lax.ppermute(given, 'seq', [(src, src ^ 1) for src in range(seq_count)])]
    dot_general x1, matrix products: 18.4 us -> 14.4 us  [per_device(): lax.dot_general(lax.all_gather(arrange_features(inputs, seq_count), 'head...]
    squeeze x0 -> x1, local copies, waits for them, and re-layouts: none -> 3.42 us  [owned_block(): given = lax.dynamic_index_in_dim(paired, 1 - core, 1, keepdims=False)]
  transfers between devices with their start and end apart: 7 -> 8, of which waited for: 3 -> 4; matrix products, arithmetic and copies ran while one was open for 12% -> 11% of each run, Pallas kernels for 9% -> 8%
where the time goes in v3:
time: 331 us; the launch traced here: 329 us
  waiting for transfers between devices  187 us (56%)
  other arithmetic  32.9 us (10%)
  local copies, waits for them, and re-layouts  30.3 us (9%)
  Pallas kernels  27.8 us (8%)
  matrix products  23.2 us (7%)
  between operations  15 us (5%)
  starting transfers between devices  12.2 us (4%)
    all_gather x1, waiting for transfers between devices, per_device(): lax.all_gather(arrange_features(inputs, seq_count), 'head', axis=0, tiled...  76.5 us
    reduce_scatter x1, waiting for transfers between devices, owned_block(): lax.psum_scatter(summed.reshape(-1, columns), 'seq', scatter_dimension=0,...  73.8 us
    pallas_call x1, Pallas kernels, attention_backward(): pl.pallas_call(attention_kernel, out_shape=(jax.ShapeDtypeStruct(queries....  27.8 us
    all_to_all x1, waiting for transfers between devices, owned_block(): received = lax.all_to_all(send, 'seq', 0, 0, tiled=False)  27.3 us
    dot_general x1, matrix products, per_device(): lax.dot_general(lax.all_gather(arrange_features(inputs, seq_count), 'head...  14.4 us
    convert_element_type x1, other arithmetic, owned_block(): (kept.astype(jnp.float32) + taken.astype(jnp.float32)).astype(jnp.bfloat16)  9.67 us
    ppermute x1, waiting for transfers between devices, owned_block(): lax.ppermute(given, 'seq', [(src, src ^ 1) for src in range(seq_count)])  9.37 us
    ppermute x4, starting transfers between devices, shifted(): lax.ppermute(value, axis, [(source, source + steps) for source in range(i...  8.39 us
  transfers between devices with their start and end apart: 8, of which 4 were waited for; matrix products, arithmetic and copies ran while one was open for 11% of the time, Pallas kernels for 8%

profile of v3, /device:TPU:0, one launch (start us, length us, event | category | flops | bytes accessed | tf_op | source)
XLA Modules:
  0.0 329.1 jit_solution(878941536003645365)
XLA Ops:
  7.2 1.3 slice-done
  8.5 1.4 copy.21
  9.9 1.4 copy.18
  11.5 1.2 pad_maximum_fusion.1
  12.7 1.3 collective-permute-start
  14.1 4.3 %collective-permute-start.1 = (bf16[1024,256]{1,0:T(8,128)(2,1)S(1)}, bf16[1024,256]{1,0:T(8,128)(2,1)S(1)}, u32[]{:S(2)}, u32[]{:S(2)}) collective-permute-start(bf16[1024,256]{1,0:T(8,128)(2,1)S(1)} %copy-done.8), channel_id=1, source_target_pairs={{0,8},{8,16},{16,24},{24,32},{32,40},{40,48},{48,56},{56,64},{64,7... | collective-permute-start | bytes 1572872 | tf_op jit(solution)/shard_map/ppermute | solution.py:84
  18.5 1.1 copy.20.band_ref
  19.5 1.9 multiply_cosine_fusion
  21.4 1.3 pad_maximum_fusion.4
  22.7 1.0 pad_maximum_fusion.2.k_ref
  23.8 1.0 pad_maximum_fusion.3.v_ref
  24.8 27.8 %shard_map.90 = (f32[1024,512]{1,0:T(8,128)}, f32[2048,256]{1,0:T(8,128)}, f32[2048,256]{1,0:T(8,128)}) custom-call(s32[1024,1]{1,0:T(8,128)} %copy.20.band_ref, bf16[1024,512]{1,0:T(8,128)(2,1)} %q_ref.1, bf16[1024,512]{1,0:T(8,128)(2,1)} %do_ref.1, bf16[2048,256]{1,0:T(8,128)(2,1)} %pad_maximum_fusion.2.k_ref, bf16[2048,256]{1,0:T(8,128)(2,1)} %pad_maximum_fusion.3.v_ref), custom_call_target="tpu_custom_call" | custom-call | tf_op jit(solution)/shard_map/pallas_call | solution.py:69
  52.7 2.4 slice.48
  55.1 2.1 slice.69
  57.2 1.0 slice.53
  58.2 0.9 slice.68
  59.1 1.7 slice.49
  60.9 2.0 convert_element_type.42
  62.9 1.3 collective-permute-start.2
  64.2 1.7 reshape.95
  65.9 2.7 slice.54
  68.7 2.0 convert_element_type.44
  70.6 1.5 collective-permute-start.3
  72.1 2.3 broadcast_multiply_fusion
  74.4 1.2 slice_negate_fusion
  75.6 1.1 pad_maximum_fusion
  77.2 1.6 fusion.1
  78.8 1.8 fusion.8
  80.5 1.1 slice_negate_fusion.1
  81.7 2.7 fusion.7
  85.2 76.5 %all-gather.2.cloned.1.call-done = bf16[1024,5376]{0,1:T(8,128)(2,1)} async-done(((bf16[128,5376]{0,1:T(8,128)(2,1)}), bf16[1024,5376]{0,1:T(8,128)(2,1)}) %all-gather.2.cloned.1.call-update) | async-done | bytes 11010064 | tf_op jit(solution)/shard_map/all_gather | solution.py:195
  161.6 14.4 %convolution_convert_fusion = bf16[5376,1024]{1,0:T(8,128)(2,1)S(1)} fusion(bf16[1024,5376]{0,1:T(8,128)(2,1)} %all-gather.2.cloned.1.call-done, bf16[1024,256]{1,0:T(8,128)(2,1)S(1)} %bitcast.65, bf16[1024,256]{1,0:T(8,128)(2,1)S(1)} %bitcast.64, bf16[1024,512]{1,0:T(8,128)(2,1)S(1)} %copy-done.6), kind=kOutput, calls=%fused_computation.5 | convolution fusion | flops 11286085632 | bytes 24117248 | tf_op jit(solution)/shard_map/dot_general | solution.py:194
  176.0 3.4 %dynamic-slice_bitcast_fusion = bf16[8,336,1024]{2,1,0:T(8,128)(2,1)} fusion(bf16[8,2,336,1024]{3,2,1,0:T(8,128)(2,1)S(1)} %bitcast.53, s32[]{:T(128)S(6)} %select_n.62), kind=kLoop, calls=%fused_computation.8 | loop fusion | bytes 11010052 | tf_op jit(solution)/shard_map/jit(dynamic_index_in_dim)/squeeze | solution.py:124
  179.4 2.5 copy-done
  181.9 9.4 %collective-permute-done.4 = bf16[8,336,1024]{2,1,0:T(8,128)(2,1)} collective-permute-done((bf16[8,336,1024]{2,1,0:T(8,128)(2,1)}, bf16[8,336,1024]{2,1,0:T(8,128)(2,1)}, u32[]{:S(2)}, u32[]{:S(2)}) %collective-permute-start.4) | collective-permute-done | bytes 5505056 | tf_op jit(solution)/shard_map/ppermute | solution.py:125
  191.3 9.7 %fusion = bf16[8,336,1024]{2,1,0:T(8,128)(2,1)} fusion(bf16[8,336,1024]{2,1,0:T(8,128)(2,1)} %collective-permute-done.4, bf16[8,2,336,1024]{3,2,1,0:T(8,128)(2,1)} %bitcast.54, s32[]{:T(128)S(6)} %select_n.61), kind=kLoop, calls=%fused_computation.7 | loop fusion | flops 11010048 | bytes 16515076 | tf_op jit(solution)/shard_map/convert_element_type | solution.py:126
  201.0 1.3 fusion.12
  202.4 73.8 %reduce-scatter.2.cloned.1.call-done = bf16[336,1024]{1,0:T(8,128)(2,1)} async-done(((bf16[2688,1024]{1,0:T(8,128)(2,1)}), bf16[336,1024]{1,0:T(8,128)(2,1)}) %reduce-scatter.2.cloned.1.call-update) | async-done | bytes 688144 | tf_op jit(solution)/shard_map/reduce_scatter | solution.py:128
  276.3 1.2 concatenate.42
  277.4 0.7 gather_fusion
  278.1 1.6 broadcast_select_fusion
  279.7 3.7 %all-to-all-start = ((bf16[16,64,1024]{2,1,0:T(8,128)(2,1)}), bf16[16,64,1024]{2,1,0:T(8,128)(2,1)S(1)}, u32[]{:S(2)}, u32[]{:S(2)}) async-start(bf16[16,64,1024]{2,1,0:T(8,128)(2,1)} %broadcast_select_fusion), calls=%async_computation.1 | async-start | bytes 4194304 | tf_op jit(solution)/shard_map/all_to_all | solution.py:145
  284.1 27.3 %all-to-all-done = bf16[16,64,1024]{2,1,0:T(8,128)(2,1)S(1)} async-done(((bf16[16,64,1024]{2,1,0:T(8,128)(2,1)}), bf16[16,64,1024]{2,1,0:T(8,128)(2,1)S(1)}, u32[]{:S(2)}, u32[]{:S(2)}) %all-to-all-start) | async-done | bytes 2097184 | tf_op jit(solution)/shard_map/all_to_all | solution.py:145
  311.4 10.9 %conditional.1 = (f32[1,1,1024,1024]{3,2,1,0:T(8,128)}, f32[1,1,1024,1024]{3,2,1,0:T(8,128)}) conditional(s32[]{:T(128)} %convert_element_type.40, () %tuple.20, (pred[6]{0:T(512)(128)(4,1)S(1)}, s32[6]{0:T(128)S(1)}, bf16[16,64,1024]{2,1,0:T(8,128)(2,1)S(1)}) %tuple.21), branch_computations={%region_3.4_spmd, %region_4.6_spmd} | conditional | flops 4298113024 | bytes 18350140 | solution.py:225
  311.4 0.6 select_reduce_fusion
  312.7 0.7 bitcast_select_fusion
  313.5 4.4 %multiply_bitcast_fusion = f32[1,1,1024,1024]{3,2,1,0:T(8,128)} fusion(bf16[1024,1024]{1,0:T(8,128)(2,1)S(1)} %bitcast_select_fusion), kind=kOutput, calls=%fused_computation.1 | convolution fusion | flops 2148532224 | bytes 6291456 | tf_op jit(solution)/shard_map/cond/branch_1_fun/dot_general | solution.py:212
  317.9 4.4 %multiply_bitcast_fusion.1 = f32[1,1,1024,1024]{3,2,1,0:T(8,128)} fusion(bf16[1024,1024]{1,0:T(8,128)(2,1)S(1)} %bitcast_select_fusion), kind=kOutput, calls=%fused_computation.2 | convolution fusion | flops 2148532224 | bytes 6291456 | tf_op jit(solution)/shard_map/cond/branch_1_fun/dot_general | solution.py:206
  (45 shorter events, 1.5 us)
Async XLA Ops:
  7.2 1.3 slice-start
  7.2 154.4 %all-gather.2.cloned.1.call-start = ((), (), s32[]{:S(2)}) async-start(), calls=%async_computation.2 | async-start | bytes 12386304 | tf_op jit(solution)/shard_map/all_gather | solution.py:195
  8.5 2.8 slice-start.1
  11.5 1.3 copy-start.7
  11.5 2.6 copy-start.8
  11.5 7.0 %copy-start.9 = (s32[1024]{0:T(1024)S(1)}, s32[1024]{0:T(1024)}, u32[]{:S(2)}) copy-start(s32[1024]{0:T(1024)} %param.14) | copy-start | bytes 12292
  12.7 263.6 %reduce-scatter.2.cloned.1.call-start = ((), (), s32[]{:S(2)}) async-start(), calls=%async_computation.3 | async-start | bytes 6193152 | tf_op jit(solution)/shard_map/reduce_scatter | solution.py:128
  12.7 10.0 %collective-permute-start = (bf16[1024,256]{1,0:T(8,128)(2,1)S(1)}, bf16[1024,256]{1,0:T(8,128)(2,1)S(1)}, u32[]{:S(2)}, u32[]{:S(2)}) collective-permute-start(bf16[1024,256]{1,0:T(8,128)(2,1)S(1)} %copy-done.7), channel_id=1, source_target_pairs={{0,8},{8,16},{16,24},{24,32},{32,40},{40,48},{48,56},{56,64},{64,7... | collective-permute-start | bytes 1572872 | tf_op jit(solution)/shard_map/ppermute | solution.py:84
  14.1 9.7 %collective-permute-start.1 = (bf16[1024,256]{1,0:T(8,128)(2,1)S(1)}, bf16[1024,256]{1,0:T(8,128)(2,1)S(1)}, u32[]{:S(2)}, u32[]{:S(2)}) collective-permute-start(bf16[1024,256]{1,0:T(8,128)(2,1)S(1)} %copy-done.8), channel_id=1, source_target_pairs={{0,8},{8,16},{16,24},{24,32},{32,40},{40,48},{48,56},{56,64},{64,7... | collective-permute-start | bytes 1572872 | tf_op jit(solution)/shard_map/ppermute | solution.py:84
  52.7 4.5 %copy-start.5 = (f32[2048,256]{1,0:T(8,128)S(1)}, f32[2048,256]{1,0:T(8,128)}, u32[]{:S(2)}) copy-start(f32[2048,256]{1,0:T(8,128)} %get-tuple-element.33) | copy-start | bytes 6291460
  58.2 5.9 %copy-start.1 = (f32[1024,512]{1,0:T(8,128)S(1)}, f32[1024,512]{1,0:T(8,128)}, u32[]{:S(2)}) copy-start(f32[1024,512]{1,0:T(8,128)} %get-tuple-element.31) | copy-start | bytes 6291460
  62.9 15.9 %collective-permute-start.2 = (bf16[1024,2,128]{2,1,0:T(2,128)(2,1)}, bf16[1024,2,128]{2,1,0:T(2,128)(2,1)}, u32[]{:S(2)}, u32[]{:S(2)}) collective-permute-start(bf16[1024,2,128]{2,1,0:T(2,128)(2,1)} %convert_element_type.42), channel_id=1, source_target_pairs={{8,0},{16,8},{24,16},{32,24},{40,32},{48,40},{56,48},{64,56},{72,6... | collective-permute-start | bytes 1572872 | tf_op jit(solution)/shard_map/ppermute | solution.py:84
  70.6 13.9 %collective-permute-start.3 = (bf16[1024,2,128]{2,1,0:T(2,128)(2,1)}, bf16[1024,2,128]{2,1,0:T(2,128)(2,1)S(1)}, u32[]{:S(2)}, u32[]{:S(2)}) collective-permute-start(bf16[1024,2,128]{2,1,0:T(2,128)(2,1)} %convert_element_type.44), channel_id=1, source_target_pairs={{8,0},{16,8},{24,16},{32,24},{40,32},{48,40},{56,48},{64,56},{72,6... | collective-permute-start | bytes 1572872 | tf_op jit(solution)/shard_map/ppermute | solution.py:84
  75.6 1.2 copy-start.2
  77.1 1.6 copy-start.3
  81.7 2.8 copy-start.4
  84.4 77.2 %copy-start.6 = (bf16[1024,512]{1,0:T(8,128)(2,1)S(1)}, bf16[1024,512]{1,0:T(8,128)(2,1)}, u32[]{:S(2)}) copy-start(bf16[1024,512]{1,0:T(8,128)(2,1)} %fusion.1) | copy-start | bytes 3145732
  176.0 5.9 %copy-start = (bf16[5376,1024]{1,0:T(8,128)(2,1)}, bf16[5376,1024]{1,0:T(8,128)(2,1)S(1)}, u32[]{:S(2)}) copy-start(bf16[5376,1024]{1,0:T(8,128)(2,1)S(1)} %convolution_convert_fusion) | copy-start | bytes 33030148
  181.9 9.4 %collective-permute-start.4 = (bf16[8,336,1024]{2,1,0:T(8,128)(2,1)}, bf16[8,336,1024]{2,1,0:T(8,128)(2,1)}, u32[]{:S(2)}, u32[]{:S(2)}) collective-permute-start(bf16[8,336,1024]{2,1,0:T(8,128)(2,1)} %dynamic-slice_bitcast_fusion), channel_id=1, source_target_pairs={{0,8},{8,0},{16,24},{24,16},{32,40},{40,32},{48,56},{56,48},{64,72... | collective-permute-start | bytes 16515080 | tf_op jit(solution)/shard_map/ppermute | solution.py:125
  279.7 31.7 %all-to-all-start = ((bf16[16,64,1024]{2,1,0:T(8,128)(2,1)}), bf16[16,64,1024]{2,1,0:T(8,128)(2,1)S(1)}, u32[]{:S(2)}, u32[]{:S(2)}) async-start(bf16[16,64,1024]{2,1,0:T(8,128)(2,1)} %broadcast_select_fusion), calls=%async_computation.1 | async-start | bytes 4194304 | tf_op jit(solution)/shard_map/all_to_all | solution.py:145
Sparse Core Ops, SparseCore 0:
  12.8 148.7 all-gather.1
  201.1 75.1 reduce-scatter.1

commit v4 on v1

--- a/solution.py
+++ b/solution.py
@@ -113,12 +113,11 @@
     return jnp.concatenate([main, tail], 2).reshape(count, D)
 
 
-def owned_block(arranged, owner_row, block_pick, seq_count):
+def owned_block(mine, owner_row, block_pick, seq_count):
     full_blocks = D // BLOCK
     piece = BLOCK // seq_count
     tail_piece = (D - full_blocks * BLOCK) // seq_count
-    columns = arranged.shape[1]
-    mine = lax.psum_scatter(arranged, "seq", scatter_dimension=0, tiled=True)
+    columns = mine.shape[1]
     mine = jnp.concatenate(
         [mine, jnp.zeros((NBLK * piece - mine.shape[0], columns), mine.dtype)], 0
     ).reshape(NBLK, piece, columns)
@@ -181,16 +180,35 @@
         1,
     ).astype(jnp.bfloat16)
     column_count = column_grads.shape[1]
-    partial_sum = lax.dot_general(
-        lax.all_gather(arrange_features(inputs, seq_count), "head", axis=0, tiled=True),
-        column_grads,
-        (((0,), (0,)), ((), ())),
+    core = seq_index % 2
+    paired = arrange_features(inputs, seq_count).reshape(inputs.shape[0], seq_count // 2, 2, -1)
+    local = jnp.concatenate(
+        [
+            lax.dynamic_index_in_dim(paired, 1 - core, 2, keepdims=False),
+            lax.dynamic_index_in_dim(paired, core, 2, keepdims=False),
+        ],
+        1,
+    ).reshape(inputs.shape[0], D)
+    gathered = lax.all_gather(local, "head", axis=0, tiled=True)
+    half = D // 2
+    given = lax.dot_general(
+        gathered[:, :half], column_grads, (((0,), (0,)), ((), ())),
         preferred_element_type=jnp.float32,
+    ).astype(jnp.bfloat16)
+    taken = lax.ppermute(given, "seq", [(src, src ^ 1) for src in range(seq_count)])
+    kept = lax.dot_general(
+        gathered[:, half:], column_grads, (((0,), (0,)), ((), ())),
+        preferred_element_type=jnp.float32,
+    ).astype(jnp.bfloat16)
+    summed = (kept.astype(jnp.float32) + taken.astype(jnp.float32)).astype(jnp.bfloat16)
+    groups = [list(range(parity, seq_count, 2)) for parity in range(2)]
+    mine = lax.psum_scatter(
+        summed, "seq", scatter_dimension=0, tiled=True, axis_index_groups=groups
     )
     owner_row = lax.dynamic_index_in_dim(owners, group_index, 0, keepdims=False)
     is_mine = owner_row == seq_index
     block_pick = jnp.sum(jnp.where(is_mine, jnp.arange(NBLK, dtype=jnp.int32), 0))
-    block_part = owned_block(partial_sum.astype(jnp.bfloat16), owner_row, block_pick, seq_count)
+    block_part = owned_block(mine, owner_row, block_pick, seq_count)
     def gram_pair(part_rows):
         left_value = (
             lax.dot_general(

time: 324 us -> 317 us (0.978)
  waiting for transfers between devices: 192 us -> 187 us
    reduce_scatter x1, waiting for transfers between devices: 87.9 us -> 73.8 us  [per_device(): lax.psum_scatter(summed, 'seq', scatter_dimension=0, tiled=True, axis_ind...]
    ppermute x0 -> x1, waiting for transfers between devices: none -> 9.02 us  [per_device(): lax.ppermute(given, 'seq', [(src, src ^ 1) for src in range(seq_count)])]
    dot_general x1 -> x2, matrix products: 18.4 us -> 16.6 us  [the longest x1 9 us: per_device(): lax.dot_general(gathered[:, :half], column_grads, (((0,), (0,)), ((), ())...]
  transfers between devices with their start and end apart: 7 -> 8, of which waited for: 3 -> 4; matrix products, arithmetic and copies ran while one was open for 12% -> 12% of each run, Pallas kernels for 9% -> 9%
where the time goes in v4:
time: 317 us; the launch traced here: 316 us
  waiting for transfers between devices  187 us (59%)
  Pallas kernels  27.9 us (9%)
  matrix products  25.4 us (8%)
  local copies, waits for them, and re-layouts  24.4 us (8%)
  other arithmetic  23.4 us (7%)
  between operations  15 us (5%)
  starting transfers between devices  12.5 us (4%)
    all_gather x1, waiting for transfers between devices, per_device(): gathered = lax.all_gather(local, 'head', axis=0, tiled=True)  76.5 us
    reduce_scatter x1, waiting for transfers between devices, per_device(): lax.psum_scatter(summed, 'seq', scatter_dimension=0, tiled=True, axis_ind...  73.8 us
    pallas_call x1, Pallas kernels, attention_backward(): pl.pallas_call(attention_kernel, out_shape=(jax.ShapeDtypeStruct(queries....  27.9 us
    all_to_all x1, waiting for transfers between devices, owned_block(): received = lax.all_to_all(send, 'seq', 0, 0, tiled=False)  27.3 us
    ppermute x1, waiting for transfers between devices, per_device(): lax.ppermute(given, 'seq', [(src, src ^ 1) for src in range(seq_count)])  9.02 us
    dot_general x1, matrix products, per_device(): lax.dot_general(gathered[:, :half], column_grads, (((0,), (0,)), ((), ())...  9 us
    ppermute x4, starting transfers between devices, shifted(): lax.ppermute(value, axis, [(source, source + steps) for source in range(i...  8.39 us
    dot_general x1, matrix products, per_device(): lax.dot_general(gathered[:, half:], column_grads, (((0,), (0,)), ((), ())...  7.61 us
  transfers between devices with their start and end apart: 8, of which 4 were waited for; matrix products, arithmetic and copies ran while one was open for 12% of the time, Pallas kernels for 9%

profile of v4, /device:TPU:0, one launch (start us, length us, event | category | flops | bytes accessed | tf_op | source)
XLA Modules:
  0.0 315.9 jit_solution(1073281339018266322)
XLA Ops:
  7.2 1.2 slice-done
  8.5 1.4 copy.21
  9.9 1.4 copy.18
  11.6 1.2 pad_maximum_fusion.2
  12.9 1.3 collective-permute-start
  14.2 4.3 %collective-permute-start.1 = (bf16[1024,256]{1,0:T(8,128)(2,1)S(1)}, bf16[1024,256]{1,0:T(8,128)(2,1)S(1)}, u32[]{:S(2)}, u32[]{:S(2)}) collective-permute-start(bf16[1024,256]{1,0:T(8,128)(2,1)S(1)} %copy-done.7), channel_id=1, source_target_pairs={{0,8},{8,16},{16,24},{24,32},{32,40},{40,48},{48,56},{56,64},{64,7... | collective-permute-start | bytes 1572872 | tf_op jit(solution)/shard_map/ppermute | solution.py:84
  18.6 1.1 copy.20.band_ref
  19.7 1.9 multiply_cosine_fusion
  21.6 1.3 pad_maximum_fusion.7
  22.9 1.0 pad_maximum_fusion.3.k_ref
  23.9 1.0 pad_maximum_fusion.4.v_ref
  24.9 27.9 %shard_map.90 = (f32[1024,512]{1,0:T(8,128)}, f32[2048,256]{1,0:T(8,128)}, f32[2048,256]{1,0:T(8,128)}) custom-call(s32[1024,1]{1,0:T(8,128)} %copy.20.band_ref, bf16[1024,512]{1,0:T(8,128)(2,1)} %q_ref.1, bf16[1024,512]{1,0:T(8,128)(2,1)} %do_ref.1, bf16[2048,256]{1,0:T(8,128)(2,1)} %pad_maximum_fusion.3.k_ref, bf16[2048,256]{1,0:T(8,128)(2,1)} %pad_maximum_fusion.4.v_ref), custom_call_target="tpu_custom_call" | custom-call | tf_op jit(solution)/shard_map/pallas_call | solution.py:69
  52.8 2.4 slice.55
  55.2 2.1 slice.85
  57.3 1.0 slice.60
  58.4 0.9 slice.84
  59.2 1.7 slice.56
  61.0 2.0 convert_element_type.42
  63.0 1.3 collective-permute-start.2
  64.3 1.7 reshape.85
  66.0 2.7 slice.61
  68.8 2.0 convert_element_type.44
  70.8 1.5 collective-permute-start.3
  72.2 2.3 broadcast_multiply_fusion
  74.5 1.2 slice_negate_fusion
  75.7 1.1 pad_maximum_fusion
  76.9 0.4 mul.59
  77.3 1.6 fusion.4
  78.9 1.8 fusion.10
  80.6 1.1 slice_negate_fusion.1
  81.8 2.7 fusion.5
  84.6 0.5 add_convert_fusion.1
  85.3 76.5 %all-gather.2.cloned.1.call-done = bf16[1024,5376]{0,1:T(8,128)(2,1)} async-done(((bf16[128,5376]{0,1:T(8,128)(2,1)}), bf16[1024,5376]{0,1:T(8,128)(2,1)}) %all-gather.2.cloned.1.call-update) | async-done | bytes 11010064 | tf_op jit(solution)/shard_map/all_gather | solution.py:192
  161.8 9.0 %convolution_convert_fusion = bf16[2688,1024]{1,0:T(8,128)(2,1)S(1)} fusion(bf16[1024,5376]{0,1:T(8,128)(2,1)} %all-gather.2.cloned.1.call-done, bf16[1024,256]{1,0:T(8,128)(2,1)S(1)} %bitcast.59, bf16[1024,256]{1,0:T(8,128)(2,1)S(1)} %bitcast.57, bf16[1024,512]{1,0:T(8,128)(2,1)S(1)} %copy-done.5), kind=kOutput, calls=%fused_computation.6 | convolution fusion | flops 5646188544 | bytes 13107200 | tf_op jit(solution)/shard_map/dot_general | solution.py:194
  171.1 9.0 %collective-permute-done.4 = bf16[2688,1024]{1,0:T(8,128)(2,1)S(1)} collective-permute-done((bf16[2688,1024]{1,0:T(8,128)(2,1)S(1)}, bf16[2688,1024]{1,0:T(8,128)(2,1)S(1)}, u32[]{:S(2)}, u32[]{:S(2)}) %collective-permute-start.4) | collective-permute-done | bytes 5505056 | tf_op jit(solution)/shard_map/ppermute | solution.py:198
  180.1 7.6 %add_convert_fusion = bf16[2688,1024]{1,0:T(8,128)(2,1)} fusion(bf16[2688,1024]{1,0:T(8,128)(2,1)S(1)} %collective-permute-done.4, bf16[1024,5376]{0,1:T(8,128)(2,1)S(1)} %copy-done.9, bf16[1024,256]{1,0:T(8,128)(2,1)S(1)} %bitcast.60, bf16[1024,256]{1,0:T(8,128)(2,1)S(1)} %bitcast.58, bf16[1024,512]{1,0:T(8,128)(2,1)S(1)} %copy-done.5), kind=kOutput, calls=%fused_computation.5 | convolution fusion | flops 5657198592 | bytes 18612224 | tf_op jit(solution)/shard_map/dot_general | solution.py:199
  187.7 1.3 fusion.15
  189.2 73.8 %reduce-scatter.2.cloned.1.call-done = bf16[336,1024]{1,0:T(8,128)(2,1)} async-done(((bf16[2688,1024]{1,0:T(8,128)(2,1)}), bf16[336,1024]{1,0:T(8,128)(2,1)}) %reduce-scatter.2.cloned.1.call-update) | async-done | bytes 688144 | tf_op jit(solution)/shard_map/reduce_scatter | solution.py:205
  263.0 1.2 concatenate.53
  264.2 0.7 gather_fusion
  264.9 1.6 broadcast_select_fusion
  266.5 3.7 %all-to-all-start = ((bf16[16,64,1024]{2,1,0:T(8,128)(2,1)}), bf16[16,64,1024]{2,1,0:T(8,128)(2,1)S(1)}, u32[]{:S(2)}, u32[]{:S(2)}) async-start(bf16[16,64,1024]{2,1,0:T(8,128)(2,1)} %broadcast_select_fusion), calls=%async_computation.1 | async-start | bytes 4194304 | tf_op jit(solution)/shard_map/all_to_all | solution.py:134
  270.8 27.3 %all-to-all-done = bf16[16,64,1024]{2,1,0:T(8,128)(2,1)S(1)} async-done(((bf16[16,64,1024]{2,1,0:T(8,128)(2,1)}), bf16[16,64,1024]{2,1,0:T(8,128)(2,1)S(1)}, u32[]{:S(2)}, u32[]{:S(2)}) %all-to-all-start) | async-done | bytes 2097184 | tf_op jit(solution)/shard_map/all_to_all | solution.py:134
  298.1 10.9 %conditional.1 = (f32[1,1,1024,1024]{3,2,1,0:T(8,128)}, f32[1,1,1024,1024]{3,2,1,0:T(8,128)}) conditional(s32[]{:T(128)} %convert_element_type.40, () %tuple.20, (pred[6]{0:T(512)(128)(4,1)S(1)}, s32[6]{0:T(128)S(1)}, bf16[16,64,1024]{2,1,0:T(8,128)(2,1)S(1)}) %tuple.21), branch_computations={%region_3.4_spmd, %region_4.6_spmd} | conditional | flops 4298113024 | bytes 18350140 | solution.py:233
  298.2 0.6 select_reduce_fusion
  299.5 0.7 bitcast_select_fusion
  300.2 4.4 %multiply_bitcast_fusion = f32[1,1,1024,1024]{3,2,1,0:T(8,128)} fusion(bf16[1024,1024]{1,0:T(8,128)(2,1)S(1)} %bitcast_select_fusion), kind=kOutput, calls=%fused_computation.1 | convolution fusion | flops 2148532224 | bytes 6291456 | tf_op jit(solution)/shard_map/cond/branch_1_fun/dot_general | solution.py:220
  304.7 4.4 %multiply_bitcast_fusion.1 = f32[1,1,1024,1024]{3,2,1,0:T(8,128)} fusion(bf16[1024,1024]{1,0:T(8,128)(2,1)S(1)} %bitcast_select_fusion), kind=kOutput, calls=%fused_computation.2 | convolution fusion | flops 2148532224 | bytes 6291456 | tf_op jit(solution)/shard_map/cond/branch_1_fun/dot_general | solution.py:214
  (45 shorter events, 1.0 us)
Async XLA Ops:
  7.2 1.3 slice-start
  7.2 154.6 %all-gather.2.cloned.1.call-start = ((), (), s32[]{:S(2)}) async-start(), calls=%async_computation.2 | async-start | bytes 12386304 | tf_op jit(solution)/shard_map/all_gather | solution.py:192
  8.5 2.8 slice-start.1
  11.6 1.3 copy-start.6
  11.6 2.6 copy-start.7
  11.6 7.0 %copy-start.8 = (s32[1024]{0:T(1024)S(1)}, s32[1024]{0:T(1024)}, u32[]{:S(2)}) copy-start(s32[1024]{0:T(1024)} %param.14) | copy-start | bytes 12292
  12.8 250.2 %reduce-scatter.2.cloned.1.call-start = ((), (), s32[]{:S(2)}) async-start(), calls=%async_computation.3 | async-start | bytes 6193152 | tf_op jit(solution)/shard_map/reduce_scatter | solution.py:205
  12.9 10.0 %collective-permute-start = (bf16[1024,256]{1,0:T(8,128)(2,1)S(1)}, bf16[1024,256]{1,0:T(8,128)(2,1)S(1)}, u32[]{:S(2)}, u32[]{:S(2)}) collective-permute-start(bf16[1024,256]{1,0:T(8,128)(2,1)S(1)} %copy-done.6), channel_id=1, source_target_pairs={{0,8},{8,16},{16,24},{24,32},{32,40},{40,48},{48,56},{56,64},{64,7... | collective-permute-start | bytes 1572872 | tf_op jit(solution)/shard_map/ppermute | solution.py:84
  14.2 9.7 %collective-permute-start.1 = (bf16[1024,256]{1,0:T(8,128)(2,1)S(1)}, bf16[1024,256]{1,0:T(8,128)(2,1)S(1)}, u32[]{:S(2)}, u32[]{:S(2)}) collective-permute-start(bf16[1024,256]{1,0:T(8,128)(2,1)S(1)} %copy-done.7), channel_id=1, source_target_pairs={{0,8},{8,16},{16,24},{24,32},{32,40},{40,48},{48,56},{56,64},{64,7... | collective-permute-start | bytes 1572872 | tf_op jit(solution)/shard_map/ppermute | solution.py:84
  52.8 4.5 %copy-start.4 = (f32[2048,256]{1,0:T(8,128)S(1)}, f32[2048,256]{1,0:T(8,128)}, u32[]{:S(2)}) copy-start(f32[2048,256]{1,0:T(8,128)} %get-tuple-element.33) | copy-start | bytes 6291460
  58.4 5.9 %copy-start = (f32[1024,512]{1,0:T(8,128)S(1)}, f32[1024,512]{1,0:T(8,128)}, u32[]{:S(2)}) copy-start(f32[1024,512]{1,0:T(8,128)} %get-tuple-element.31) | copy-start | bytes 6291460
  63.0 15.8 %collective-permute-start.2 = (bf16[1024,2,128]{2,1,0:T(2,128)(2,1)}, bf16[1024,2,128]{2,1,0:T(2,128)(2,1)}, u32[]{:S(2)}, u32[]{:S(2)}) collective-permute-start(bf16[1024,2,128]{2,1,0:T(2,128)(2,1)} %convert_element_type.42), channel_id=1, source_target_pairs={{8,0},{16,8},{24,16},{32,24},{40,32},{48,40},{56,48},{64,56},{72,6... | collective-permute-start | bytes 1572872 | tf_op jit(solution)/shard_map/ppermute | solution.py:84
  70.8 13.9 %collective-permute-start.3 = (bf16[1024,2,128]{2,1,0:T(2,128)(2,1)}, bf16[1024,2,128]{2,1,0:T(2,128)(2,1)S(1)}, u32[]{:S(2)}, u32[]{:S(2)}) collective-permute-start(bf16[1024,2,128]{2,1,0:T(2,128)(2,1)} %convert_element_type.44), channel_id=1, source_target_pairs={{8,0},{16,8},{24,16},{32,24},{40,32},{48,40},{56,48},{64,56},{72,6... | collective-permute-start | bytes 1572872 | tf_op jit(solution)/shard_map/ppermute | solution.py:84
  75.7 1.2 copy-start.1
  77.3 1.6 copy-start.2
  81.8 2.8 copy-start.3
  84.5 77.3 %copy-start.5 = (bf16[1024,512]{1,0:T(8,128)(2,1)S(1)}, bf16[1024,512]{1,0:T(8,128)(2,1)}, u32[]{:S(2)}) copy-start(bf16[1024,512]{1,0:T(8,128)(2,1)} %fusion.4) | copy-start | bytes 3145732
  161.8 18.3 %copy-start.9 = (bf16[1024,5376]{0,1:T(8,128)(2,1)S(1)}, bf16[1024,5376]{0,1:T(8,128)(2,1)}, u32[]{:S(2)}) copy-start(bf16[1024,5376]{0,1:T(8,128)(2,1)} %all-gather.2.cloned.1.call-done) | copy-start | bytes 33030148
  170.8 9.3 %collective-permute-start.4 = (bf16[2688,1024]{1,0:T(8,128)(2,1)S(1)}, bf16[2688,1024]{1,0:T(8,128)(2,1)S(1)}, u32[]{:S(2)}, u32[]{:S(2)}) collective-permute-start(bf16[2688,1024]{1,0:T(8,128)(2,1)S(1)} %convolution_convert_fusion), channel_id=1, source_target_pairs={{0,8},{8,0},{16,24},{24,16},{32,40},{40,32},{48,56},{56,48},{64,72... | collective-permute-start | bytes 16515080 | tf_op jit(solution)/shard_map/ppermute | solution.py:198
  266.5 31.7 %all-to-all-start = ((bf16[16,64,1024]{2,1,0:T(8,128)(2,1)}), bf16[16,64,1024]{2,1,0:T(8,128)(2,1)S(1)}, u32[]{:S(2)}, u32[]{:S(2)}) async-start(bf16[16,64,1024]{2,1,0:T(8,128)(2,1)} %broadcast_select_fusion), calls=%async_computation.1 | async-start | bytes 4194304 | tf_op jit(solution)/shard_map/all_to_all | solution.py:134
Sparse Core Ops, SparseCore 0:
  13.0 148.7 all-gather.1
  187.9 75.1 reduce-scatter.1

commit v5 on v4

--- a/solution.py
+++ b/solution.py
@@ -200,6 +200,7 @@
         gathered[:, half:], column_grads, (((0,), (0,)), ((), ())),
         preferred_element_type=jnp.float32,
     ).astype(jnp.bfloat16)
+    kept, taken = lax.optimization_barrier((kept, taken))
     summed = (kept.astype(jnp.float32) + taken.astype(jnp.float32)).astype(jnp.bfloat16)
     groups = [list(range(parity, seq_count, 2)) for parity in range(2)]
     mine = lax.psum_scatter(

time: 317 us -> 313 us (0.987)
  waiting for transfers between devices: 187 us -> 180 us
  other arithmetic: 23.4 us -> 29.8 us
  local copies, waits for them, and re-layouts: 24.4 us -> 20.2 us
    ppermute x1, waiting for transfers between devices: 9.02 us -> 1.82 us  [per_device(): lax.ppermute(given, 'seq', [(src, src ^ 1) for src in range(seq_count)])]
    convert_element_type x0 -> x1, other arithmetic: none -> 5.21 us  [per_device(): (kept.astype(jnp.float32) + taken.astype(jnp.float32)).astype(jnp.bfloat16)]
  transfers between devices with their start and end apart: 8 -> 8, of which waited for: 4 -> 4; matrix products, arithmetic and copies ran while one was open for 12% -> 14% of each run, Pallas kernels for 9% -> 9%
where the time goes in v5:
time: 313 us; the launch traced here: 312 us
  waiting for transfers between devices  180 us (58%)
  other arithmetic  29.8 us (10%)
  Pallas kernels  27.8 us (9%)
  matrix products  25 us (8%)
  local copies, waits for them, and re-layouts  20.2 us (6%)
  between operations  15.1 us (5%)
  starting transfers between devices  12.5 us (4%)
    all_gather x1, waiting for transfers between devices, per_device(): gathered = lax.all_gather(local, 'head', axis=0, tiled=True)  77.4 us
    reduce_scatter x1, waiting for transfers between devices, per_device(): lax.psum_scatter(summed, 'seq', scatter_dimension=0, tiled=True, axis_ind...  73.8 us
    pallas_call x1, Pallas kernels, attention_backward(): pl.pallas_call(attention_kernel, out_shape=(jax.ShapeDtypeStruct(queries....  27.8 us
    all_to_all x1, waiting for transfers between devices, owned_block(): received = lax.all_to_all(send, 'seq', 0, 0, tiled=False)  27.3 us
    dot_general x1, matrix products, per_device(): lax.dot_general(gathered[:, :half], column_grads, (((0,), (0,)), ((), ())...  9 us
    ppermute x4, starting transfers between devices, shifted(): lax.ppermute(value, axis, [(source, source + steps) for source in range(i...  8.39 us
    dot_general x1, matrix products, per_device(): lax.dot_general(gathered[:, half:], column_grads, (((0,), (0,)), ((), ())...  7.18 us
  transfers between devices with their start and end apart: 8, of which 4 were waited for; matrix products, arithmetic and copies ran while one was open for 14% of the time, Pallas kernels for 9%

profile of v5, /device:TPU:0, one launch (start us, length us, event | category | flops | bytes accessed | tf_op | source)
XLA Modules:
  0.0 311.5 jit_solution(17318456360905261515)
XLA Ops:
  7.2 1.2 slice-done
  8.5 0.8 copy.21
  9.6 1.2 pad_maximum_fusion.2
  10.9 1.3 collective-permute-start
  12.3 4.3 %collective-permute-start.1 = (bf16[1024,256]{1,0:T(8,128)(2,1)S(1)}, bf16[1024,256]{1,0:T(8,128)(2,1)S(1)}, u32[]{:S(2)}, u32[]{:S(2)}) collective-permute-start(bf16[1024,256]{1,0:T(8,128)(2,1)S(1)} %copy-done.8), channel_id=1, source_target_pairs={{0,8},{8,16},{16,24},{24,32},{32,40},{40,48},{48,56},{56,64},{64,7... | collective-permute-start | bytes 1572872 | tf_op jit(solution)/shard_map/ppermute | solution.py:84
  16.6 1.0 copy.20.band_ref
  17.7 1.9 multiply_cosine_fusion
  19.6 1.3 pad_maximum_fusion.7
  20.9 1.1 pad_maximum_fusion.3.k_ref
  22.0 1.0 pad_maximum_fusion.4.v_ref
  23.0 27.8 %shard_map.90 = (f32[1024,512]{1,0:T(8,128)}, f32[2048,256]{1,0:T(8,128)}, f32[2048,256]{1,0:T(8,128)}) custom-call(s32[1024,1]{1,0:T(8,128)} %copy.20.band_ref, bf16[1024,512]{1,0:T(8,128)(2,1)} %q_ref.1, bf16[1024,512]{1,0:T(8,128)(2,1)} %do_ref.1, bf16[2048,256]{1,0:T(8,128)(2,1)} %pad_maximum_fusion.3.k_ref, bf16[2048,256]{1,0:T(8,128)(2,1)} %pad_maximum_fusion.4.v_ref), custom_call_target="tpu_custom_call" | custom-call | tf_op jit(solution)/shard_map/pallas_call | solution.py:69
  50.8 1.5 slice.60
  52.3 2.1 slice.82
  54.4 1.0 slice.55
  55.4 0.8 slice.83
  56.3 1.5 slice.61
  57.8 2.1 convert_element_type.44
  59.9 1.3 collective-permute-start.3
  61.2 1.7 slice.56
  62.9 2.0 convert_element_type.42
  64.9 1.5 collective-permute-start.2
  66.4 1.7 reshape.85
  68.1 2.3 broadcast_multiply_fusion
  70.4 1.2 slice_negate_fusion
  71.7 1.1 pad_maximum_fusion
  72.8 0.4 mul.59
  73.2 1.6 fusion.2
  74.8 1.7 add_convert_fusion.1
  76.6 1.8 fusion.8
  78.4 1.1 slice_negate_fusion.1
  79.6 2.7 fusion.3
  82.4 77.4 %all-gather.2.cloned.1.call-done = bf16[1024,5376]{0,1:T(8,128)(2,1)} async-done(((bf16[128,5376]{0,1:T(8,128)(2,1)}), bf16[1024,5376]{0,1:T(8,128)(2,1)}) %all-gather.2.cloned.1.call-update) | async-done | bytes 11010064 | tf_op jit(solution)/shard_map/all_gather | solution.py:192
  159.8 9.0 %convolution_convert_fusion = bf16[2688,1024]{1,0:T(8,128)(2,1)S(1)} fusion(bf16[1024,5376]{0,1:T(8,128)(2,1)} %all-gather.2.cloned.1.call-done, bf16[1024,256]{1,0:T(8,128)(2,1)S(1)} %bitcast.57, bf16[1024,256]{1,0:T(8,128)(2,1)S(1)} %bitcast.59, bf16[1024,512]{1,0:T(8,128)(2,1)S(1)} %copy-done.5), kind=kOutput, calls=%fused_computation.6 | convolution fusion | flops 5646188544 | bytes 13107200 | tf_op jit(solution)/shard_map/dot_general | solution.py:194
  169.1 7.2 %convolution_convert_fusion.1 = bf16[2688,1024]{1,0:T(8,128)(2,1)S(1)} fusion(bf16[1024,5376]{0,1:T(8,128)(2,1)S(1)} %copy-done.10, bf16[1024,256]{1,0:T(8,128)(2,1)S(1)} %bitcast.58, bf16[1024,256]{1,0:T(8,128)(2,1)} %bitcast.60, bf16[1024,512]{1,0:T(8,128)(2,1)S(1)} %copy-done.5), kind=kOutput, calls=%fused_computation.7 | convolution fusion | flops 5646188544 | bytes 13107200 | tf_op jit(solution)/shard_map/dot_general | solution.py:199
  176.3 1.8 collective-permute-done.4
  178.2 5.2 %add_convert_fusion = bf16[2688,1024]{1,0:T(8,128)(2,1)} fusion(bf16[2688,1024]{1,0:T(8,128)(2,1)S(1)} %collective-permute-done.4, bf16[2688,1024]{1,0:T(8,128)(2,1)S(1)} %convolution_convert_fusion.1), kind=kLoop, calls=%fused_computation.5 | loop fusion | flops 11010048 | bytes 16515072 | tf_op jit(solution)/shard_map/convert_element_type | solution.py:204
  183.4 1.3 fusion.13
  184.8 73.8 %reduce-scatter.2.cloned.1.call-done = bf16[336,1024]{1,0:T(8,128)(2,1)} async-done(((bf16[2688,1024]{1,0:T(8,128)(2,1)}), bf16[336,1024]{1,0:T(8,128)(2,1)}) %reduce-scatter.2.cloned.1.call-update) | async-done | bytes 688144 | tf_op jit(solution)/shard_map/reduce_scatter | solution.py:206
  258.7 1.2 concatenate.53
  259.8 0.7 gather_fusion
  260.5 1.6 broadcast_select_fusion
  262.1 3.7 %all-to-all-start = ((bf16[16,64,1024]{2,1,0:T(8,128)(2,1)}), bf16[16,64,1024]{2,1,0:T(8,128)(2,1)S(1)}, u32[]{:S(2)}, u32[]{:S(2)}) async-start(bf16[16,64,1024]{2,1,0:T(8,128)(2,1)} %broadcast_select_fusion), calls=%async_computation.1 | async-start | bytes 4194304 | tf_op jit(solution)/shard_map/all_to_all | solution.py:134
  266.5 27.3 %all-to-all-done = bf16[16,64,1024]{2,1,0:T(8,128)(2,1)S(1)} async-done(((bf16[16,64,1024]{2,1,0:T(8,128)(2,1)}), bf16[16,64,1024]{2,1,0:T(8,128)(2,1)S(1)}, u32[]{:S(2)}, u32[]{:S(2)}) %all-to-all-start) | async-done | bytes 2097184 | tf_op jit(solution)/shard_map/all_to_all | solution.py:134
  293.8 10.9 %conditional.1 = (f32[1,1,1024,1024]{3,2,1,0:T(8,128)}, f32[1,1,1024,1024]{3,2,1,0:T(8,128)}) conditional(s32[]{:T(128)} %convert_element_type.40, () %tuple.21, (pred[6]{0:T(512)(128)(4,1)S(1)}, s32[6]{0:T(128)S(1)}, bf16[16,64,1024]{2,1,0:T(8,128)(2,1)S(1)}) %tuple.23), branch_computations={%region_3.4_spmd, %region_4.6_spmd} | conditional | flops 4298113024 | bytes 18350140 | solution.py:234
  293.8 0.6 select_reduce_fusion
  295.1 0.7 bitcast_select_fusion
  295.9 4.4 %multiply_bitcast_fusion.1 = f32[1,1,1024,1024]{3,2,1,0:T(8,128)} fusion(bf16[1024,1024]{1,0:T(8,128)(2,1)S(1)} %bitcast_select_fusion), kind=kOutput, calls=%fused_computation.2 | convolution fusion | flops 2148532224 | bytes 6291456 | tf_op jit(solution)/shard_map/cond/branch_1_fun/dot_general | solution.py:215
  300.3 4.4 %multiply_bitcast_fusion = f32[1,1,1024,1024]{3,2,1,0:T(8,128)} fusion(bf16[1024,1024]{1,0:T(8,128)(2,1)S(1)} %bitcast_select_fusion), kind=kOutput, calls=%fused_computation.1 | convolution fusion | flops 2148532224 | bytes 6291456 | tf_op jit(solution)/shard_map/cond/branch_1_fun/dot_general | solution.py:221
  (48 shorter events, 1.1 us)
Async XLA Ops:
  7.2 1.3 slice-start
  7.2 152.6 %all-gather.2.cloned.1.call-start = ((), (), s32[]{:S(2)}) async-start(), calls=%async_computation.2 | async-start | bytes 12386304 | tf_op jit(solution)/shard_map/all_gather | solution.py:192
  8.5 0.9 slice-start.1
  9.6 1.3 copy-start.7
  9.6 2.6 copy-start.8
  9.6 7.0 %copy-start.9 = (s32[1024]{0:T(1024)S(1)}, s32[1024]{0:T(1024)}, u32[]{:S(2)}) copy-start(s32[1024]{0:T(1024)} %param.14) | copy-start | bytes 12292
  10.9 247.8 %reduce-scatter.2.cloned.1.call-start = ((), (), s32[]{:S(2)}) async-start(), calls=%async_computation.3 | async-start | bytes 6193152 | tf_op jit(solution)/shard_map/reduce_scatter | solution.py:206
  10.9 10.0 %collective-permute-start = (bf16[1024,256]{1,0:T(8,128)(2,1)S(1)}, bf16[1024,256]{1,0:T(8,128)(2,1)S(1)}, u32[]{:S(2)}, u32[]{:S(2)}) collective-permute-start(bf16[1024,256]{1,0:T(8,128)(2,1)S(1)} %copy-done.7), channel_id=1, source_target_pairs={{0,8},{8,16},{16,24},{24,32},{32,40},{40,48},{48,56},{56,64},{64,7... | collective-permute-start | bytes 1572872 | tf_op jit(solution)/shard_map/ppermute | solution.py:84
  12.3 9.7 %collective-permute-start.1 = (bf16[1024,256]{1,0:T(8,128)(2,1)S(1)}, bf16[1024,256]{1,0:T(8,128)(2,1)S(1)}, u32[]{:S(2)}, u32[]{:S(2)}) collective-permute-start(bf16[1024,256]{1,0:T(8,128)(2,1)S(1)} %copy-done.8), channel_id=1, source_target_pairs={{0,8},{8,16},{16,24},{24,32},{32,40},{40,48},{48,56},{56,64},{64,7... | collective-permute-start | bytes 1572872 | tf_op jit(solution)/shard_map/ppermute | solution.py:84
  50.8 3.6 %copy-start.4 = (f32[2048,256]{1,0:T(8,128)S(1)}, f32[2048,256]{1,0:T(8,128)}, u32[]{:S(2)}) copy-start(f32[2048,256]{1,0:T(8,128)} %get-tuple-element.34) | copy-start | bytes 6291460
  57.8 8.6 %copy-start = (f32[1024,512]{1,0:T(8,128)S(1)}, f32[1024,512]{1,0:T(8,128)}, u32[]{:S(2)}) copy-start(f32[1024,512]{1,0:T(8,128)} %get-tuple-element.33) | copy-start | bytes 6291460
  59.9 14.9 %collective-permute-start.3 = (bf16[1024,2,128]{2,1,0:T(2,128)(2,1)}, bf16[1024,2,128]{2,1,0:T(2,128)(2,1)}, u32[]{:S(2)}, u32[]{:S(2)}) collective-permute-start(bf16[1024,2,128]{2,1,0:T(2,128)(2,1)} %convert_element_type.44), channel_id=1, source_target_pairs={{8,0},{16,8},{24,16},{32,24},{40,32},{48,40},{56,48},{64,56},{72,6... | collective-permute-start | bytes 1572872 | tf_op jit(solution)/shard_map/ppermute | solution.py:84
  64.9 11.7 %collective-permute-start.2 = (bf16[1024,2,128]{2,1,0:T(2,128)(2,1)}, bf16[1024,2,128]{2,1,0:T(2,128)(2,1)}, u32[]{:S(2)}, u32[]{:S(2)}) collective-permute-start(bf16[1024,2,128]{2,1,0:T(2,128)(2,1)} %convert_element_type.42), channel_id=1, source_target_pairs={{8,0},{16,8},{24,16},{32,24},{40,32},{48,40},{56,48},{64,56},{72,6... | collective-permute-start | bytes 1572872 | tf_op jit(solution)/shard_map/ppermute | solution.py:84
  71.7 1.2 copy-start.1
  73.2 1.6 copy-start.3
  74.8 1.8 copy-start.2
  79.5 80.3 %copy-start.5 = (bf16[1024,512]{1,0:T(8,128)(2,1)S(1)}, bf16[1024,512]{1,0:T(8,128)(2,1)}, u32[]{:S(2)}) copy-start(bf16[1024,512]{1,0:T(8,128)(2,1)} %fusion.2) | copy-start | bytes 3145732
  82.4 86.5 %copy-start.6 = (bf16[128,8,2,128]{3,1,2,0:T(8,128)(2,1)}, bf16[128,8,2,128]{3,1,2,0:T(8,128)(2,1)S(1)}, u32[]{:S(2)}) copy-start(bf16[128,8,2,128]{3,1,2,0:T(8,128)(2,1)S(1)} %copy.32) | copy-start | bytes 1572868
  159.8 9.3 %copy-start.10 = (bf16[1024,5376]{0,1:T(8,128)(2,1)S(1)}, bf16[1024,5376]{0,1:T(8,128)(2,1)}, u32[]{:S(2)}) copy-start(bf16[1024,5376]{0,1:T(8,128)(2,1)} %all-gather.2.cloned.1.call-done) | copy-start | bytes 33030148
  168.8 9.3 %collective-permute-start.4 = (bf16[2688,1024]{1,0:T(8,128)(2,1)S(1)}, bf16[2688,1024]{1,0:T(8,128)(2,1)S(1)}, u32[]{:S(2)}, u32[]{:S(2)}) collective-permute-start(bf16[2688,1024]{1,0:T(8,128)(2,1)S(1)} %convolution_convert_fusion), channel_id=1, source_target_pairs={{0,8},{8,0},{16,24},{24,16},{32,40},{40,32},{48,56},{56,48},{64,72... | collective-permute-start | bytes 16515080 | tf_op jit(solution)/shard_map/ppermute | solution.py:198
  262.1 31.7 %all-to-all-start = ((bf16[16,64,1024]{2,1,0:T(8,128)(2,1)}), bf16[16,64,1024]{2,1,0:T(8,128)(2,1)S(1)}, u32[]{:S(2)}, u32[]{:S(2)}) async-start(bf16[16,64,1024]{2,1,0:T(8,128)(2,1)} %broadcast_select_fusion), calls=%async_computation.1 | async-start | bytes 4194304 | tf_op jit(solution)/shard_map/all_to_all | solution.py:134
Sparse Core Ops, SparseCore 0:
  11.0 148.7 all-gather.1
  183.5 75.1 reduce-scatter.1

commit v6 on v5

--- a/solution.py
+++ b/solution.py
@@ -189,7 +189,21 @@
         ],
         1,
     ).reshape(inputs.shape[0], D)
-    gathered = lax.all_gather(local, "head", axis=0, tiled=True)
+    head_count = lax.axis_size("head")
+    lane_count = head_count // 2
+    partner = lax.ppermute(
+        local, "head", [(src, (src + lane_count) % head_count) for src in range(head_count)]
+    )
+    upper = group_index // lane_count
+    pair = jnp.where(upper == 0, jnp.stack([local, partner]), jnp.stack([partner, local]))
+    lanes = [list(range(start, start + lane_count)) for start in (0, lane_count)]
+    gathered = lax.all_gather(pair, "head", axis=0, tiled=False, axis_index_groups=lanes)
+    gathered = gathered.reshape(-1, D)
+    column_grads = (
+        column_grads.reshape(2, lane_count, inputs.shape[0], -1)
+        .transpose(1, 0, 2, 3)
+        .reshape(column_grads.shape)
+    )
     half = D // 2
     given = lax.dot_general(
         gathered[:, :half], column_grads, (((0,), (0,)), ((), ())),

time: 313 us -> 303 us (0.968)
  waiting for transfers between devices: 180 us -> 157 us
  local copies, waits for them, and re-layouts: 20.2 us -> 25.8 us
  starting transfers between devices: 12.5 us -> 16.4 us
    all_gather x1, waiting for transfers between devices: 77.4 us -> 33.7 us  [per_device(): lax.all_gather(pair, 'head', axis=0, tiled=False, axis_index_groups=lanes)]
    ppermute x0 -> x1, waiting for transfers between devices: none -> 30.2 us  [per_device(): lax.ppermute(local, 'head', [(src, (src + lane_count) % head_count) for s...]
    reduce_scatter x1, waiting for transfers between devices: 73.8 us -> 65.2 us  [per_device(): lax.psum_scatter(summed, 'seq', scatter_dimension=0, tiled=True, axis_ind...]
    ppermute x0 -> x1, starting transfers between devices: none -> 4.07 us  [per_device(): lax.ppermute(local, 'head', [(src, (src + lane_count) % head_count) for s...]
    select_n x0 -> x1, other arithmetic: none -> 3.31 us  [per_device(): jnp.where(upper == 0, jnp.stack([local, partner]), jnp.stack([partner, lo...]
  transfers between devices with their start and end apart: 8 -> 9, of which waited for: 4 -> 5; matrix products, arithmetic and copies ran while one was open for 14% -> 15% of each run, Pallas kernels for 9% -> 9%
where the time goes in v6:
time: 303 us; the launch traced here: 301 us
  waiting for transfers between devices  157 us (52%)
  other arithmetic  32.3 us (11%)
  Pallas kernels  27.8 us (9%)
  local copies, waits for them, and re-layouts  25.8 us (9%)
  matrix products  25.7 us (8%)
  starting transfers between devices  16.4 us (5%)
  between operations  15.1 us (5%)
    reduce_scatter x1, waiting for transfers between devices, per_device(): lax.psum_scatter(summed, 'seq', scatter_dimension=0, tiled=True, axis_ind...  65.2 us
    all_gather x1, waiting for transfers between devices, per_device(): lax.all_gather(pair, 'head', axis=0, tiled=False, axis_index_groups=lanes)  33.7 us
    ppermute x1, waiting for transfers between devices, per_device(): lax.ppermute(local, 'head', [(src, (src + lane_count) % head_count) for s...  30.2 us
    pallas_call x1, Pallas kernels, attention_backward(): pl.pallas_call(attention_kernel, out_shape=(jax.ShapeDtypeStruct(queries....  27.8 us
    all_to_all x1, waiting for transfers between devices, owned_block(): received = lax.all_to_all(send, 'seq', 0, 0, tiled=False)  27.3 us
    dot_general x1, matrix products, per_device(): lax.dot_general(gathered[:, :half], column_grads, (((0,), (0,)), ((), ())...  8.86 us
    ppermute x4, starting transfers between devices, shifted(): lax.ppermute(value, axis, [(source, source + steps) for source in range(i...  8.27 us
    dot_general x1, matrix products, per_device(): lax.dot_general(gathered[:, half:], column_grads, (((0,), (0,)), ((), ())...  8 us
  transfers between devices with their start and end apart: 9, of which 5 were waited for; matrix products, arithmetic and copies ran while one was open for 15% of the time, Pallas kernels for 9%

profile of v6, /device:TPU:0, one launch (start us, length us, event | category | flops | bytes accessed | tf_op | source)
XLA Modules:
  0.0 301.2 jit_solution(6589382775779589704)
XLA Ops:
  7.2 1.2 slice-done
  9.8 4.1 %collective-permute-start = (bf16[128,5376]{0,1:T(8,128)(2,1)S(1)}, bf16[128,5376]{0,1:T(8,128)(2,1)S(1)}, u32[]{:S(2)}, u32[]{:S(2)}) collective-permute-start(bf16[128,5376]{0,1:T(8,128)(2,1)S(1)} %bitcast.52), channel_id=1, source_target_pairs={{0,4},{1,5},{2,6},{3,7},{4,0},{5,1},{6,2},{7,3},{8,12},{9,13},{10,... | collective-permute-start | bytes 4128776 | tf_op jit(solution)/shard_map/ppermute | solution.py:194
  13.8 30.2 %collective-permute-done = bf16[128,5376]{0,1:T(8,128)(2,1)S(1)} collective-permute-done((bf16[128,5376]{0,1:T(8,128)(2,1)S(1)}, bf16[128,5376]{0,1:T(8,128)(2,1)S(1)}, u32[]{:S(2)}, u32[]{:S(2)}) %collective-permute-start) | collective-permute-done | bytes 1376288 | tf_op jit(solution)/shard_map/ppermute | solution.py:194
  44.0 1.1 copy-done.8
  45.1 3.3 %maximum_select_fusion = bf16[1,2,128,5376]{2,3,1,0:T(8,128)(2,1)S(1)} fusion(bf16[1,1,128,5376]{2,3,1,0:T(8,128)(2,1)} %bitcast.60, bf16[1,1,128,5376]{2,3,1,0:T(8,128)(2,1)} %bitcast.53, pred[]{:T(512)S(6)} %eq.33), kind=kLoop, calls=%fused_computation.10 | loop fusion | flops 4128768 | bytes 5505025 | tf_op jit(solution)/shard_map/jit(_where)/select_n | solution.py:198
  48.4 2.7 copy.38
  51.2 1.0 copy-done.10
  52.1 1.3 collective-permute-start.1
  53.5 4.2 %collective-permute-start.2 = (bf16[1024,256]{1,0:T(8,128)(2,1)S(1)}, bf16[1024,256]{1,0:T(8,128)(2,1)S(1)}, u32[]{:S(2)}, u32[]{:S(2)}) collective-permute-start(bf16[1024,256]{1,0:T(8,128)(2,1)S(1)} %copy-done.11), channel_id=1, source_target_pairs={{0,8},{8,16},{16,24},{24,32},{32,40},{40,48},{48,56},{56,64},{64,7... | collective-permute-start | bytes 1572872 | tf_op jit(solution)/shard_map/ppermute | solution.py:84
  57.7 1.0 copy.39.band_ref
  58.7 1.9 multiply_cosine_fusion
  60.6 1.4 pad_maximum_fusion.5
  62.0 1.1 pad_maximum_fusion.3.k_ref
  63.1 1.0 pad_maximum_fusion.4.v_ref
  64.1 27.8 %shard_map.90 = (f32[1024,512]{1,0:T(8,128)}, f32[2048,256]{1,0:T(8,128)}, f32[2048,256]{1,0:T(8,128)}) custom-call(s32[1024,1]{1,0:T(8,128)} %copy.39.band_ref, bf16[1024,512]{1,0:T(8,128)(2,1)} %q_ref.1, bf16[1024,512]{1,0:T(8,128)(2,1)} %do_ref.1, bf16[2048,256]{1,0:T(8,128)(2,1)} %pad_maximum_fusion.3.k_ref, bf16[2048,256]{1,0:T(8,128)(2,1)} %pad_maximum_fusion.4.v_ref), custom_call_target="tpu_custom_call" | custom-call | tf_op jit(solution)/shard_map/pallas_call | solution.py:69
  91.9 1.5 slice.60
  93.4 2.1 slice.82
  95.5 1.1 slice.55
  96.6 0.9 slice.83
  97.4 1.5 slice.61
  98.9 2.1 convert_element_type.45
  101.1 1.3 collective-permute-start.4
  102.4 1.8 slice.56
  104.1 2.0 convert_element_type.43
  106.1 1.5 collective-permute-start.3
  107.6 1.7 reshape.154
  109.3 2.3 broadcast_multiply_fusion
  111.6 1.2 slice_negate_fusion
  112.8 1.1 pad_maximum_fusion
  114.3 1.6 fusion.2
  115.9 1.7 add_convert_fusion.1
  118.0 1.8 fusion.8
  119.7 1.1 slice_negate_fusion.1
  120.9 2.7 fusion.3
  124.6 33.7 %all-gather.2.cloned.1.call-done = bf16[4,2,128,5376]{3,2,1,0:T(8,128)(2,1)} async-done(((bf16[1,2,128,5376]{3,2,1,0:T(8,128)(2,1)}), bf16[4,2,128,5376]{3,2,1,0:T(8,128)(2,1)}) %all-gather.2.cloned.1.call-update) | async-done | bytes 11010064 | tf_op jit(solution)/shard_map/all_gather | solution.py:200
  158.2 8.9 %convolution_convert_fusion = bf16[2688,1024]{1,0:T(8,128)(2,1)S(1)} fusion(bf16[1024,1024]{1,0:T(8,128)(2,1)S(1)} %bitcast.58, bf16[1024,5376]{1,0:T(8,128)(2,1)} %bitcast.63), kind=kOutput, calls=%fused_computation.6 | convolution fusion | flops 5639897088 | bytes 13107200 | tf_op jit(solution)/shard_map/dot_general | solution.py:208
  167.4 8.0 %convolution_convert_fusion.1 = bf16[2688,1024]{1,0:T(8,128)(2,1)S(1)} fusion(bf16[1024,1024]{1,0:T(8,128)(2,1)} %bitcast.59, bf16[1024,5376]{1,0:T(8,128)(2,1)S(1)} %bitcast.64), kind=kOutput, calls=%fused_computation.7 | convolution fusion | flops 5639897088 | bytes 13107200 | tf_op jit(solution)/shard_map/dot_general | solution.py:213
  175.4 1.0 collective-permute-done.5
  176.5 5.2 %add_convert_fusion = bf16[2688,1024]{1,0:T(8,128)(2,1)} fusion(bf16[2688,1024]{1,0:T(8,128)(2,1)S(1)} %collective-permute-done.5, bf16[2688,1024]{1,0:T(8,128)(2,1)S(1)} %convolution_convert_fusion.1), kind=kLoop, calls=%fused_computation.5 | loop fusion | flops 11010048 | bytes 16515072 | tf_op jit(solution)/shard_map/convert_element_type | solution.py:218
  181.7 1.3 fusion.11
  183.1 65.2 %reduce-scatter.2.cloned.1.call-done = bf16[336,1024]{1,0:T(8,128)(2,1)} async-done(((bf16[2688,1024]{1,0:T(8,128)(2,1)}), bf16[336,1024]{1,0:T(8,128)(2,1)}) %reduce-scatter.2.cloned.1.call-update) | async-done | bytes 688144 | tf_op jit(solution)/shard_map/reduce_scatter | solution.py:220
  248.4 1.2 concatenate.77
  250.2 1.6 broadcast_select_fusion
  251.8 3.7 %all-to-all-start = ((bf16[16,64,1024]{2,1,0:T(8,128)(2,1)}), bf16[16,64,1024]{2,1,0:T(8,128)(2,1)S(1)}, u32[]{:S(2)}, u32[]{:S(2)}) async-start(bf16[16,64,1024]{2,1,0:T(8,128)(2,1)} %broadcast_select_fusion), calls=%async_computation.1 | async-start | bytes 4194304 | tf_op jit(solution)/shard_map/all_to_all | solution.py:134
  256.2 27.3 %all-to-all-done = bf16[16,64,1024]{2,1,0:T(8,128)(2,1)S(1)} async-done(((bf16[16,64,1024]{2,1,0:T(8,128)(2,1)}), bf16[16,64,1024]{2,1,0:T(8,128)(2,1)S(1)}, u32[]{:S(2)}, u32[]{:S(2)}) %all-to-all-start) | async-done | bytes 2097184 | tf_op jit(solution)/shard_map/all_to_all | solution.py:134
  283.5 10.9 %conditional.1 = (f32[1,1,1024,1024]{3,2,1,0:T(8,128)}, f32[1,1,1024,1024]{3,2,1,0:T(8,128)}) conditional(s32[]{:T(128)} %convert_element_type.41, () %tuple.21, (pred[6]{0:T(512)(128)(4,1)S(1)}, s32[6]{0:T(128)S(1)}, bf16[16,64,1024]{2,1,0:T(8,128)(2,1)S(1)}) %tuple.23), branch_computations={%region_3.4_spmd, %region_4.6_spmd} | conditional | flops 4298113024 | bytes 18350140 | solution.py:248
  285.6 4.4 %multiply_bitcast_fusion.1 = f32[1,1,1024,1024]{3,2,1,0:T(8,128)} fusion(bf16[1024,1024]{1,0:T(8,128)(2,1)S(1)} %bitcast_select_fusion), kind=kOutput, calls=%fused_computation.2 | convolution fusion | flops 2148532224 | bytes 6291456 | tf_op jit(solution)/shard_map/cond/branch_1_fun/dot_general | solution.py:229
  290.0 4.4 %multiply_bitcast_fusion = f32[1,1,1024,1024]{3,2,1,0:T(8,128)} fusion(bf16[1024,1024]{1,0:T(8,128)(2,1)S(1)} %bitcast_select_fusion), kind=kOutput, calls=%fused_computation.1 | convolution fusion | flops 2148532224 | bytes 6291456 | tf_op jit(solution)/shard_map/cond/branch_1_fun/dot_general | solution.py:235
  (60 shorter events, 5.5 us)
Async XLA Ops:
  7.2 1.3 slice-start
  7.2 151.1 %all-gather.2.cloned.1.call-start = ((), (), s32[]{:S(2)}) async-start(), calls=%async_computation.2 | async-start | bytes 13762560 | tf_op jit(solution)/shard_map/all_gather | solution.py:200
  8.5 0.9 slice-start.1
  9.7 34.3 %copy-start.1 = (bf16[128,16,336]{0,2,1:T(8,128)(2,1)}, bf16[128,16,336]{0,2,1:T(8,128)(2,1)S(1)}, u32[]{:S(2)}) copy-start(bf16[128,16,336]{0,2,1:T(8,128)(2,1)S(1)} %pad_maximum_fusion.2) | copy-start | bytes 4128772
  9.8 34.2 %collective-permute-start = (bf16[128,5376]{0,1:T(8,128)(2,1)S(1)}, bf16[128,5376]{0,1:T(8,128)(2,1)S(1)}, u32[]{:S(2)}, u32[]{:S(2)}) collective-permute-start(bf16[128,5376]{0,1:T(8,128)(2,1)S(1)} %bitcast.52), channel_id=1, source_target_pairs={{0,4},{1,5},{2,6},{3,7},{4,0},{5,1},{6,2},{7,3},{8,12},{9,13},{10,... | collective-permute-start | bytes 4128776 | tf_op jit(solution)/shard_map/ppermute | solution.py:194
  44.0 1.1 copy-start.8
  51.1 1.0 copy-start.10
  51.1 2.4 copy-start.11
  51.1 6.6 %copy-start.12 = (s32[1024]{0:T(1024)S(1)}, s32[1024]{0:T(1024)}, u32[]{:S(2)}) copy-start(s32[1024]{0:T(1024)} %param.14) | copy-start | bytes 12292
  51.1 197.3 %reduce-scatter.2.cloned.1.call-start = ((), (), s32[]{:S(2)}) async-start(), calls=%async_computation.3 | async-start | bytes 6193152 | tf_op jit(solution)/shard_map/reduce_scatter | solution.py:220
  52.1 9.9 %collective-permute-start.1 = (bf16[1024,256]{1,0:T(8,128)(2,1)S(1)}, bf16[1024,256]{1,0:T(8,128)(2,1)S(1)}, u32[]{:S(2)}, u32[]{:S(2)}) collective-permute-start(bf16[1024,256]{1,0:T(8,128)(2,1)S(1)} %copy-done.10), channel_id=1, source_target_pairs={{0,8},{8,16},{16,24},{24,32},{32,40},{40,48},{48,56},{56,64},{64,7... | collective-permute-start | bytes 1572872 | tf_op jit(solution)/shard_map/ppermute | solution.py:84
  53.5 9.6 %collective-permute-start.2 = (bf16[1024,256]{1,0:T(8,128)(2,1)S(1)}, bf16[1024,256]{1,0:T(8,128)(2,1)S(1)}, u32[]{:S(2)}, u32[]{:S(2)}) collective-permute-start(bf16[1024,256]{1,0:T(8,128)(2,1)S(1)} %copy-done.11), channel_id=1, source_target_pairs={{0,8},{8,16},{16,24},{24,32},{32,40},{40,48},{48,56},{56,64},{64,7... | collective-permute-start | bytes 1572872 | tf_op jit(solution)/shard_map/ppermute | solution.py:84
  91.9 3.6 %copy-start.9 = (f32[2048,256]{1,0:T(8,128)S(1)}, f32[2048,256]{1,0:T(8,128)}, u32[]{:S(2)}) copy-start(f32[2048,256]{1,0:T(8,128)} %get-tuple-element.34) | copy-start | bytes 6291460
  98.9 8.7 %copy-start = (f32[1024,512]{1,0:T(8,128)S(1)}, f32[1024,512]{1,0:T(8,128)}, u32[]{:S(2)}) copy-start(f32[1024,512]{1,0:T(8,128)} %get-tuple-element.33) | copy-start | bytes 6291460
  101.1 14.9 %collective-permute-start.4 = (bf16[1024,2,128]{2,1,0:T(2,128)(2,1)}, bf16[1024,2,128]{2,1,0:T(2,128)(2,1)}, u32[]{:S(2)}, u32[]{:S(2)}) collective-permute-start(bf16[1024,2,128]{2,1,0:T(2,128)(2,1)} %convert_element_type.45), channel_id=1, source_target_pairs={{8,0},{16,8},{24,16},{32,24},{40,32},{48,40},{56,48},{64,56},{72,6... | collective-permute-start | bytes 1572872 | tf_op jit(solution)/shard_map/ppermute | solution.py:84
  106.1 11.8 %collective-permute-start.3 = (bf16[1024,2,128]{2,1,0:T(2,128)(2,1)}, bf16[1024,2,128]{2,1,0:T(2,128)(2,1)}, u32[]{:S(2)}, u32[]{:S(2)}) collective-permute-start(bf16[1024,2,128]{2,1,0:T(2,128)(2,1)} %convert_element_type.43), channel_id=1, source_target_pairs={{8,0},{16,8},{24,16},{32,24},{40,32},{48,40},{56,48},{64,56},{72,6... | collective-permute-start | bytes 1572872 | tf_op jit(solution)/shard_map/ppermute | solution.py:84
  112.8 1.2 copy-start.2
  114.3 1.6 copy-start.5
  115.9 2.0 copy-start.4
  119.7 1.2 copy-start.3
  120.9 3.1 %copy-start.6 = (bf16[1024,512]{1,0:T(8,128)(2,1)S(1)}, bf16[1024,512]{1,0:T(8,128)(2,1)}, u32[]{:S(2)}) copy-start(bf16[1024,512]{1,0:T(8,128)(2,1)} %fusion.2) | copy-start | bytes 3145732
  124.5 42.6 %copy-start.7 = (bf16[2,4,128,1024]{3,2,0,1:T(8,128)(2,1)}, bf16[2,4,128,1024]{3,2,0,1:T(8,128)(2,1)S(1)}, u32[]{:S(2)}) copy-start(bf16[2,4,128,1024]{3,2,0,1:T(8,128)(2,1)S(1)} %copy.43) | copy-start | bytes 6291460
  158.2 9.2 %copy-start.13 = (bf16[4,2,128,5376]{3,2,1,0:T(8,128)(2,1)S(1)}, bf16[4,2,128,5376]{3,2,1,0:T(8,128)(2,1)}, u32[]{:S(2)}) copy-start(bf16[4,2,128,5376]{3,2,1,0:T(8,128)(2,1)} %all-gather.2.cloned.1.call-done) | copy-start | bytes 33030148
  167.1 9.3 %collective-permute-start.5 = (bf16[2688,1024]{1,0:T(8,128)(2,1)S(1)}, bf16[2688,1024]{1,0:T(8,128)(2,1)S(1)}, u32[]{:S(2)}, u32[]{:S(2)}) collective-permute-start(bf16[2688,1024]{1,0:T(8,128)(2,1)S(1)} %convolution_convert_fusion), channel_id=1, source_target_pairs={{0,8},{8,0},{16,24},{24,16},{32,40},{40,32},{48,56},{56,48},{64,72... | collective-permute-start | bytes 16515080 | tf_op jit(solution)/shard_map/ppermute | solution.py:212
  251.8 31.7 %all-to-all-start = ((bf16[16,64,1024]{2,1,0:T(8,128)(2,1)}), bf16[16,64,1024]{2,1,0:T(8,128)(2,1)S(1)}, u32[]{:S(2)}, u32[]{:S(2)}) async-start(bf16[16,64,1024]{2,1,0:T(8,128)(2,1)} %broadcast_select_fusion), calls=%async_computation.1 | async-start | bytes 4194304 | tf_op jit(solution)/shard_map/all_to_all | solution.py:134
Sparse Core Ops, SparseCore 0:
  51.2 106.9 all-gather.1
  181.8 66.5 reduce-scatter.1

commit v7 on v6

--- a/solution.py
+++ b/solution.py
@@ -32,8 +32,8 @@
         col = lax.broadcasted_iota(jnp.int32, (QPK * QBLK, span), 1)
         row = lax.broadcasted_iota(jnp.int32, (QPK * QBLK, span), 0) % QBLK
         allowed = (col + q0 >= band) & (col <= row + WINDOW)
-        for g in range(KV_DEV):
-            base = g * QPK * HD
+        for g in range(1):
+            base = 0
             qs = jnp.concatenate(
                 [q_ref[pl.ds(q0, QBLK), base + r * HD:base + (r + 1) * HD] for r in range(QPK)], 0)
             dos = jnp.concatenate(
@@ -65,16 +65,19 @@
 
 def attention_backward(band_rel, queries, out_grad, key_all, value_all):
     tok_rows = queries.shape[0]
-    vmem = pl.BlockSpec(memory_space=pltpu.VMEM)
+    head_cols = pl.BlockSpec((tok_rows, QPK * HD), lambda g: (0, g))
+    kv_cols = pl.BlockSpec((2 * tok_rows, HD), lambda g: (0, g))
+    band_spec = pl.BlockSpec((tok_rows, 1), lambda g: (0, 0))
     return pl.pallas_call(
         attention_kernel,
+        grid=(KV_DEV,),
         out_shape=(
             jax.ShapeDtypeStruct(queries.shape, jnp.float32),
             jax.ShapeDtypeStruct(key_all.shape, jnp.float32),
             jax.ShapeDtypeStruct(value_all.shape, jnp.float32),
         ),
-        in_specs=[vmem] * 5,
-        out_specs=(vmem, vmem, vmem),
+        in_specs=[band_spec, head_cols, head_cols, kv_cols, kv_cols],
+        out_specs=(head_cols, kv_cols, kv_cols),
     )(band_rel.reshape(tok_rows, 1), queries, out_grad, key_all, value_all)
 
 

time: 303 us -> 303 us (level)
  no operation moved by 1% of the time
where the time goes in v7:
time: 303 us; the launch traced here: 301 us
  waiting for transfers between devices  158 us (52%)
  other arithmetic  32.3 us (11%)
  Pallas kernels  27.4 us (9%)
  local copies, waits for them, and re-layouts  25.8 us (9%)
  matrix products  25.7 us (8%)
  starting transfers between devices  16.4 us (5%)
  between operations  15.1 us (5%)
    reduce_scatter x1, waiting for transfers between devices, per_device(): lax.psum_scatter(summed, 'seq', scatter_dimension=0, tiled=True, axis_ind...  65.2 us
    all_gather x1, waiting for transfers between devices, per_device(): lax.all_gather(pair, 'head', axis=0, tiled=False, axis_index_groups=lanes)  34.1 us
    ppermute x1, waiting for transfers between devices, per_device(): lax.ppermute(local, 'head', [(src, (src + lane_count) % head_count) for s...  30.2 us
    pallas_call x1, Pallas kernels, attention_backward(): pl.pallas_call(attention_kernel, grid=(KV_DEV,), out_shape=(jax.ShapeDtyp...  27.4 us
    all_to_all x1, waiting for transfers between devices, owned_block(): received = lax.all_to_all(send, 'seq', 0, 0, tiled=False)  27.3 us
    dot_general x1, matrix products, per_device(): lax.dot_general(gathered[:, :half], column_grads, (((0,), (0,)), ((), ())...  8.86 us
    ppermute x4, starting transfers between devices, shifted(): lax.ppermute(value, axis, [(source, source + steps) for source in range(i...  8.27 us
    dot_general x1, matrix products, per_device(): lax.dot_general(gathered[:, half:], column_grads, (((0,), (0,)), ((), ())...  8 us
  transfers between devices with their start and end apart: 9, of which 5 were waited for; matrix products, arithmetic and copies ran while one was open for 15% of the time, Pallas kernels for 9%

profile of v7, /device:TPU:0, one launch (start us, length us, event | category | flops | bytes accessed | tf_op | source)
XLA Modules:
  0.0 301.2 jit_solution(10514638294254155356)
XLA Ops:
  7.2 1.2 slice-done
  9.8 4.1 %collective-permute-start = (bf16[128,5376]{0,1:T(8,128)(2,1)S(1)}, bf16[128,5376]{0,1:T(8,128)(2,1)S(1)}, u32[]{:S(2)}, u32[]{:S(2)}) collective-permute-start(bf16[128,5376]{0,1:T(8,128)(2,1)S(1)} %bitcast.52), channel_id=1, source_target_pairs={{0,4},{1,5},{2,6},{3,7},{4,0},{5,1},{6,2},{7,3},{8,12},{9,13},{10,... | collective-permute-start | bytes 4128776 | tf_op jit(solution)/shard_map/ppermute | solution.py:197
  13.8 30.2 %collective-permute-done = bf16[128,5376]{0,1:T(8,128)(2,1)S(1)} collective-permute-done((bf16[128,5376]{0,1:T(8,128)(2,1)S(1)}, bf16[128,5376]{0,1:T(8,128)(2,1)S(1)}, u32[]{:S(2)}, u32[]{:S(2)}) %collective-permute-start) | collective-permute-done | bytes 1376288 | tf_op jit(solution)/shard_map/ppermute | solution.py:197
  44.0 1.1 copy-done.8
  45.1 3.3 %maximum_select_fusion = bf16[1,2,128,5376]{2,3,1,0:T(8,128)(2,1)S(1)} fusion(bf16[1,1,128,5376]{2,3,1,0:T(8,128)(2,1)} %bitcast.60, bf16[1,1,128,5376]{2,3,1,0:T(8,128)(2,1)} %bitcast.53, pred[]{:T(512)S(6)} %eq.33), kind=kLoop, calls=%fused_computation.10 | loop fusion | flops 4128768 | bytes 5505025 | tf_op jit(solution)/shard_map/jit(_where)/select_n | solution.py:201
  48.4 2.7 copy.38
  51.2 1.0 copy-done.10
  52.1 1.3 collective-permute-start.1
  53.5 4.2 %collective-permute-start.2 = (bf16[1024,256]{1,0:T(8,128)(2,1)S(1)}, bf16[1024,256]{1,0:T(8,128)(2,1)S(1)}, u32[]{:S(2)}, u32[]{:S(2)}) collective-permute-start(bf16[1024,256]{1,0:T(8,128)(2,1)S(1)} %copy-done.11), channel_id=1, source_target_pairs={{0,8},{8,16},{16,24},{24,32},{32,40},{40,48},{48,56},{56,64},{64,7... | collective-permute-start | bytes 1572872 | tf_op jit(solution)/shard_map/ppermute | solution.py:87
  57.7 1.0 copy.39.band_ref
  58.7 1.9 multiply_cosine_fusion
  60.6 1.4 pad_maximum_fusion.5
  62.0 1.1 pad_maximum_fusion.3.k_ref
  63.1 1.0 pad_maximum_fusion.4.v_ref
  64.1 27.4 %shard_map.90 = (f32[1024,512]{1,0:T(8,128)}, f32[2048,256]{1,0:T(8,128)}, f32[2048,256]{1,0:T(8,128)}) custom-call(s32[1024,1]{1,0:T(8,128)} %copy.39.band_ref, bf16[1024,512]{1,0:T(8,128)(2,1)} %q_ref.1, bf16[1024,512]{1,0:T(8,128)(2,1)} %do_ref.1, bf16[2048,256]{1,0:T(8,128)(2,1)} %pad_maximum_fusion.3.k_ref, bf16[2048,256]{1,0:T(8,128)(2,1)} %pad_maximum_fusion.4.v_ref), custom_call_target="tpu_custom_call" | custom-call | tf_op jit(solution)/shard_map/pallas_call | solution.py:71
  91.5 1.4 slice.60
  93.0 2.1 slice.82
  95.0 1.1 slice.55
  96.2 0.9 slice.83
  97.0 1.5 slice.61
  98.5 2.1 convert_element_type.45
  100.7 1.3 collective-permute-start.4
  101.9 1.8 slice.56
  103.7 2.0 convert_element_type.43
  105.7 1.5 collective-permute-start.3
  107.2 1.7 reshape.154
  108.9 2.3 broadcast_multiply_fusion
  111.2 1.2 slice_negate_fusion
  112.4 1.1 pad_maximum_fusion
  113.9 1.6 fusion.2
  115.5 1.7 add_convert_fusion.1
  117.5 1.8 fusion.8
  119.3 1.1 slice_negate_fusion.1
  120.5 2.7 fusion.3
  124.1 34.1 %all-gather.2.cloned.1.call-done = bf16[4,2,128,5376]{3,2,1,0:T(8,128)(2,1)} async-done(((bf16[1,2,128,5376]{3,2,1,0:T(8,128)(2,1)}), bf16[4,2,128,5376]{3,2,1,0:T(8,128)(2,1)}) %all-gather.2.cloned.1.call-update) | async-done | bytes 11010064 | tf_op jit(solution)/shard_map/all_gather | solution.py:203
  158.2 8.9 %convolution_convert_fusion = bf16[2688,1024]{1,0:T(8,128)(2,1)S(1)} fusion(bf16[1024,1024]{1,0:T(8,128)(2,1)S(1)} %bitcast.58, bf16[1024,5376]{1,0:T(8,128)(2,1)} %bitcast.63), kind=kOutput, calls=%fused_computation.6 | convolution fusion | flops 5639897088 | bytes 13107200 | tf_op jit(solution)/shard_map/dot_general | solution.py:211
  167.4 8.0 %convolution_convert_fusion.1 = bf16[2688,1024]{1,0:T(8,128)(2,1)S(1)} fusion(bf16[1024,1024]{1,0:T(8,128)(2,1)} %bitcast.59, bf16[1024,5376]{1,0:T(8,128)(2,1)S(1)} %bitcast.64), kind=kOutput, calls=%fused_computation.7 | convolution fusion | flops 5639897088 | bytes 13107200 | tf_op jit(solution)/shard_map/dot_general | solution.py:216
  175.4 1.0 collective-permute-done.5
  176.5 5.2 %add_convert_fusion = bf16[2688,1024]{1,0:T(8,128)(2,1)} fusion(bf16[2688,1024]{1,0:T(8,128)(2,1)S(1)} %collective-permute-done.5, bf16[2688,1024]{1,0:T(8,128)(2,1)S(1)} %convolution_convert_fusion.1), kind=kLoop, calls=%fused_computation.5 | loop fusion | flops 11010048 | bytes 16515072 | tf_op jit(solution)/shard_map/convert_element_type | solution.py:221
  181.7 1.3 fusion.11
  183.1 65.2 %reduce-scatter.2.cloned.1.call-done = bf16[336,1024]{1,0:T(8,128)(2,1)} async-done(((bf16[2688,1024]{1,0:T(8,128)(2,1)}), bf16[336,1024]{1,0:T(8,128)(2,1)}) %reduce-scatter.2.cloned.1.call-update) | async-done | bytes 688144 | tf_op jit(solution)/shard_map/reduce_scatter | solution.py:223
  248.4 1.2 concatenate.77
  250.2 1.6 broadcast_select_fusion
  251.8 3.7 %all-to-all-start = ((bf16[16,64,1024]{2,1,0:T(8,128)(2,1)}), bf16[16,64,1024]{2,1,0:T(8,128)(2,1)S(1)}, u32[]{:S(2)}, u32[]{:S(2)}) async-start(bf16[16,64,1024]{2,1,0:T(8,128)(2,1)} %broadcast_select_fusion), calls=%async_computation.1 | async-start | bytes 4194304 | tf_op jit(solution)/shard_map/all_to_all | solution.py:137
  256.2 27.3 %all-to-all-done = bf16[16,64,1024]{2,1,0:T(8,128)(2,1)S(1)} async-done(((bf16[16,64,1024]{2,1,0:T(8,128)(2,1)}), bf16[16,64,1024]{2,1,0:T(8,128)(2,1)S(1)}, u32[]{:S(2)}, u32[]{:S(2)}) %all-to-all-start) | async-done | bytes 2097184 | tf_op jit(solution)/shard_map/all_to_all | solution.py:137
  283.5 10.9 %conditional.1 = (f32[1,1,1024,1024]{3,2,1,0:T(8,128)}, f32[1,1,1024,1024]{3,2,1,0:T(8,128)}) conditional(s32[]{:T(128)} %convert_element_type.41, () %tuple.21, (pred[6]{0:T(512)(128)(4,1)S(1)}, s32[6]{0:T(128)S(1)}, bf16[16,64,1024]{2,1,0:T(8,128)(2,1)S(1)}) %tuple.23), branch_computations={%region_3.4_spmd, %region_4.6_spmd} | conditional | flops 4298113024 | bytes 18350140 | solution.py:251
  285.6 4.4 %multiply_bitcast_fusion.1 = f32[1,1,1024,1024]{3,2,1,0:T(8,128)} fusion(bf16[1024,1024]{1,0:T(8,128)(2,1)S(1)} %bitcast_select_fusion), kind=kOutput, calls=%fused_computation.2 | convolution fusion | flops 2148532224 | bytes 6291456 | tf_op jit(solution)/shard_map/cond/branch_1_fun/dot_general | solution.py:232
  290.0 4.4 %multiply_bitcast_fusion = f32[1,1,1024,1024]{3,2,1,0:T(8,128)} fusion(bf16[1024,1024]{1,0:T(8,128)(2,1)S(1)} %bitcast_select_fusion), kind=kOutput, calls=%fused_computation.1 | convolution fusion | flops 2148532224 | bytes 6291456 | tf_op jit(solution)/shard_map/cond/branch_1_fun/dot_general | solution.py:238
  (60 shorter events, 5.5 us)
Async XLA Ops:
  7.2 1.3 slice-start
  7.2 151.1 %all-gather.2.cloned.1.call-start = ((), (), s32[]{:S(2)}) async-start(), calls=%async_computation.2 | async-start | bytes 13762560 | tf_op jit(solution)/shard_map/all_gather | solution.py:203
  8.5 0.9 slice-start.1
  9.7 34.3 %copy-start.1 = (bf16[128,16,336]{0,2,1:T(8,128)(2,1)}, bf16[128,16,336]{0,2,1:T(8,128)(2,1)S(1)}, u32[]{:S(2)}) copy-start(bf16[128,16,336]{0,2,1:T(8,128)(2,1)S(1)} %pad_maximum_fusion.2) | copy-start | bytes 4128772
  9.8 34.2 %collective-permute-start = (bf16[128,5376]{0,1:T(8,128)(2,1)S(1)}, bf16[128,5376]{0,1:T(8,128)(2,1)S(1)}, u32[]{:S(2)}, u32[]{:S(2)}) collective-permute-start(bf16[128,5376]{0,1:T(8,128)(2,1)S(1)} %bitcast.52), channel_id=1, source_target_pairs={{0,4},{1,5},{2,6},{3,7},{4,0},{5,1},{6,2},{7,3},{8,12},{9,13},{10,... | collective-permute-start | bytes 4128776 | tf_op jit(solution)/shard_map/ppermute | solution.py:197
  44.0 1.1 copy-start.8
  51.1 1.0 copy-start.10
  51.1 2.4 copy-start.11
  51.1 6.6 %copy-start.12 = (s32[1024]{0:T(1024)S(1)}, s32[1024]{0:T(1024)}, u32[]{:S(2)}) copy-start(s32[1024]{0:T(1024)} %param.14) | copy-start | bytes 12292
  51.1 197.3 %reduce-scatter.2.cloned.1.call-start = ((), (), s32[]{:S(2)}) async-start(), calls=%async_computation.3 | async-start | bytes 6193152 | tf_op jit(solution)/shard_map/reduce_scatter | solution.py:223
  52.1 9.9 %collective-permute-start.1 = (bf16[1024,256]{1,0:T(8,128)(2,1)S(1)}, bf16[1024,256]{1,0:T(8,128)(2,1)S(1)}, u32[]{:S(2)}, u32[]{:S(2)}) collective-permute-start(bf16[1024,256]{1,0:T(8,128)(2,1)S(1)} %copy-done.10), channel_id=1, source_target_pairs={{0,8},{8,16},{16,24},{24,32},{32,40},{40,48},{48,56},{56,64},{64,7... | collective-permute-start | bytes 1572872 | tf_op jit(solution)/shard_map/ppermute | solution.py:87
  53.5 9.6 %collective-permute-start.2 = (bf16[1024,256]{1,0:T(8,128)(2,1)S(1)}, bf16[1024,256]{1,0:T(8,128)(2,1)S(1)}, u32[]{:S(2)}, u32[]{:S(2)}) collective-permute-start(bf16[1024,256]{1,0:T(8,128)(2,1)S(1)} %copy-done.11), channel_id=1, source_target_pairs={{0,8},{8,16},{16,24},{24,32},{32,40},{40,48},{48,56},{56,64},{64,7... | collective-permute-start | bytes 1572872 | tf_op jit(solution)/shard_map/ppermute | solution.py:87
  91.5 3.5 %copy-start.9 = (f32[2048,256]{1,0:T(8,128)S(1)}, f32[2048,256]{1,0:T(8,128)}, u32[]{:S(2)}) copy-start(f32[2048,256]{1,0:T(8,128)} %get-tuple-element.34) | copy-start | bytes 6291460
  98.5 8.7 %copy-start = (f32[1024,512]{1,0:T(8,128)S(1)}, f32[1024,512]{1,0:T(8,128)}, u32[]{:S(2)}) copy-start(f32[1024,512]{1,0:T(8,128)} %get-tuple-element.33) | copy-start | bytes 6291460
  100.7 14.9 %collective-permute-start.4 = (bf16[1024,2,128]{2,1,0:T(2,128)(2,1)}, bf16[1024,2,128]{2,1,0:T(2,128)(2,1)}, u32[]{:S(2)}, u32[]{:S(2)}) collective-permute-start(bf16[1024,2,128]{2,1,0:T(2,128)(2,1)} %convert_element_type.45), channel_id=1, source_target_pairs={{8,0},{16,8},{24,16},{32,24},{40,32},{48,40},{56,48},{64,56},{72,6... | collective-permute-start | bytes 1572872 | tf_op jit(solution)/shard_map/ppermute | solution.py:87
  105.7 11.8 %collective-permute-start.3 = (bf16[1024,2,128]{2,1,0:T(2,128)(2,1)}, bf16[1024,2,128]{2,1,0:T(2,128)(2,1)}, u32[]{:S(2)}, u32[]{:S(2)}) collective-permute-start(bf16[1024,2,128]{2,1,0:T(2,128)(2,1)} %convert_element_type.43), channel_id=1, source_target_pairs={{8,0},{16,8},{24,16},{32,24},{40,32},{48,40},{56,48},{64,56},{72,6... | collective-permute-start | bytes 1572872 | tf_op jit(solution)/shard_map/ppermute | solution.py:87
  112.4 1.2 copy-start.2
  113.9 1.6 copy-start.5
  115.5 2.0 copy-start.4
  119.3 1.2 copy-start.3
  120.5 3.1 %copy-start.6 = (bf16[1024,512]{1,0:T(8,128)(2,1)S(1)}, bf16[1024,512]{1,0:T(8,128)(2,1)}, u32[]{:S(2)}) copy-start(bf16[1024,512]{1,0:T(8,128)(2,1)} %fusion.2) | copy-start | bytes 3145732
  124.1 43.0 %copy-start.7 = (bf16[2,4,128,1024]{3,2,0,1:T(8,128)(2,1)}, bf16[2,4,128,1024]{3,2,0,1:T(8,128)(2,1)S(1)}, u32[]{:S(2)}) copy-start(bf16[2,4,128,1024]{3,2,0,1:T(8,128)(2,1)S(1)} %copy.43) | copy-start | bytes 6291460
  158.2 9.2 %copy-start.13 = (bf16[4,2,128,5376]{3,2,1,0:T(8,128)(2,1)S(1)}, bf16[4,2,128,5376]{3,2,1,0:T(8,128)(2,1)}, u32[]{:S(2)}) copy-start(bf16[4,2,128,5376]{3,2,1,0:T(8,128)(2,1)} %all-gather.2.cloned.1.call-done) | copy-start | bytes 33030148
  167.1 9.3 %collective-permute-start.5 = (bf16[2688,1024]{1,0:T(8,128)(2,1)S(1)}, bf16[2688,1024]{1,0:T(8,128)(2,1)S(1)}, u32[]{:S(2)}, u32[]{:S(2)}) collective-permute-start(bf16[2688,1024]{1,0:T(8,128)(2,1)S(1)} %convolution_convert_fusion), channel_id=1, source_target_pairs={{0,8},{8,0},{16,24},{24,16},{32,40},{40,32},{48,56},{56,48},{64,72... | collective-permute-start | bytes 16515080 | tf_op jit(solution)/shard_map/ppermute | solution.py:215
  251.8 31.7 %all-to-all-start = ((bf16[16,64,1024]{2,1,0:T(8,128)(2,1)}), bf16[16,64,1024]{2,1,0:T(8,128)(2,1)S(1)}, u32[]{:S(2)}, u32[]{:S(2)}) async-start(bf16[16,64,1024]{2,1,0:T(8,128)(2,1)} %broadcast_select_fusion), calls=%async_computation.1 | async-start | bytes 4194304 | tf_op jit(solution)/shard_map/all_to_all | solution.py:137
Sparse Core Ops, SparseCore 0:
  51.2 106.9 all-gather.1
  181.8 66.5 reduce-scatter.1

commit v8 on v7

--- a/solution.py
+++ b/solution.py
@@ -194,9 +194,23 @@
     ).reshape(inputs.shape[0], D)
     head_count = lax.axis_size("head")
     lane_count = head_count // 2
-    partner = lax.ppermute(
-        local, "head", [(src, (src + lane_count) % head_count) for src in range(head_count)]
-    )
+    split = D // 2
+    direct = lax.ppermute(
+        local[:, :split], "head",
+        [(src, (src + lane_count) % head_count) for src in range(head_count)],
+    )
+    relay_pairs = []
+    for seq_at in range(seq_count):
+        for head_at in range(head_count):
+            z_here = (head_at // lane_count) * 2 + seq_at // (seq_count // 2)
+            z_next = (z_here - 1) % 4
+            seq_next = (z_next % 2) * (seq_count // 2) + seq_at % (seq_count // 2)
+            head_next = (z_next // 2) * lane_count + head_at % lane_count
+            relay_pairs.append((seq_at * head_count + head_at, seq_next * head_count + head_next))
+    relayed = local[:, split:]
+    for hop in range(2):
+        relayed = lax.ppermute(relayed, ("seq", "head"), relay_pairs)
+    partner = jnp.concatenate([direct, relayed], 1)
     upper = group_index // lane_count
     pair = jnp.where(upper == 0, jnp.stack([local, partner]), jnp.stack([partner, local]))
     lanes = [list(range(start, start + lane_count)) for start in (0, lane_count)]

time: 303 us -> 320 us (1.056)
  waiting for transfers between devices: 158 us -> 171 us
  starting transfers between devices: 16.4 us -> 20.4 us
    ppermute x1 -> x3, waiting for transfers between devices: 30.2 us -> 43.6 us  [the longest x2 43.6 us: per_device(): relayed = lax.ppermute(relayed, ('seq', 'head'), relay_pairs)]
    ppermute x1 -> x3, starting transfers between devices: 4.07 us -> 8.02 us  [the longest x2 8.01 us: per_device(): relayed = lax.ppermute(relayed, ('seq', 'head'), relay_pairs)]
  transfers between devices with their start and end apart: 9 -> 11, of which waited for: 5 -> 6; matrix products, arithmetic and copies ran while one was open for 15% -> 14% of each run, Pallas kernels for 9% -> 9%
where the time goes in v8:
time: 320 us; the launch traced here: 318 us
  waiting for transfers between devices  171 us (53%)
  other arithmetic  30.9 us (10%)
  Pallas kernels  27.4 us (9%)
  local copies, waits for them, and re-layouts  26.6 us (8%)
  matrix products  25.7 us (8%)
  starting transfers between devices  20.4 us (6%)
  between operations  15.1 us (5%)
    reduce_scatter x1, waiting for transfers between devices, per_device(): lax.psum_scatter(summed, 'seq', scatter_dimension=0, tiled=True, axis_ind...  65.2 us
    ppermute x2, waiting for transfers between devices, per_device(): relayed = lax.ppermute(relayed, ('seq', 'head'), relay_pairs)  43.6 us
    all_gather x1, waiting for transfers between devices, per_device(): lax.all_gather(pair, 'head', axis=0, tiled=False, axis_index_groups=lanes)  34.2 us
    pallas_call x1, Pallas kernels, attention_backward(): pl.pallas_call(attention_kernel, grid=(KV_DEV,), out_shape=(jax.ShapeDtyp...  27.4 us
    all_to_all x1, waiting for transfers between devices, owned_block(): received = lax.all_to_all(send, 'seq', 0, 0, tiled=False)  27.3 us
    dot_general x1, matrix products, per_device(): lax.dot_general(gathered[:, :half], column_grads, (((0,), (0,)), ((), ())...  8.87 us
    ppermute x4, starting transfers between devices, shifted(): lax.ppermute(value, axis, [(source, source + steps) for source in range(i...  8.27 us
    ppermute x2, starting transfers between devices, per_device(): relayed = lax.ppermute(relayed, ('seq', 'head'), relay_pairs)  8.01 us
  transfers between devices with their start and end apart: 11, of which 6 were waited for; matrix products, arithmetic and copies ran while one was open for 14% of the time, Pallas kernels for 9%

profile of v8, /device:TPU:0, one launch (start us, length us, event | category | flops | bytes accessed | tf_op | source)
XLA Modules:
  0.0 318.1 jit_solution(17995032668125189493)
XLA Ops:
  7.2 1.2 slice-done
  9.8 4.2 %collective-permute-start.1 = (bf16[128,2688]{0,1:T(8,128)(2,1)S(1)}, bf16[128,2688]{0,1:T(8,128)(2,1)}, u32[]{:S(2)}, u32[]{:S(2)}) collective-permute-start(bf16[128,2688]{0,1:T(8,128)(2,1)S(1)} %get-tuple-element.46), channel_id=1, source_target_pairs={{0,68},{1,69},{2,70},{3,71},{4,64},{5,65},{6,66},{7,67},{8,76},{9,... | collective-permute-start | bytes 2064392 | tf_op jit(solution)/shard_map/ppermute | solution.py:212
  14.1 29.4 %collective-permute-done.1 = bf16[128,2688]{0,1:T(8,128)(2,1)} collective-permute-done((bf16[128,2688]{0,1:T(8,128)(2,1)S(1)}, bf16[128,2688]{0,1:T(8,128)(2,1)}, u32[]{:S(2)}, u32[]{:S(2)}) %collective-permute-start.1) | collective-permute-done | bytes 688160 | tf_op jit(solution)/shard_map/ppermute | solution.py:212
  43.5 3.8 %collective-permute-start.2 = (bf16[128,2688]{0,1:T(8,128)(2,1)}, bf16[128,2688]{0,1:T(8,128)(2,1)S(1)}, u32[]{:S(2)}, u32[]{:S(2)}) collective-permute-start(bf16[128,2688]{0,1:T(8,128)(2,1)} %collective-permute-done.1), channel_id=1, source_target_pairs={{0,68},{1,69},{2,70},{3,71},{4,64},{5,65},{6,66},{7,67},{8,76},{9,... | collective-permute-start | bytes 2064392 | tf_op jit(solution)/shard_map/ppermute | solution.py:212
  47.3 14.1 %collective-permute-done.2 = bf16[128,2688]{0,1:T(8,128)(2,1)S(1)} collective-permute-done((bf16[128,2688]{0,1:T(8,128)(2,1)}, bf16[128,2688]{0,1:T(8,128)(2,1)S(1)}, u32[]{:S(2)}, u32[]{:S(2)}) %collective-permute-start.2) | collective-permute-done | bytes 688160 | tf_op jit(solution)/shard_map/ppermute | solution.py:212
  61.5 1.8 maximum_select_fusion
  63.3 4.5 %copy.38 = bf16[1,2,128,5376]{3,2,1,0:T(8,128)(2,1)} copy(bf16[1,2,128,5376]{2,3,1,0:T(8,128)(2,1)} %maximum_select_fusion) | data formatting | bytes 5505024 | tf_op jit(solution)/shard_map/jit(_where)/select_n | solution.py:215
  67.9 1.0 copy-done.8
  68.8 1.3 collective-permute-start.3
  70.2 4.2 %collective-permute-start.4 = (bf16[1024,256]{1,0:T(8,128)(2,1)S(1)}, bf16[1024,256]{1,0:T(8,128)(2,1)S(1)}, u32[]{:S(2)}, u32[]{:S(2)}) collective-permute-start(bf16[1024,256]{1,0:T(8,128)(2,1)S(1)} %copy-done.9), channel_id=1, source_target_pairs={{0,8},{8,16},{16,24},{24,32},{32,40},{40,48},{48,56},{56,64},{64,7... | collective-permute-start | bytes 1572872 | tf_op jit(solution)/shard_map/ppermute | solution.py:87
  74.4 1.0 copy.39.band_ref
  75.4 1.9 multiply_cosine_fusion
  77.3 1.4 pad_maximum_fusion.5
  78.7 1.1 pad_maximum_fusion.3.k_ref
  79.8 1.1 pad_maximum_fusion.4.v_ref
  80.9 27.4 %shard_map.90 = (f32[1024,512]{1,0:T(8,128)}, f32[2048,256]{1,0:T(8,128)}, f32[2048,256]{1,0:T(8,128)}) custom-call(s32[1024,1]{1,0:T(8,128)} %copy.39.band_ref, bf16[1024,512]{1,0:T(8,128)(2,1)} %q_ref.1, bf16[1024,512]{1,0:T(8,128)(2,1)} %do_ref.1, bf16[2048,256]{1,0:T(8,128)(2,1)} %pad_maximum_fusion.3.k_ref, bf16[2048,256]{1,0:T(8,128)(2,1)} %pad_maximum_fusion.4.v_ref), custom_call_target="tpu_custom_call" | custom-call | tf_op jit(solution)/shard_map/pallas_call | solution.py:71
  108.3 1.4 slice.68
  109.7 2.1 slice.92
  111.8 1.1 slice.63
  113.8 1.5 slice.69
  115.3 2.1 convert_element_type.45
  117.4 1.3 collective-permute-start.6
  118.7 1.8 slice.64
  120.5 2.0 convert_element_type.43
  122.5 1.5 collective-permute-start.5
  123.9 1.7 reshape.154
  125.7 2.3 broadcast_multiply_fusion
  127.9 1.2 slice_negate_fusion
  129.2 1.1 pad_maximum_fusion
  130.7 1.6 fusion.2
  132.3 1.7 add_convert_fusion.1
  134.3 1.8 fusion.8
  136.1 1.1 slice_negate_fusion.1
  137.3 2.7 fusion.3
  140.9 34.2 %all-gather.2.cloned.1.call-done = bf16[4,2,128,5376]{3,2,1,0:T(8,128)(2,1)} async-done(((bf16[1,2,128,5376]{3,2,1,0:T(8,128)(2,1)}), bf16[4,2,128,5376]{3,2,1,0:T(8,128)(2,1)}) %all-gather.2.cloned.1.call-update) | async-done | bytes 11010064 | tf_op jit(solution)/shard_map/all_gather | solution.py:217
  175.1 8.9 %convolution_convert_fusion = bf16[2688,1024]{1,0:T(8,128)(2,1)S(1)} fusion(bf16[1024,1024]{1,0:T(8,128)(2,1)S(1)} %bitcast.59, bf16[1024,5376]{1,0:T(8,128)(2,1)} %bitcast.63), kind=kOutput, calls=%fused_computation.6 | convolution fusion | flops 5639897088 | bytes 13107200 | tf_op jit(solution)/shard_map/dot_general | solution.py:225
  184.3 8.0 %convolution_convert_fusion.1 = bf16[2688,1024]{1,0:T(8,128)(2,1)S(1)} fusion(bf16[1024,1024]{1,0:T(8,128)(2,1)} %bitcast.60, bf16[1024,5376]{1,0:T(8,128)(2,1)S(1)} %bitcast.64), kind=kOutput, calls=%fused_computation.7 | convolution fusion | flops 5639897088 | bytes 13107200 | tf_op jit(solution)/shard_map/dot_general | solution.py:230
  192.3 1.0 collective-permute-done.7
  193.4 5.2 %add_convert_fusion = bf16[2688,1024]{1,0:T(8,128)(2,1)} fusion(bf16[2688,1024]{1,0:T(8,128)(2,1)S(1)} %collective-permute-done.7, bf16[2688,1024]{1,0:T(8,128)(2,1)S(1)} %convolution_convert_fusion.1), kind=kLoop, calls=%fused_computation.5 | loop fusion | flops 11010048 | bytes 16515072 | tf_op jit(solution)/shard_map/convert_element_type | solution.py:235
  198.6 1.3 fusion.11
  200.0 65.2 %reduce-scatter.2.cloned.1.call-done = bf16[336,1024]{1,0:T(8,128)(2,1)} async-done(((bf16[2688,1024]{1,0:T(8,128)(2,1)}), bf16[336,1024]{1,0:T(8,128)(2,1)}) %reduce-scatter.2.cloned.1.call-update) | async-done | bytes 688144 | tf_op jit(solution)/shard_map/reduce_scatter | solution.py:237
  265.3 1.2 concatenate.81
  267.1 1.6 broadcast_select_fusion
  268.7 3.7 %all-to-all-start = ((bf16[16,64,1024]{2,1,0:T(8,128)(2,1)}), bf16[16,64,1024]{2,1,0:T(8,128)(2,1)S(1)}, u32[]{:S(2)}, u32[]{:S(2)}) async-start(bf16[16,64,1024]{2,1,0:T(8,128)(2,1)} %broadcast_select_fusion), calls=%async_computation.1 | async-start | bytes 4194304 | tf_op jit(solution)/shard_map/all_to_all | solution.py:137
  273.1 27.3 %all-to-all-done = bf16[16,64,1024]{2,1,0:T(8,128)(2,1)S(1)} async-done(((bf16[16,64,1024]{2,1,0:T(8,128)(2,1)}), bf16[16,64,1024]{2,1,0:T(8,128)(2,1)S(1)}, u32[]{:S(2)}, u32[]{:S(2)}) %all-to-all-start) | async-done | bytes 2097184 | tf_op jit(solution)/shard_map/all_to_all | solution.py:137
  300.4 10.9 %conditional.1 = (f32[1,1,1024,1024]{3,2,1,0:T(8,128)}, f32[1,1,1024,1024]{3,2,1,0:T(8,128)}) conditional(s32[]{:T(128)} %convert_element_type.41, () %tuple.21, (pred[6]{0:T(512)(128)(4,1)S(1)}, s32[6]{0:T(128)S(1)}, bf16[16,64,1024]{2,1,0:T(8,128)(2,1)S(1)}) %tuple.23), branch_computations={%region_3.4_spmd, %region_4.6_spmd} | conditional | flops 4298113024 | bytes 18350140 | solution.py:265
  302.5 4.4 %multiply_bitcast_fusion.1 = f32[1,1,1024,1024]{3,2,1,0:T(8,128)} fusion(bf16[1024,1024]{1,0:T(8,128)(2,1)S(1)} %bitcast_select_fusion), kind=kOutput, calls=%fused_computation.2 | convolution fusion | flops 2148532224 | bytes 6291456 | tf_op jit(solution)/shard_map/cond/branch_1_fun/dot_general | solution.py:246
  306.9 4.4 %multiply_bitcast_fusion = f32[1,1,1024,1024]{3,2,1,0:T(8,128)} fusion(bf16[1024,1024]{1,0:T(8,128)(2,1)S(1)} %bitcast_select_fusion), kind=kOutput, calls=%fused_computation.1 | convolution fusion | flops 2148532224 | bytes 6291456 | tf_op jit(solution)/shard_map/cond/branch_1_fun/dot_general | solution.py:252
  (62 shorter events, 6.5 us)
Async XLA Ops:
  7.2 1.3 slice-start
  7.2 168.0 %all-gather.2.cloned.1.call-start = ((), (), s32[]{:S(2)}) async-start(), calls=%async_computation.2 | async-start | bytes 13762560 | tf_op jit(solution)/shard_map/all_gather | solution.py:217
  8.5 0.9 slice-start.1
  9.8 33.7 %collective-permute-start.1 = (bf16[128,2688]{0,1:T(8,128)(2,1)S(1)}, bf16[128,2688]{0,1:T(8,128)(2,1)}, u32[]{:S(2)}, u32[]{:S(2)}) collective-permute-start(bf16[128,2688]{0,1:T(8,128)(2,1)S(1)} %get-tuple-element.46), channel_id=1, source_target_pairs={{0,68},{1,69},{2,70},{3,71},{4,64},{5,65},{6,66},{7,67},{8,76},{9,... | collective-permute-start | bytes 2064392 | tf_op jit(solution)/shard_map/ppermute | solution.py:212
  14.1 33.2 %collective-permute-start = (bf16[128,2688]{0,1:T(8,128)(2,1)S(1)}, bf16[128,2688]{0,1:T(8,128)(2,1)S(1)}, u32[]{:S(2)}, u32[]{:S(2)}) collective-permute-start(bf16[128,2688]{0,1:T(8,128)(2,1)S(1)} %get-tuple-element.45), channel_id=1, source_target_pairs={{0,4},{1,5},{2,6},{3,7},{4,0},{5,1},{6,2},{7,3},{8,12},{9,13},{10,... | collective-permute-start | bytes 2064392 | tf_op jit(solution)/shard_map/ppermute | solution.py:198
  43.5 17.9 %collective-permute-start.2 = (bf16[128,2688]{0,1:T(8,128)(2,1)}, bf16[128,2688]{0,1:T(8,128)(2,1)S(1)}, u32[]{:S(2)}, u32[]{:S(2)}) collective-permute-start(bf16[128,2688]{0,1:T(8,128)(2,1)} %collective-permute-done.1), channel_id=1, source_target_pairs={{0,68},{1,69},{2,70},{3,71},{4,64},{5,65},{6,66},{7,67},{8,76},{9,... | collective-permute-start | bytes 2064392 | tf_op jit(solution)/shard_map/ppermute | solution.py:212
  67.8 1.0 copy-start.8
  67.8 2.4 copy-start.9
  67.8 6.6 %copy-start.10 = (s32[1024]{0:T(1024)S(1)}, s32[1024]{0:T(1024)}, u32[]{:S(2)}) copy-start(s32[1024]{0:T(1024)} %param.14) | copy-start | bytes 12292
  67.8 197.5 %reduce-scatter.2.cloned.1.call-start = ((), (), s32[]{:S(2)}) async-start(), calls=%async_computation.3 | async-start | bytes 6193152 | tf_op jit(solution)/shard_map/reduce_scatter | solution.py:237
  68.8 9.9 %collective-permute-start.3 = (bf16[1024,256]{1,0:T(8,128)(2,1)S(1)}, bf16[1024,256]{1,0:T(8,128)(2,1)S(1)}, u32[]{:S(2)}, u32[]{:S(2)}) collective-permute-start(bf16[1024,256]{1,0:T(8,128)(2,1)S(1)} %copy-done.8), channel_id=1, source_target_pairs={{0,8},{8,16},{16,24},{24,32},{32,40},{40,48},{48,56},{56,64},{64,7... | collective-permute-start | bytes 1572872 | tf_op jit(solution)/shard_map/ppermute | solution.py:87
  70.2 9.6 %collective-permute-start.4 = (bf16[1024,256]{1,0:T(8,128)(2,1)S(1)}, bf16[1024,256]{1,0:T(8,128)(2,1)S(1)}, u32[]{:S(2)}, u32[]{:S(2)}) collective-permute-start(bf16[1024,256]{1,0:T(8,128)(2,1)S(1)} %copy-done.9), channel_id=1, source_target_pairs={{0,8},{8,16},{16,24},{24,32},{32,40},{40,48},{48,56},{56,64},{64,7... | collective-permute-start | bytes 1572872 | tf_op jit(solution)/shard_map/ppermute | solution.py:87
  108.3 3.5 %copy-start.7 = (f32[2048,256]{1,0:T(8,128)S(1)}, f32[2048,256]{1,0:T(8,128)}, u32[]{:S(2)}) copy-start(f32[2048,256]{1,0:T(8,128)} %get-tuple-element.34) | copy-start | bytes 6291460
  115.3 8.6 %copy-start = (f32[1024,512]{1,0:T(8,128)S(1)}, f32[1024,512]{1,0:T(8,128)}, u32[]{:S(2)}) copy-start(f32[1024,512]{1,0:T(8,128)} %get-tuple-element.33) | copy-start | bytes 6291460
  117.4 14.9 %collective-permute-start.6 = (bf16[1024,2,128]{2,1,0:T(2,128)(2,1)}, bf16[1024,2,128]{2,1,0:T(2,128)(2,1)}, u32[]{:S(2)}, u32[]{:S(2)}) collective-permute-start(bf16[1024,2,128]{2,1,0:T(2,128)(2,1)} %convert_element_type.45), channel_id=1, source_target_pairs={{8,0},{16,8},{24,16},{32,24},{40,32},{48,40},{56,48},{64,56},{72,6... | collective-permute-start | bytes 1572872 | tf_op jit(solution)/shard_map/ppermute | solution.py:87
  122.5 11.8 %collective-permute-start.5 = (bf16[1024,2,128]{2,1,0:T(2,128)(2,1)}, bf16[1024,2,128]{2,1,0:T(2,128)(2,1)}, u32[]{:S(2)}, u32[]{:S(2)}) collective-permute-start(bf16[1024,2,128]{2,1,0:T(2,128)(2,1)} %convert_element_type.43), channel_id=1, source_target_pairs={{8,0},{16,8},{24,16},{32,24},{40,32},{48,40},{56,48},{64,56},{72,6... | collective-permute-start | bytes 1572872 | tf_op jit(solution)/shard_map/ppermute | solution.py:87
  129.1 1.2 copy-start.1
  130.7 1.6 copy-start.4
  132.3 2.0 copy-start.3
  136.1 1.2 copy-start.2
  137.3 3.1 copy-start.5
  140.9 43.1 %copy-start.6 = (bf16[2,4,128,1024]{3,2,0,1:T(8,128)(2,1)}, bf16[2,4,128,1024]{3,2,0,1:T(8,128)(2,1)S(1)}, u32[]{:S(2)}) copy-start(bf16[2,4,128,1024]{3,2,0,1:T(8,128)(2,1)S(1)} %copy.43) | copy-start | bytes 6291460
  175.1 9.2 %copy-start.11 = (bf16[4,2,128,5376]{3,2,1,0:T(8,128)(2,1)S(1)}, bf16[4,2,128,5376]{3,2,1,0:T(8,128)(2,1)}, u32[]{:S(2)}) copy-start(bf16[4,2,128,5376]{3,2,1,0:T(8,128)(2,1)} %all-gather.2.cloned.1.call-done) | copy-start | bytes 33030148
  184.0 9.3 %collective-permute-start.7 = (bf16[2688,1024]{1,0:T(8,128)(2,1)S(1)}, bf16[2688,1024]{1,0:T(8,128)(2,1)S(1)}, u32[]{:S(2)}, u32[]{:S(2)}) collective-permute-start(bf16[2688,1024]{1,0:T(8,128)(2,1)S(1)} %convolution_convert_fusion), channel_id=1, source_target_pairs={{0,8},{8,0},{16,24},{24,16},{32,40},{40,32},{48,56},{56,48},{64,72... | collective-permute-start | bytes 16515080 | tf_op jit(solution)/shard_map/ppermute | solution.py:229
  268.7 31.7 %all-to-all-start = ((bf16[16,64,1024]{2,1,0:T(8,128)(2,1)}), bf16[16,64,1024]{2,1,0:T(8,128)(2,1)S(1)}, u32[]{:S(2)}, u32[]{:S(2)}) async-start(bf16[16,64,1024]{2,1,0:T(8,128)(2,1)} %broadcast_select_fusion), calls=%async_computation.1 | async-start | bytes 4194304 | tf_op jit(solution)/shard_map/all_to_all | solution.py:137
Sparse Core Ops, SparseCore 0:
  67.9 107.1 all-gather.1
  198.7 66.5 reduce-scatter.1

commit v9 on v7

--- a/solution.py
+++ b/solution.py
@@ -198,15 +198,13 @@
         local, "head", [(src, (src + lane_count) % head_count) for src in range(head_count)]
     )
     upper = group_index // lane_count
-    pair = jnp.where(upper == 0, jnp.stack([local, partner]), jnp.stack([partner, local]))
+    pair = jnp.stack([local, partner])
     lanes = [list(range(start, start + lane_count)) for start in (0, lane_count)]
     gathered = lax.all_gather(pair, "head", axis=0, tiled=False, axis_index_groups=lanes)
     gathered = gathered.reshape(-1, D)
-    column_grads = (
-        column_grads.reshape(2, lane_count, inputs.shape[0], -1)
-        .transpose(1, 0, 2, 3)
-        .reshape(column_grads.shape)
-    )
+    halves = column_grads.reshape(2, lane_count, inputs.shape[0], -1)
+    halves = lax.dynamic_slice_in_dim(jnp.concatenate([halves, halves], 0), upper, 2, 0)
+    column_grads = halves.transpose(1, 0, 2, 3).reshape(column_grads.shape)
     half = D // 2
     given = lax.dot_general(
         gathered[:, :half], column_grads, (((0,), (0,)), ((), ())),

time: 303 us -> 298 us (0.983)
  waiting for transfers between devices: 158 us -> 153 us
    all_gather x1, waiting for transfers between devices: 34.1 us -> 28.9 us  [per_device(): lax.all_gather(pair, 'head', axis=0, tiled=False, axis_index_groups=lanes)]
    select_n x1 -> x0, other arithmetic: 3.31 us -> none  [per_device(): jnp.where(upper == 0, jnp.stack([local, partner]), jnp.stack([partner, lo...]
    another operation x3 -> x4, other arithmetic: 5.94 us -> 6.82 us
  transfers between devices with their start and end apart: 9 -> 9, of which waited for: 5 -> 5; matrix products, arithmetic and copies ran while one was open for 15% -> 17% of each run, Pallas kernels for 9% -> 9%
where the time goes in v9:
time: 298 us; the launch traced here: 297 us
  waiting for transfers between devices  153 us (51%)
  other arithmetic  31.2 us (10%)
  local copies, waits for them, and re-layouts  28 us (9%)
  Pallas kernels  27.4 us (9%)
  matrix products  25.7 us (9%)
  starting transfers between devices  16.2 us (5%)
  between operations  15.1 us (5%)
    reduce_scatter x1, waiting for transfers between devices, per_device(): lax.psum_scatter(summed, 'seq', scatter_dimension=0, tiled=True, axis_ind...  65.2 us
    ppermute x1, waiting for transfers between devices, per_device(): lax.ppermute(local, 'head', [(src, (src + lane_count) % head_count) for s...  30.2 us
    all_gather x1, waiting for transfers between devices, per_device(): lax.all_gather(pair, 'head', axis=0, tiled=False, axis_index_groups=lanes)  28.9 us
    pallas_call x1, Pallas kernels, attention_backward(): pl.pallas_call(attention_kernel, grid=(KV_DEV,), out_shape=(jax.ShapeDtyp...  27.4 us
    all_to_all x1, waiting for transfers between devices, owned_block(): received = lax.all_to_all(send, 'seq', 0, 0, tiled=False)  27.3 us
    dot_general x1, matrix products, per_device(): lax.dot_general(gathered[:, :half], column_grads, (((0,), (0,)), ((), ())...  8.87 us
    ppermute x4, starting transfers between devices, shifted(): lax.ppermute(value, axis, [(source, source + steps) for source in range(i...  8.27 us
    dot_general x1, matrix products, per_device(): lax.dot_general(gathered[:, half:], column_grads, (((0,), (0,)), ((), ())...  7.99 us
  transfers between devices with their start and end apart: 9, of which 5 were waited for; matrix products, arithmetic and copies ran while one was open for 17% of the time, Pallas kernels for 9%

profile of v9, /device:TPU:0, one launch (start us, length us, event | category | flops | bytes accessed | tf_op | source)
XLA Modules:
  0.0 296.9 jit_solution(2229182574701896520)
XLA Ops:
  7.2 1.2 slice-done
  9.7 4.1 %collective-permute-start = (bf16[128,5376]{0,1:T(8,128)(2,1)S(1)}, bf16[128,5376]{0,1:T(8,128)(2,1)S(1)}, u32[]{:S(2)}, u32[]{:S(2)}) collective-permute-start(bf16[128,5376]{0,1:T(8,128)(2,1)S(1)} %bitcast.52), channel_id=1, source_target_pairs={{0,4},{1,5},{2,6},{3,7},{4,0},{5,1},{6,2},{7,3},{8,12},{9,13},{10,... | collective-permute-start | bytes 4128776 | tf_op jit(solution)/shard_map/ppermute | solution.py:197
  13.8 30.2 %collective-permute-done = bf16[128,5376]{0,1:T(8,128)(2,1)S(1)} collective-permute-done((bf16[128,5376]{0,1:T(8,128)(2,1)S(1)}, bf16[128,5376]{0,1:T(8,128)(2,1)S(1)}, u32[]{:S(2)}, u32[]{:S(2)}) %collective-permute-start) | collective-permute-done | bytes 1376288 | tf_op jit(solution)/shard_map/ppermute | solution.py:197
  44.2 2.7 copy.37
  47.0 1.0 copy-done.7
  48.0 1.3 collective-permute-start.1
  49.3 4.2 %collective-permute-start.2 = (bf16[1024,256]{1,0:T(8,128)(2,1)S(1)}, bf16[1024,256]{1,0:T(8,128)(2,1)S(1)}, u32[]{:S(2)}, u32[]{:S(2)}) collective-permute-start(bf16[1024,256]{1,0:T(8,128)(2,1)S(1)} %copy-done.8), channel_id=1, source_target_pairs={{0,8},{8,16},{16,24},{24,32},{32,40},{40,48},{48,56},{56,64},{64,7... | collective-permute-start | bytes 1572872 | tf_op jit(solution)/shard_map/ppermute | solution.py:87
  53.6 1.0 copy.38.band_ref
  54.6 1.9 multiply_cosine_fusion
  56.5 1.3 pad_maximum_fusion.5
  57.8 1.1 pad_maximum_fusion.3.k_ref
  58.9 1.0 pad_maximum_fusion.4.v_ref
  60.0 27.4 %shard_map.90 = (f32[1024,512]{1,0:T(8,128)}, f32[2048,256]{1,0:T(8,128)}, f32[2048,256]{1,0:T(8,128)}) custom-call(s32[1024,1]{1,0:T(8,128)} %copy.38.band_ref, bf16[1024,512]{1,0:T(8,128)(2,1)} %q_ref.1, bf16[1024,512]{1,0:T(8,128)(2,1)} %do_ref.1, bf16[2048,256]{1,0:T(8,128)(2,1)} %pad_maximum_fusion.3.k_ref, bf16[2048,256]{1,0:T(8,128)(2,1)} %pad_maximum_fusion.4.v_ref), custom_call_target="tpu_custom_call" | custom-call | tf_op jit(solution)/shard_map/pallas_call | solution.py:71
  87.4 2.5 slice.55
  89.9 2.2 slice.83
  92.1 1.1 slice.60
  93.2 0.9 slice.82
  94.1 1.7 reshape.95
  95.8 1.8 slice.56
  97.5 2.0 convert_element_type.43
  99.5 1.3 collective-permute-start.3
  100.8 2.7 slice.61
  103.5 2.0 convert_element_type.45
  105.5 1.5 collective-permute-start.4
  107.0 2.2 broadcast_multiply_fusion
  109.2 1.2 slice_negate_fusion
  110.4 1.1 pad_maximum_fusion.1
  112.0 1.6 fusion.7
  113.6 1.8 fusion.13
  115.3 1.1 slice_negate_fusion.1
  116.5 3.4 %fusion.8 = bf16[1024,2,128]{2,1,0:T(2,128)(2,1)} fusion(f32[1024,2,64]{2,1,0:T(2,128)S(1)} %get-tuple-element.48, f32[1024,2,64]{2,1,0:T(2,128)S(1)} %get-tuple-element.47, f32[1024,2,128]{2,1,0:T(2,128)S(1)} %slice.56, bf16[1024,2,128]{2,1,0:T(2,128)(2,1)} %collective-permute-done.3, f32[1024,128]{1,0:T(8,128)S(1)} %copy-done.1), kind=kLoop, calls=%fused_computation.39 | loop fusion | flops 1572864 | bytes 3670016 | tf_op jit(solution)/shard_map/convert.4
  119.9 1.5 concatenate.63
  121.4 1.6 add_convert_fusion.1
  123.3 1.7 fusion.4
  125.2 28.9 %all-gather.3.cloned.1.call-done = bf16[8,128,5376]{2,1,0:T(8,128)(2,1)} async-done(((bf16[2,128,5376]{2,1,0:T(8,128)(2,1)}), bf16[8,128,5376]{2,1,0:T(8,128)(2,1)}) %all-gather.3.cloned.1.call-update) | async-done | bytes 11010064 | tf_op jit(solution)/shard_map/all_gather | solution.py:203
  154.1 8.9 %convolution_convert_fusion = bf16[2688,1024]{1,0:T(8,128)(2,1)S(1)} fusion(bf16[1024,1024]{1,0:T(8,128)(2,1)S(1)} %bitcast.58, bf16[1024,5376]{1,0:T(8,128)(2,1)} %bitcast.63), kind=kOutput, calls=%fused_computation.6 | convolution fusion | flops 5639897088 | bytes 13107200 | tf_op jit(solution)/shard_map/dot_general | solution.py:209
  163.1 8.0 %convolution_convert_fusion.1 = bf16[2688,1024]{1,0:T(8,128)(2,1)S(1)} fusion(bf16[1024,1024]{1,0:T(8,128)(2,1)} %bitcast.59, bf16[1024,5376]{1,0:T(8,128)(2,1)S(1)} %bitcast.64), kind=kOutput, calls=%fused_computation.7 | convolution fusion | flops 5639897088 | bytes 13107200 | tf_op jit(solution)/shard_map/dot_general | solution.py:214
  171.1 1.0 collective-permute-done.5
  172.1 5.2 %add_convert_fusion = bf16[2688,1024]{1,0:T(8,128)(2,1)} fusion(bf16[2688,1024]{1,0:T(8,128)(2,1)S(1)} %collective-permute-done.5, bf16[2688,1024]{1,0:T(8,128)(2,1)S(1)} %convolution_convert_fusion.1), kind=kLoop, calls=%fused_computation.5 | loop fusion | flops 11010048 | bytes 16515072 | tf_op jit(solution)/shard_map/convert_element_type | solution.py:219
  177.3 1.3 fusion.16
  178.8 65.2 %reduce-scatter.2.cloned.1.call-done = bf16[336,1024]{1,0:T(8,128)(2,1)} async-done(((bf16[2688,1024]{1,0:T(8,128)(2,1)}), bf16[336,1024]{1,0:T(8,128)(2,1)}) %reduce-scatter.2.cloned.1.call-update) | async-done | bytes 688144 | tf_op jit(solution)/shard_map/reduce_scatter | solution.py:221
  244.0 1.2 concatenate.67
  245.9 1.6 broadcast_select_fusion
  247.4 3.7 %all-to-all-start = ((bf16[16,64,1024]{2,1,0:T(8,128)(2,1)}), bf16[16,64,1024]{2,1,0:T(8,128)(2,1)S(1)}, u32[]{:S(2)}, u32[]{:S(2)}) async-start(bf16[16,64,1024]{2,1,0:T(8,128)(2,1)} %broadcast_select_fusion), calls=%async_computation.1 | async-start | bytes 4194304 | tf_op jit(solution)/shard_map/all_to_all | solution.py:137
  251.8 27.3 %all-to-all-done = bf16[16,64,1024]{2,1,0:T(8,128)(2,1)S(1)} async-done(((bf16[16,64,1024]{2,1,0:T(8,128)(2,1)}), bf16[16,64,1024]{2,1,0:T(8,128)(2,1)S(1)}, u32[]{:S(2)}, u32[]{:S(2)}) %all-to-all-start) | async-done | bytes 2097184 | tf_op jit(solution)/shard_map/all_to_all | solution.py:137
  279.1 10.9 %conditional.1 = (f32[1,1,1024,1024]{3,2,1,0:T(8,128)}, f32[1,1,1024,1024]{3,2,1,0:T(8,128)}) conditional(s32[]{:T(128)} %convert_element_type.41, () %tuple.21, (pred[6]{0:T(512)(128)(4,1)S(1)}, s32[6]{0:T(128)S(1)}, bf16[16,64,1024]{2,1,0:T(8,128)(2,1)S(1)}) %tuple.23), branch_computations={%region_3.4_spmd, %region_4.6_spmd} | conditional | flops 4298113024 | bytes 18350140 | solution.py:249
  281.2 4.4 %multiply_bitcast_fusion.1 = f32[1,1,1024,1024]{3,2,1,0:T(8,128)} fusion(bf16[1024,1024]{1,0:T(8,128)(2,1)S(1)} %bitcast_select_fusion), kind=kOutput, calls=%fused_computation.2 | convolution fusion | flops 2148532224 | bytes 6291456 | tf_op jit(solution)/shard_map/cond/branch_1_fun/dot_general | solution.py:230
  285.6 4.4 %multiply_bitcast_fusion = f32[1,1,1024,1024]{3,2,1,0:T(8,128)} fusion(bf16[1024,1024]{1,0:T(8,128)(2,1)S(1)} %bitcast_select_fusion), kind=kOutput, calls=%fused_computation.1 | convolution fusion | flops 2148532224 | bytes 6291456 | tf_op jit(solution)/shard_map/cond/branch_1_fun/dot_general | solution.py:236
  (54 shorter events, 4.8 us)
Async XLA Ops:
  7.2 1.3 slice-start
  7.2 146.9 %all-gather.3.cloned.1.call-start = ((), (), s32[]{:S(2)}) async-start(), calls=%async_computation.3 | async-start | bytes 13762560 | tf_op jit(solution)/shard_map/all_gather | solution.py:203
  8.5 0.9 slice-start.1
  9.7 34.2 %collective-permute-start = (bf16[128,5376]{0,1:T(8,128)(2,1)S(1)}, bf16[128,5376]{0,1:T(8,128)(2,1)S(1)}, u32[]{:S(2)}, u32[]{:S(2)}) collective-permute-start(bf16[128,5376]{0,1:T(8,128)(2,1)S(1)} %bitcast.52), channel_id=1, source_target_pairs={{0,4},{1,5},{2,6},{3,7},{4,0},{5,1},{6,2},{7,3},{8,12},{9,13},{10,... | collective-permute-start | bytes 4128776 | tf_op jit(solution)/shard_map/ppermute | solution.py:197
  46.9 1.0 copy-start.7
  46.9 2.4 copy-start.8
  46.9 6.6 %copy-start.9 = (s32[1024]{0:T(1024)S(1)}, s32[1024]{0:T(1024)}, u32[]{:S(2)}) copy-start(s32[1024]{0:T(1024)} %param.14) | copy-start | bytes 12292
  47.0 197.0 %reduce-scatter.2.cloned.1.call-start = ((), (), s32[]{:S(2)}) async-start(), calls=%async_computation.2 | async-start | bytes 6193152 | tf_op jit(solution)/shard_map/reduce_scatter | solution.py:221
  48.0 9.9 %collective-permute-start.1 = (bf16[1024,256]{1,0:T(8,128)(2,1)S(1)}, bf16[1024,256]{1,0:T(8,128)(2,1)S(1)}, u32[]{:S(2)}, u32[]{:S(2)}) collective-permute-start(bf16[1024,256]{1,0:T(8,128)(2,1)S(1)} %copy-done.7), channel_id=1, source_target_pairs={{0,8},{8,16},{16,24},{24,32},{32,40},{40,48},{48,56},{56,64},{64,7... | collective-permute-start | bytes 1572872 | tf_op jit(solution)/shard_map/ppermute | solution.py:87
  49.3 9.6 %collective-permute-start.2 = (bf16[1024,256]{1,0:T(8,128)(2,1)S(1)}, bf16[1024,256]{1,0:T(8,128)(2,1)S(1)}, u32[]{:S(2)}, u32[]{:S(2)}) collective-permute-start(bf16[1024,256]{1,0:T(8,128)(2,1)S(1)} %copy-done.8), channel_id=1, source_target_pairs={{0,8},{8,16},{16,24},{24,32},{32,40},{40,48},{48,56},{56,64},{64,7... | collective-permute-start | bytes 1572872 | tf_op jit(solution)/shard_map/ppermute | solution.py:87
  87.4 4.7 %copy-start.6 = (f32[2048,256]{1,0:T(8,128)S(1)}, f32[2048,256]{1,0:T(8,128)}, u32[]{:S(2)}) copy-start(f32[2048,256]{1,0:T(8,128)} %get-tuple-element.35) | copy-start | bytes 6291460
  89.9 4.2 %copy-start = (f32[1024,512]{1,0:T(8,128)S(1)}, f32[1024,512]{1,0:T(8,128)}, u32[]{:S(2)}) copy-start(f32[1024,512]{1,0:T(8,128)} %get-tuple-element.33) | copy-start | bytes 6291460
  99.5 14.0 %collective-permute-start.3 = (bf16[1024,2,128]{2,1,0:T(2,128)(2,1)}, bf16[1024,2,128]{2,1,0:T(2,128)(2,1)}, u32[]{:S(2)}, u32[]{:S(2)}) collective-permute-start(bf16[1024,2,128]{2,1,0:T(2,128)(2,1)} %convert_element_type.43), channel_id=1, source_target_pairs={{8,0},{16,8},{24,16},{32,24},{40,32},{48,40},{56,48},{64,56},{72,6... | collective-permute-start | bytes 1572872 | tf_op jit(solution)/shard_map/ppermute | solution.py:87
  105.5 15.9 %collective-permute-start.4 = (bf16[1024,2,128]{2,1,0:T(2,128)(2,1)}, bf16[1024,2,128]{2,1,0:T(2,128)(2,1)}, u32[]{:S(2)}, u32[]{:S(2)}) collective-permute-start(bf16[1024,2,128]{2,1,0:T(2,128)(2,1)} %convert_element_type.45), channel_id=1, source_target_pairs={{8,0},{16,8},{24,16},{32,24},{40,32},{48,40},{56,48},{64,56},{72,6... | collective-permute-start | bytes 1572872 | tf_op jit(solution)/shard_map/ppermute | solution.py:87
  110.4 1.2 copy-start.1
  111.9 1.6 copy-start.2
  116.5 4.9 %copy-start.4 = (f32[1024,2,128]{2,1,0:T(2,128)S(1)}, f32[1024,2,128]{2,1,0:T(2,128)}, u32[]{:S(2)}) copy-start(f32[1024,2,128]{2,1,0:T(2,128)} %slice.61) | copy-start | bytes 3145732
  119.9 3.4 %copy-start.3 = (bf16[1024,512]{1,0:T(8,128)(2,1)S(1)}, bf16[1024,512]{1,0:T(8,128)(2,1)}, u32[]{:S(2)}) copy-start(bf16[1024,512]{1,0:T(8,128)(2,1)} %fusion.7) | copy-start | bytes 3145732
  125.2 37.8 %copy-start.5 = (bf16[2,4,128,1024]{3,2,0,1:T(8,128)(2,1)}, bf16[2,4,128,1024]{3,2,0,1:T(8,128)(2,1)S(1)}, u32[]{:S(2)}) copy-start(bf16[2,4,128,1024]{3,2,0,1:T(8,128)(2,1)S(1)} %copy.46) | copy-start | bytes 6291460
  154.1 9.0 %copy-start.10 = (bf16[8,128,5376]{2,1,0:T(8,128)(2,1)S(1)}, bf16[8,128,5376]{2,1,0:T(8,128)(2,1)}, u32[]{:S(2)}) copy-start(bf16[8,128,5376]{2,1,0:T(8,128)(2,1)} %all-gather.3.cloned.1.call-done) | copy-start | bytes 33030148
  163.0 9.1 %collective-permute-start.5 = (bf16[2688,1024]{1,0:T(8,128)(2,1)S(1)}, bf16[2688,1024]{1,0:T(8,128)(2,1)S(1)}, u32[]{:S(2)}, u32[]{:S(2)}) collective-permute-start(bf16[2688,1024]{1,0:T(8,128)(2,1)S(1)} %convolution_convert_fusion), channel_id=1, source_target_pairs={{0,8},{8,0},{16,24},{24,16},{32,40},{40,32},{48,56},{56,48},{64,72... | collective-permute-start | bytes 16515080 | tf_op jit(solution)/shard_map/ppermute | solution.py:213
  247.4 31.7 %all-to-all-start = ((bf16[16,64,1024]{2,1,0:T(8,128)(2,1)}), bf16[16,64,1024]{2,1,0:T(8,128)(2,1)S(1)}, u32[]{:S(2)}, u32[]{:S(2)}) async-start(bf16[16,64,1024]{2,1,0:T(8,128)(2,1)} %broadcast_select_fusion), calls=%async_computation.1 | async-start | bytes 4194304 | tf_op jit(solution)/shard_map/all_to_all | solution.py:137
Sparse Core Ops, SparseCore 0:
  47.1 106.9 all-gather.2
  177.4 66.5 reduce-scatter.1

commit v10 on v9

--- a/solution.py
+++ b/solution.py
@@ -184,19 +184,24 @@
     ).astype(jnp.bfloat16)
     column_count = column_grads.shape[1]
     core = seq_index % 2
-    paired = arrange_features(inputs, seq_count).reshape(inputs.shape[0], seq_count // 2, 2, -1)
-    local = jnp.concatenate(
-        [
-            lax.dynamic_index_in_dim(paired, 1 - core, 2, keepdims=False),
-            lax.dynamic_index_in_dim(paired, core, 2, keepdims=False),
-        ],
-        1,
-    ).reshape(inputs.shape[0], D)
     head_count = lax.axis_size("head")
     lane_count = head_count // 2
-    partner = lax.ppermute(
-        local, "head", [(src, (src + lane_count) % head_count) for src in range(head_count)]
-    )
+    raw_partner = lax.ppermute(
+        inputs, "head", [(src, (src + lane_count) % head_count) for src in range(head_count)]
+    )
+
+    def parity_order(rows):
+        paired = arrange_features(rows, seq_count).reshape(rows.shape[0], seq_count // 2, 2, -1)
+        return jnp.concatenate(
+            [
+                lax.dynamic_index_in_dim(paired, 1 - core, 2, keepdims=False),
+                lax.dynamic_index_in_dim(paired, core, 2, keepdims=False),
+            ],
+            1,
+        ).reshape(rows.shape[0], D)
+
+    local = parity_order(inputs)
+    partner = parity_order(raw_partner)
     upper = group_index // lane_count
     pair = jnp.stack([local, partner])
     lanes = [list(range(start, start + lane_count)) for start in (0, lane_count)]

time: 298 us -> 301 us (1.010)
  local copies, waits for them, and re-layouts: 28 us -> 31.2 us
where the time goes in v10:
time: 301 us; the launch traced here: 299 us
  waiting for transfers between devices  152 us (50%)
  other arithmetic  31.4 us (10%)
  local copies, waits for them, and re-layouts  31.2 us (10%)
  Pallas kernels  27.4 us (9%)
  matrix products  25.7 us (9%)
  starting transfers between devices  16.2 us (5%)
  between operations  15 us (5%)
    reduce_scatter x1, waiting for transfers between devices, per_device(): lax.psum_scatter(summed, 'seq', scatter_dimension=0, tiled=True, axis_ind...  65.2 us
    ppermute x1, waiting for transfers between devices, per_device(): lax.ppermute(inputs, 'head', [(src, (src + lane_count) % head_count) for...  29 us
    all_gather x1, waiting for transfers between devices, per_device(): lax.all_gather(pair, 'head', axis=0, tiled=False, axis_index_groups=lanes)  29 us
    pallas_call x1, Pallas kernels, attention_backward(): pl.pallas_call(attention_kernel, grid=(KV_DEV,), out_shape=(jax.ShapeDtyp...  27.4 us
    all_to_all x1, waiting for transfers between devices, owned_block(): received = lax.all_to_all(send, 'seq', 0, 0, tiled=False)  27.3 us
    dot_general x1, matrix products, per_device(): lax.dot_general(gathered[:, :half], column_grads, (((0,), (0,)), ((), ())...  8.87 us
    ppermute x4, starting transfers between devices, shifted(): lax.ppermute(value, axis, [(source, source + steps) for source in range(i...  8.27 us
    dot_general x1, matrix products, per_device(): lax.dot_general(gathered[:, half:], column_grads, (((0,), (0,)), ((), ())...  7.99 us
  transfers between devices with their start and end apart: 9, of which 5 were waited for; matrix products, arithmetic and copies ran while one was open for 17% of the time, Pallas kernels for 9%

profile of v10, /device:TPU:0, one launch (start us, length us, event | category | flops | bytes accessed | tf_op | source)
XLA Modules:
  0.0 299.1 jit_solution(13472596471541169614)
XLA Ops:
  7.2 1.8 copy.41
  9.0 4.1 %collective-permute-start = (bf16[128,5376]{0,1:T(8,128)(2,1)S(1)}, bf16[128,5376]{0,1:T(8,128)(2,1)}, u32[]{:S(2)}, u32[]{:S(2)}) collective-permute-start(bf16[128,5376]{0,1:T(8,128)(2,1)S(1)} %copy.41), channel_id=1, source_target_pairs={{0,4},{1,5},{2,6},{3,7},{4,0},{5,1},{6,2},{7,3},{8,12},{9,13},{10,... | collective-permute-start | bytes 4128776 | tf_op jit(solution)/shard_map/ppermute | solution.py:189
  13.2 1.2 copy.42
  14.4 29.0 %collective-permute-done = bf16[128,5376]{0,1:T(8,128)(2,1)} collective-permute-done((bf16[128,5376]{0,1:T(8,128)(2,1)S(1)}, bf16[128,5376]{0,1:T(8,128)(2,1)}, u32[]{:S(2)}, u32[]{:S(2)}) %collective-permute-start) | collective-permute-done | bytes 1376288 | tf_op jit(solution)/shard_map/ppermute | solution.py:189
  43.4 1.4 slice.76
  46.5 2.7 copy.46
  50.2 1.3 collective-permute-start.1
  51.5 4.2 %collective-permute-start.2 = (bf16[1024,256]{1,0:T(8,128)(2,1)S(1)}, bf16[1024,256]{1,0:T(8,128)(2,1)S(1)}, u32[]{:S(2)}, u32[]{:S(2)}) collective-permute-start(bf16[1024,256]{1,0:T(8,128)(2,1)S(1)} %copy-done.9), channel_id=1, source_target_pairs={{0,8},{8,16},{16,24},{24,32},{32,40},{40,48},{48,56},{56,64},{64,7... | collective-permute-start | bytes 1572872 | tf_op jit(solution)/shard_map/ppermute | solution.py:87
  55.8 1.0 copy.47.band_ref
  56.9 1.9 multiply_cosine_fusion
  58.8 1.3 pad_maximum_fusion.6
  60.1 1.1 pad_maximum_fusion.4.k_ref
  61.1 1.1 pad_maximum_fusion.5.v_ref
  62.2 27.4 %shard_map.90 = (f32[1024,512]{1,0:T(8,128)}, f32[2048,256]{1,0:T(8,128)}, f32[2048,256]{1,0:T(8,128)}) custom-call(s32[1024,1]{1,0:T(8,128)} %copy.47.band_ref, bf16[1024,512]{1,0:T(8,128)(2,1)} %q_ref.1, bf16[1024,512]{1,0:T(8,128)(2,1)} %do_ref.1, bf16[2048,256]{1,0:T(8,128)(2,1)} %pad_maximum_fusion.4.k_ref, bf16[2048,256]{1,0:T(8,128)(2,1)} %pad_maximum_fusion.5.v_ref), custom_call_target="tpu_custom_call" | custom-call | tf_op jit(solution)/shard_map/pallas_call | solution.py:71
  89.6 2.4 slice.63
  92.0 2.2 slice.95
  94.2 1.1 slice.68
  96.2 1.7 reshape.101
  97.9 1.8 slice.64
  99.7 2.0 convert_element_type.43
  101.6 1.3 collective-permute-start.3
  102.9 2.7 slice.69
  105.6 2.0 convert_element_type.45
  107.6 1.5 collective-permute-start.4
  109.1 2.2 broadcast_multiply_fusion
  111.3 1.2 slice_negate_fusion
  112.6 1.1 pad_maximum_fusion.1
  114.1 1.6 fusion.7
  115.7 1.8 fusion.17
  117.5 1.1 slice_negate_fusion.1
  118.6 3.4 %fusion.8 = bf16[1024,2,128]{2,1,0:T(2,128)(2,1)} fusion(f32[1024,2,64]{2,1,0:T(2,128)S(1)} %get-tuple-element.50, f32[1024,2,64]{2,1,0:T(2,128)S(1)} %get-tuple-element.49, f32[1024,2,128]{2,1,0:T(2,128)S(1)} %slice.64, bf16[1024,2,128]{2,1,0:T(2,128)(2,1)} %collective-permute-done.3, f32[1024,128]{1,0:T(8,128)S(1)} %copy-done.2), kind=kLoop, calls=%fused_computation.44 | loop fusion | flops 1572864 | bytes 3670016 | tf_op jit(solution)/shard_map/convert.4
  122.0 1.5 concatenate.78
  123.5 1.6 add_convert_fusion.1
  125.5 1.7 fusion.4
  127.4 29.0 %all-gather.3.cloned.1.call-done = bf16[8,128,5376]{2,1,0:T(8,128)(2,1)} async-done(((bf16[2,128,5376]{2,1,0:T(8,128)(2,1)}), bf16[8,128,5376]{2,1,0:T(8,128)(2,1)}) %all-gather.3.cloned.1.call-update) | async-done | bytes 11010064 | tf_op jit(solution)/shard_map/all_gather | solution.py:208
  156.3 8.9 %convolution_convert_fusion = bf16[2688,1024]{1,0:T(8,128)(2,1)S(1)} fusion(bf16[1024,1024]{1,0:T(8,128)(2,1)S(1)} %bitcast.68, bf16[1024,5376]{1,0:T(8,128)(2,1)} %bitcast.73), kind=kOutput, calls=%fused_computation.6 | convolution fusion | flops 5639897088 | bytes 13107200 | tf_op jit(solution)/shard_map/dot_general | solution.py:214
  165.3 8.0 %convolution_convert_fusion.1 = bf16[2688,1024]{1,0:T(8,128)(2,1)S(1)} fusion(bf16[1024,1024]{1,0:T(8,128)(2,1)} %bitcast.69, bf16[1024,5376]{1,0:T(8,128)(2,1)S(1)} %bitcast.74), kind=kOutput, calls=%fused_computation.7 | convolution fusion | flops 5639897088 | bytes 13107200 | tf_op jit(solution)/shard_map/dot_general | solution.py:219
  173.3 1.0 collective-permute-done.5
  174.3 5.2 %add_convert_fusion = bf16[2688,1024]{1,0:T(8,128)(2,1)} fusion(bf16[2688,1024]{1,0:T(8,128)(2,1)S(1)} %collective-permute-done.5, bf16[2688,1024]{1,0:T(8,128)(2,1)S(1)} %convolution_convert_fusion.1), kind=kLoop, calls=%fused_computation.5 | loop fusion | flops 11010048 | bytes 16515072 | tf_op jit(solution)/shard_map/convert_element_type | solution.py:224
  179.6 1.3 fusion.20
  181.0 65.2 %reduce-scatter.2.cloned.1.call-done = bf16[336,1024]{1,0:T(8,128)(2,1)} async-done(((bf16[2688,1024]{1,0:T(8,128)(2,1)}), bf16[336,1024]{1,0:T(8,128)(2,1)}) %reduce-scatter.2.cloned.1.call-update) | async-done | bytes 688144 | tf_op jit(solution)/shard_map/reduce_scatter | solution.py:226
  246.3 1.2 concatenate.82
  248.1 1.6 broadcast_select_fusion
  249.7 3.7 %all-to-all-start = ((bf16[16,64,1024]{2,1,0:T(8,128)(2,1)}), bf16[16,64,1024]{2,1,0:T(8,128)(2,1)S(1)}, u32[]{:S(2)}, u32[]{:S(2)}) async-start(bf16[16,64,1024]{2,1,0:T(8,128)(2,1)} %broadcast_select_fusion), calls=%async_computation.1 | async-start | bytes 4194304 | tf_op jit(solution)/shard_map/all_to_all | solution.py:137
  254.1 27.3 %all-to-all-done = bf16[16,64,1024]{2,1,0:T(8,128)(2,1)S(1)} async-done(((bf16[16,64,1024]{2,1,0:T(8,128)(2,1)}), bf16[16,64,1024]{2,1,0:T(8,128)(2,1)S(1)}, u32[]{:S(2)}, u32[]{:S(2)}) %all-to-all-start) | async-done | bytes 2097184 | tf_op jit(solution)/shard_map/all_to_all | solution.py:137
  281.4 10.9 %conditional.1 = (f32[1,1,1024,1024]{3,2,1,0:T(8,128)}, f32[1,1,1024,1024]{3,2,1,0:T(8,128)}) conditional(s32[]{:T(128)} %convert_element_type.41, () %tuple.21, (pred[6]{0:T(512)(128)(4,1)S(1)}, s32[6]{0:T(128)S(1)}, bf16[16,64,1024]{2,1,0:T(8,128)(2,1)S(1)}) %tuple.23), branch_computations={%region_3.4_spmd, %region_4.6_spmd} | conditional | flops 4298113024 | bytes 18350140 | solution.py:254
  283.5 4.4 %multiply_bitcast_fusion.1 = f32[1,1,1024,1024]{3,2,1,0:T(8,128)} fusion(bf16[1024,1024]{1,0:T(8,128)(2,1)S(1)} %bitcast_select_fusion), kind=kOutput, calls=%fused_computation.2 | convolution fusion | flops 2148532224 | bytes 6291456 | tf_op jit(solution)/shard_map/cond/branch_1_fun/dot_general | solution.py:235
  287.8 4.4 %multiply_bitcast_fusion = f32[1,1,1024,1024]{3,2,1,0:T(8,128)} fusion(bf16[1024,1024]{1,0:T(8,128)(2,1)S(1)} %bitcast_select_fusion), kind=kOutput, calls=%fused_computation.1 | convolution fusion | flops 2148532224 | bytes 6291456 | tf_op jit(solution)/shard_map/cond/branch_1_fun/dot_general | solution.py:241
  (57 shorter events, 6.9 us)
Async XLA Ops:
  7.2 149.2 %all-gather.3.cloned.1.call-start = ((), (), s32[]{:S(2)}) async-start(), calls=%async_computation.3 | async-start | bytes 13762560 | tf_op jit(solution)/shard_map/all_gather | solution.py:208
  9.0 34.4 %collective-permute-start = (bf16[128,5376]{0,1:T(8,128)(2,1)S(1)}, bf16[128,5376]{0,1:T(8,128)(2,1)}, u32[]{:S(2)}, u32[]{:S(2)}) collective-permute-start(bf16[128,5376]{0,1:T(8,128)(2,1)S(1)} %copy.41), channel_id=1, source_target_pairs={{0,4},{1,5},{2,6},{3,7},{4,0},{5,1},{6,2},{7,3},{8,12},{9,13},{10,... | collective-permute-start | bytes 4128776 | tf_op jit(solution)/shard_map/ppermute | solution.py:189
  14.3 31.4 %copy-start.1 = (bf16[128,16,5,64]{0,3,2,1:T(8,128)(2,1)S(1)}, bf16[128,16,5,64]{0,3,2,1:T(8,128)(2,1)}, u32[]{:S(2)}) copy-start(bf16[128,16,5,64]{0,3,2,1:T(8,128)(2,1)} %copy.42) | copy-start | bytes 3932164
  49.2 1.0 copy-start.8
  49.2 2.4 copy-start.9
  49.2 6.6 %copy-start.10 = (s32[1024]{0:T(1024)S(1)}, s32[1024]{0:T(1024)}, u32[]{:S(2)}) copy-start(s32[1024]{0:T(1024)} %param.14) | copy-start | bytes 12292
  49.2 197.0 %reduce-scatter.2.cloned.1.call-start = ((), (), s32[]{:S(2)}) async-start(), calls=%async_computation.2 | async-start | bytes 6193152 | tf_op jit(solution)/shard_map/reduce_scatter | solution.py:226
  50.2 9.9 %collective-permute-start.1 = (bf16[1024,256]{1,0:T(8,128)(2,1)S(1)}, bf16[1024,256]{1,0:T(8,128)(2,1)S(1)}, u32[]{:S(2)}, u32[]{:S(2)}) collective-permute-start(bf16[1024,256]{1,0:T(8,128)(2,1)S(1)} %copy-done.8), channel_id=1, source_target_pairs={{0,8},{8,16},{16,24},{24,32},{32,40},{40,48},{48,56},{56,64},{64,7... | collective-permute-start | bytes 1572872 | tf_op jit(solution)/shard_map/ppermute | solution.py:87
  51.5 9.6 %collective-permute-start.2 = (bf16[1024,256]{1,0:T(8,128)(2,1)S(1)}, bf16[1024,256]{1,0:T(8,128)(2,1)S(1)}, u32[]{:S(2)}, u32[]{:S(2)}) collective-permute-start(bf16[1024,256]{1,0:T(8,128)(2,1)S(1)} %copy-done.9), channel_id=1, source_target_pairs={{0,8},{8,16},{16,24},{24,32},{32,40},{40,48},{48,56},{56,64},{64,7... | collective-permute-start | bytes 1572872 | tf_op jit(solution)/shard_map/ppermute | solution.py:87
  89.5 4.7 %copy-start.7 = (f32[2048,256]{1,0:T(8,128)S(1)}, f32[2048,256]{1,0:T(8,128)}, u32[]{:S(2)}) copy-start(f32[2048,256]{1,0:T(8,128)} %get-tuple-element.35) | copy-start | bytes 6291460
  92.0 4.2 %copy-start = (f32[1024,512]{1,0:T(8,128)S(1)}, f32[1024,512]{1,0:T(8,128)}, u32[]{:S(2)}) copy-start(f32[1024,512]{1,0:T(8,128)} %get-tuple-element.33) | copy-start | bytes 6291460
  101.6 14.0 %collective-permute-start.3 = (bf16[1024,2,128]{2,1,0:T(2,128)(2,1)}, bf16[1024,2,128]{2,1,0:T(2,128)(2,1)}, u32[]{:S(2)}, u32[]{:S(2)}) collective-permute-start(bf16[1024,2,128]{2,1,0:T(2,128)(2,1)} %convert_element_type.43), channel_id=1, source_target_pairs={{8,0},{16,8},{24,16},{32,24},{40,32},{48,40},{56,48},{64,56},{72,6... | collective-permute-start | bytes 1572872 | tf_op jit(solution)/shard_map/ppermute | solution.py:87
  107.6 15.9 %collective-permute-start.4 = (bf16[1024,2,128]{2,1,0:T(2,128)(2,1)}, bf16[1024,2,128]{2,1,0:T(2,128)(2,1)}, u32[]{:S(2)}, u32[]{:S(2)}) collective-permute-start(bf16[1024,2,128]{2,1,0:T(2,128)(2,1)} %convert_element_type.45), channel_id=1, source_target_pairs={{8,0},{16,8},{24,16},{32,24},{40,32},{48,40},{56,48},{64,56},{72,6... | collective-permute-start | bytes 1572872 | tf_op jit(solution)/shard_map/ppermute | solution.py:87
  112.6 1.2 copy-start.2
  114.1 1.6 copy-start.3
  118.6 4.9 %copy-start.5 = (f32[1024,2,128]{2,1,0:T(2,128)S(1)}, f32[1024,2,128]{2,1,0:T(2,128)}, u32[]{:S(2)}) copy-start(f32[1024,2,128]{2,1,0:T(2,128)} %slice.69) | copy-start | bytes 3145732
  122.0 3.4 %copy-start.4 = (bf16[1024,512]{1,0:T(8,128)(2,1)S(1)}, bf16[1024,512]{1,0:T(8,128)(2,1)}, u32[]{:S(2)}) copy-start(bf16[1024,512]{1,0:T(8,128)(2,1)} %fusion.7) | copy-start | bytes 3145732
  127.3 37.9 %copy-start.6 = (bf16[2,4,128,1024]{3,2,0,1:T(8,128)(2,1)}, bf16[2,4,128,1024]{3,2,0,1:T(8,128)(2,1)S(1)}, u32[]{:S(2)}) copy-start(bf16[2,4,128,1024]{3,2,0,1:T(8,128)(2,1)S(1)} %copy.53) | copy-start | bytes 6291460
  156.3 9.0 %copy-start.11 = (bf16[8,128,5376]{2,1,0:T(8,128)(2,1)S(1)}, bf16[8,128,5376]{2,1,0:T(8,128)(2,1)}, u32[]{:S(2)}) copy-start(bf16[8,128,5376]{2,1,0:T(8,128)(2,1)} %all-gather.3.cloned.1.call-done) | copy-start | bytes 33030148
  165.2 9.1 %collective-permute-start.5 = (bf16[2688,1024]{1,0:T(8,128)(2,1)S(1)}, bf16[2688,1024]{1,0:T(8,128)(2,1)S(1)}, u32[]{:S(2)}, u32[]{:S(2)}) collective-permute-start(bf16[2688,1024]{1,0:T(8,128)(2,1)S(1)} %convolution_convert_fusion), channel_id=1, source_target_pairs={{0,8},{8,0},{16,24},{24,16},{32,40},{40,32},{48,56},{56,48},{64,72... | collective-permute-start | bytes 16515080 | tf_op jit(solution)/shard_map/ppermute | solution.py:218
  249.7 31.7 %all-to-all-start = ((bf16[16,64,1024]{2,1,0:T(8,128)(2,1)}), bf16[16,64,1024]{2,1,0:T(8,128)(2,1)S(1)}, u32[]{:S(2)}, u32[]{:S(2)}) async-start(bf16[16,64,1024]{2,1,0:T(8,128)(2,1)} %broadcast_select_fusion), calls=%async_computation.1 | async-start | bytes 4194304 | tf_op jit(solution)/shard_map/all_to_all | solution.py:137
Sparse Core Ops, SparseCore 0:
  49.3 106.9 all-gather.2
  179.7 66.5 reduce-scatter.1

commit v11 on v9

--- a/solution.py
+++ b/solution.py
@@ -133,7 +133,7 @@
         ),
         1,
     )
-    send = jnp.take(mine, dest_block, axis=0)
+    send = jnp.take(mine, dest_block, axis=0, mode="clip")
     received = lax.all_to_all(send, "seq", 0, 0, tiled=False)
     main_block = received.reshape(BLOCK, columns)
     tail_block = jnp.concatenate(

time: 298 us -> 298 us (level)
  no operation moved by 1% of the time
where the time goes in v11:
time: 298 us; the launch traced here: 297 us
  waiting for transfers between devices  153 us (51%)
  other arithmetic  29.6 us (10%)
  local copies, waits for them, and re-layouts  29.3 us (10%)
  Pallas kernels  27.4 us (9%)
  matrix products  25.7 us (9%)
  starting transfers between devices  16.2 us (5%)
  between operations  15.1 us (5%)
    reduce_scatter x1, waiting for transfers between devices, per_device(): lax.psum_scatter(summed, 'seq', scatter_dimension=0, tiled=True, axis_ind...  65.3 us
    ppermute x1, waiting for transfers between devices, per_device(): lax.ppermute(local, 'head', [(src, (src + lane_count) % head_count) for s...  30.2 us
    all_gather x1, waiting for transfers between devices, per_device(): lax.all_gather(pair, 'head', axis=0, tiled=False, axis_index_groups=lanes)  28.9 us
    pallas_call x1, Pallas kernels, attention_backward(): pl.pallas_call(attention_kernel, grid=(KV_DEV,), out_shape=(jax.ShapeDtyp...  27.4 us
    all_to_all x1, waiting for transfers between devices, owned_block(): received = lax.all_to_all(send, 'seq', 0, 0, tiled=False)  27.3 us
    dot_general x1, matrix products, per_device(): lax.dot_general(gathered[:, :half], column_grads, (((0,), (0,)), ((), ())...  8.87 us
    ppermute x4, starting transfers between devices, shifted(): lax.ppermute(value, axis, [(source, source + steps) for source in range(i...  8.27 us
    dot_general x1, matrix products, per_device(): lax.dot_general(gathered[:, half:], column_grads, (((0,), (0,)), ((), ())...  7.99 us
  transfers between devices with their start and end apart: 9, of which 5 were waited for; matrix products, arithmetic and copies ran while one was open for 17% of the time, Pallas kernels for 9%

profile of v11, /device:TPU:0, one launch (start us, length us, event | category | flops | bytes accessed | tf_op | source)
XLA Modules:
  0.0 296.6 jit_solution(6132928698615947826)
XLA Ops:
  7.2 1.2 slice-done
  9.7 4.1 %collective-permute-start = (bf16[128,5376]{0,1:T(8,128)(2,1)S(1)}, bf16[128,5376]{0,1:T(8,128)(2,1)S(1)}, u32[]{:S(2)}, u32[]{:S(2)}) collective-permute-start(bf16[128,5376]{0,1:T(8,128)(2,1)S(1)} %bitcast.48), channel_id=1, source_target_pairs={{0,4},{1,5},{2,6},{3,7},{4,0},{5,1},{6,2},{7,3},{8,12},{9,13},{10,... | collective-permute-start | bytes 4128776 | tf_op jit(solution)/shard_map/ppermute | solution.py:197
  13.8 30.2 %collective-permute-done = bf16[128,5376]{0,1:T(8,128)(2,1)S(1)} collective-permute-done((bf16[128,5376]{0,1:T(8,128)(2,1)S(1)}, bf16[128,5376]{0,1:T(8,128)(2,1)S(1)}, u32[]{:S(2)}, u32[]{:S(2)}) %collective-permute-start) | collective-permute-done | bytes 1376288 | tf_op jit(solution)/shard_map/ppermute | solution.py:197
  44.2 2.7 copy.37
  47.0 1.0 copy-done.7
  48.0 1.3 collective-permute-start.1
  49.3 4.2 %collective-permute-start.2 = (bf16[1024,256]{1,0:T(8,128)(2,1)S(1)}, bf16[1024,256]{1,0:T(8,128)(2,1)S(1)}, u32[]{:S(2)}, u32[]{:S(2)}) collective-permute-start(bf16[1024,256]{1,0:T(8,128)(2,1)S(1)} %copy-done.8), channel_id=1, source_target_pairs={{0,8},{8,16},{16,24},{24,32},{32,40},{40,48},{48,56},{56,64},{64,7... | collective-permute-start | bytes 1572872 | tf_op jit(solution)/shard_map/ppermute | solution.py:87
  53.6 1.0 copy.38.band_ref
  54.6 1.9 multiply_cosine_fusion
  56.5 1.3 pad_maximum_fusion.5
  57.8 1.1 pad_maximum_fusion.3.k_ref
  58.9 1.0 pad_maximum_fusion.4.v_ref
  60.0 27.4 %shard_map.90 = (f32[1024,512]{1,0:T(8,128)}, f32[2048,256]{1,0:T(8,128)}, f32[2048,256]{1,0:T(8,128)}) custom-call(s32[1024,1]{1,0:T(8,128)} %copy.38.band_ref, bf16[1024,512]{1,0:T(8,128)(2,1)} %q_ref.1, bf16[1024,512]{1,0:T(8,128)(2,1)} %do_ref.1, bf16[2048,256]{1,0:T(8,128)(2,1)} %pad_maximum_fusion.3.k_ref, bf16[2048,256]{1,0:T(8,128)(2,1)} %pad_maximum_fusion.4.v_ref), custom_call_target="tpu_custom_call" | custom-call | tf_op jit(solution)/shard_map/pallas_call | solution.py:71
  87.4 2.5 slice.56
  89.9 2.2 slice.84
  92.1 1.1 slice.61
  93.2 0.9 slice.83
  94.1 1.7 reshape.79
  95.8 1.8 slice.57
  97.5 2.0 convert_element_type.43
  99.5 1.3 collective-permute-start.3
  100.8 2.7 slice.62
  103.5 2.0 convert_element_type.45
  105.5 1.5 collective-permute-start.4
  107.0 2.2 broadcast_multiply_fusion
  109.2 1.2 slice_negate_fusion
  110.4 1.1 pad_maximum_fusion.1
  112.0 1.6 fusion.7
  113.6 1.8 fusion.13
  115.3 1.1 slice_negate_fusion.1
  116.5 3.4 %fusion.8 = bf16[1024,2,128]{2,1,0:T(2,128)(2,1)} fusion(f32[1024,2,64]{2,1,0:T(2,128)S(1)} %get-tuple-element.62, f32[1024,2,64]{2,1,0:T(2,128)S(1)} %get-tuple-element.61, f32[1024,2,128]{2,1,0:T(2,128)S(1)} %slice.57, bf16[1024,2,128]{2,1,0:T(2,128)(2,1)} %collective-permute-done.3, f32[1024,128]{1,0:T(8,128)S(1)} %copy-done.1), kind=kLoop, calls=%fused_computation.38 | loop fusion | flops 1572864 | bytes 3670016 | tf_op jit(solution)/shard_map/convert.4
  119.9 1.5 concatenate.63
  121.4 1.6 add_convert_fusion.1
  123.3 1.7 fusion.4
  125.2 28.9 %all-gather.3.cloned.1.call-done = bf16[8,128,5376]{2,1,0:T(8,128)(2,1)} async-done(((bf16[2,128,5376]{2,1,0:T(8,128)(2,1)}), bf16[8,128,5376]{2,1,0:T(8,128)(2,1)}) %all-gather.3.cloned.1.call-update) | async-done | bytes 11010064 | tf_op jit(solution)/shard_map/all_gather | solution.py:203
  154.1 8.9 %convolution_convert_fusion = bf16[2688,1024]{1,0:T(8,128)(2,1)S(1)} fusion(bf16[1024,1024]{1,0:T(8,128)(2,1)S(1)} %bitcast.54, bf16[1024,5376]{1,0:T(8,128)(2,1)} %bitcast.59), kind=kOutput, calls=%fused_computation.6 | convolution fusion | flops 5639897088 | bytes 13107200 | tf_op jit(solution)/shard_map/dot_general | solution.py:209
  163.1 8.0 %convolution_convert_fusion.1 = bf16[2688,1024]{1,0:T(8,128)(2,1)S(1)} fusion(bf16[1024,1024]{1,0:T(8,128)(2,1)} %bitcast.55, bf16[1024,5376]{1,0:T(8,128)(2,1)S(1)} %bitcast.60), kind=kOutput, calls=%fused_computation.7 | convolution fusion | flops 5639897088 | bytes 13107200 | tf_op jit(solution)/shard_map/dot_general | solution.py:214
  171.1 1.0 collective-permute-done.5
  172.1 5.2 %add_convert_fusion = bf16[2688,1024]{1,0:T(8,128)(2,1)} fusion(bf16[2688,1024]{1,0:T(8,128)(2,1)S(1)} %collective-permute-done.5, bf16[2688,1024]{1,0:T(8,128)(2,1)S(1)} %convolution_convert_fusion.1), kind=kLoop, calls=%fused_computation.5 | loop fusion | flops 11010048 | bytes 16515072 | tf_op jit(solution)/shard_map/convert_element_type | solution.py:219
  177.3 1.3 fusion.15
  178.7 65.3 %reduce-scatter.2.cloned.1.call-done = bf16[336,1024]{1,0:T(8,128)(2,1)} async-done(((bf16[2688,1024]{1,0:T(8,128)(2,1)}), bf16[336,1024]{1,0:T(8,128)(2,1)}) %reduce-scatter.2.cloned.1.call-update) | async-done | bytes 688144 | tf_op jit(solution)/shard_map/reduce_scatter | solution.py:221
  244.0 1.2 concatenate.67
  245.2 2.0 gather_fusion
  247.2 3.7 %all-to-all-start = ((bf16[16,64,1024]{2,1,0:T(8,128)(2,1)}), bf16[16,64,1024]{2,1,0:T(8,128)(2,1)S(1)}, u32[]{:S(2)}, u32[]{:S(2)}) async-start(bf16[16,64,1024]{2,1,0:T(8,128)(2,1)} %gather_fusion), calls=%async_computation.1 | async-start | bytes 4194304 | tf_op jit(solution)/shard_map/all_to_all | solution.py:137
  251.5 27.3 %all-to-all-done = bf16[16,64,1024]{2,1,0:T(8,128)(2,1)S(1)} async-done(((bf16[16,64,1024]{2,1,0:T(8,128)(2,1)}), bf16[16,64,1024]{2,1,0:T(8,128)(2,1)S(1)}, u32[]{:S(2)}, u32[]{:S(2)}) %all-to-all-start) | async-done | bytes 2097184 | tf_op jit(solution)/shard_map/all_to_all | solution.py:137
  278.9 10.9 %conditional.1 = (f32[1,1,1024,1024]{3,2,1,0:T(8,128)}, f32[1,1,1024,1024]{3,2,1,0:T(8,128)}) conditional(s32[]{:T(128)} %convert_element_type.41, () %tuple.27, (pred[6]{0:T(512)(128)(4,1)S(1)}, s32[6]{0:T(128)S(1)}, bf16[16,64,1024]{2,1,0:T(8,128)(2,1)S(1)}) %tuple.29), branch_computations={%region_3.4_spmd, %region_4.6_spmd} | conditional | flops 4298113024 | bytes 18350140 | solution.py:249
  280.9 4.4 %multiply_bitcast_fusion.1 = f32[1,1,1024,1024]{3,2,1,0:T(8,128)} fusion(bf16[1024,1024]{1,0:T(8,128)(2,1)S(1)} %bitcast_select_fusion), kind=kOutput, calls=%fused_computation.2 | convolution fusion | flops 2148532224 | bytes 6291456 | tf_op jit(solution)/shard_map/cond/branch_1_fun/dot_general | solution.py:230
  285.3 4.4 %multiply_bitcast_fusion = f32[1,1,1024,1024]{3,2,1,0:T(8,128)} fusion(bf16[1024,1024]{1,0:T(8,128)(2,1)S(1)} %bitcast_select_fusion), kind=kOutput, calls=%fused_computation.1 | convolution fusion | flops 2148532224 | bytes 6291456 | tf_op jit(solution)/shard_map/cond/branch_1_fun/dot_general | solution.py:236
  (51 shorter events, 4.1 us)
Async XLA Ops:
  7.2 1.3 slice-start
  7.2 146.9 %all-gather.3.cloned.1.call-start = ((), (), s32[]{:S(2)}) async-start(), calls=%async_computation.3 | async-start | bytes 13762560 | tf_op jit(solution)/shard_map/all_gather | solution.py:203
  8.5 0.9 slice-start.1
  9.7 34.2 %collective-permute-start = (bf16[128,5376]{0,1:T(8,128)(2,1)S(1)}, bf16[128,5376]{0,1:T(8,128)(2,1)S(1)}, u32[]{:S(2)}, u32[]{:S(2)}) collective-permute-start(bf16[128,5376]{0,1:T(8,128)(2,1)S(1)} %bitcast.48), channel_id=1, source_target_pairs={{0,4},{1,5},{2,6},{3,7},{4,0},{5,1},{6,2},{7,3},{8,12},{9,13},{10,... | collective-permute-start | bytes 4128776 | tf_op jit(solution)/shard_map/ppermute | solution.py:197
  46.9 1.0 copy-start.7
  46.9 2.4 copy-start.8
  46.9 6.6 %copy-start.9 = (s32[1024]{0:T(1024)S(1)}, s32[1024]{0:T(1024)}, u32[]{:S(2)}) copy-start(s32[1024]{0:T(1024)} %param.14) | copy-start | bytes 12292
  47.0 197.0 %reduce-scatter.2.cloned.1.call-start = ((), (), s32[]{:S(2)}) async-start(), calls=%async_computation.2 | async-start | bytes 6193152 | tf_op jit(solution)/shard_map/reduce_scatter | solution.py:221
  48.0 9.9 %collective-permute-start.1 = (bf16[1024,256]{1,0:T(8,128)(2,1)S(1)}, bf16[1024,256]{1,0:T(8,128)(2,1)S(1)}, u32[]{:S(2)}, u32[]{:S(2)}) collective-permute-start(bf16[1024,256]{1,0:T(8,128)(2,1)S(1)} %copy-done.7), channel_id=1, source_target_pairs={{0,8},{8,16},{16,24},{24,32},{32,40},{40,48},{48,56},{56,64},{64,7... | collective-permute-start | bytes 1572872 | tf_op jit(solution)/shard_map/ppermute | solution.py:87
  49.3 9.6 %collective-permute-start.2 = (bf16[1024,256]{1,0:T(8,128)(2,1)S(1)}, bf16[1024,256]{1,0:T(8,128)(2,1)S(1)}, u32[]{:S(2)}, u32[]{:S(2)}) collective-permute-start(bf16[1024,256]{1,0:T(8,128)(2,1)S(1)} %copy-done.8), channel_id=1, source_target_pairs={{0,8},{8,16},{16,24},{24,32},{32,40},{40,48},{48,56},{56,64},{64,7... | collective-permute-start | bytes 1572872 | tf_op jit(solution)/shard_map/ppermute | solution.py:87
  87.4 4.7 %copy-start.6 = (f32[2048,256]{1,0:T(8,128)S(1)}, f32[2048,256]{1,0:T(8,128)}, u32[]{:S(2)}) copy-start(f32[2048,256]{1,0:T(8,128)} %get-tuple-element.49) | copy-start | bytes 6291460
  89.9 4.2 %copy-start = (f32[1024,512]{1,0:T(8,128)S(1)}, f32[1024,512]{1,0:T(8,128)}, u32[]{:S(2)}) copy-start(f32[1024,512]{1,0:T(8,128)} %get-tuple-element.47) | copy-start | bytes 6291460
  99.5 14.0 %collective-permute-start.3 = (bf16[1024,2,128]{2,1,0:T(2,128)(2,1)}, bf16[1024,2,128]{2,1,0:T(2,128)(2,1)}, u32[]{:S(2)}, u32[]{:S(2)}) collective-permute-start(bf16[1024,2,128]{2,1,0:T(2,128)(2,1)} %convert_element_type.43), channel_id=1, source_target_pairs={{8,0},{16,8},{24,16},{32,24},{40,32},{48,40},{56,48},{64,56},{72,6... | collective-permute-start | bytes 1572872 | tf_op jit(solution)/shard_map/ppermute | solution.py:87
  105.5 15.9 %collective-permute-start.4 = (bf16[1024,2,128]{2,1,0:T(2,128)(2,1)}, bf16[1024,2,128]{2,1,0:T(2,128)(2,1)}, u32[]{:S(2)}, u32[]{:S(2)}) collective-permute-start(bf16[1024,2,128]{2,1,0:T(2,128)(2,1)} %convert_element_type.45), channel_id=1, source_target_pairs={{8,0},{16,8},{24,16},{32,24},{40,32},{48,40},{56,48},{64,56},{72,6... | collective-permute-start | bytes 1572872 | tf_op jit(solution)/shard_map/ppermute | solution.py:87
  110.4 1.2 copy-start.1
  111.9 1.6 copy-start.2
  116.5 4.9 %copy-start.4 = (f32[1024,2,128]{2,1,0:T(2,128)S(1)}, f32[1024,2,128]{2,1,0:T(2,128)}, u32[]{:S(2)}) copy-start(f32[1024,2,128]{2,1,0:T(2,128)} %slice.62) | copy-start | bytes 3145732
  119.9 3.4 %copy-start.3 = (bf16[1024,512]{1,0:T(8,128)(2,1)S(1)}, bf16[1024,512]{1,0:T(8,128)(2,1)}, u32[]{:S(2)}) copy-start(bf16[1024,512]{1,0:T(8,128)(2,1)} %fusion.7) | copy-start | bytes 3145732
  125.2 37.8 %copy-start.5 = (bf16[2,4,128,1024]{3,2,0,1:T(8,128)(2,1)}, bf16[2,4,128,1024]{3,2,0,1:T(8,128)(2,1)S(1)}, u32[]{:S(2)}) copy-start(bf16[2,4,128,1024]{3,2,0,1:T(8,128)(2,1)S(1)} %copy.46) | copy-start | bytes 6291460
  154.1 9.0 %copy-start.10 = (bf16[8,128,5376]{2,1,0:T(8,128)(2,1)S(1)}, bf16[8,128,5376]{2,1,0:T(8,128)(2,1)}, u32[]{:S(2)}) copy-start(bf16[8,128,5376]{2,1,0:T(8,128)(2,1)} %all-gather.3.cloned.1.call-done) | copy-start | bytes 33030148
  163.0 9.1 %collective-permute-start.5 = (bf16[2688,1024]{1,0:T(8,128)(2,1)S(1)}, bf16[2688,1024]{1,0:T(8,128)(2,1)S(1)}, u32[]{:S(2)}, u32[]{:S(2)}) collective-permute-start(bf16[2688,1024]{1,0:T(8,128)(2,1)S(1)} %convolution_convert_fusion), channel_id=1, source_target_pairs={{0,8},{8,0},{16,24},{24,16},{32,40},{40,32},{48,56},{56,48},{64,72... | collective-permute-start | bytes 16515080 | tf_op jit(solution)/shard_map/ppermute | solution.py:213
  247.2 31.7 %all-to-all-start = ((bf16[16,64,1024]{2,1,0:T(8,128)(2,1)}), bf16[16,64,1024]{2,1,0:T(8,128)(2,1)S(1)}, u32[]{:S(2)}, u32[]{:S(2)}) async-start(bf16[16,64,1024]{2,1,0:T(8,128)(2,1)} %gather_fusion), calls=%async_computation.1 | async-start | bytes 4194304 | tf_op jit(solution)/shard_map/all_to_all | solution.py:137
Sparse Core Ops, SparseCore 0:
  47.1 106.9 all-gather.2
  177.4 66.5 reduce-scatter.1

commit v12 on v11

--- a/solution.py
+++ b/solution.py
@@ -121,9 +121,6 @@
     piece = BLOCK // seq_count
     tail_piece = (D - full_blocks * BLOCK) // seq_count
     columns = mine.shape[1]
-    mine = jnp.concatenate(
-        [mine, jnp.zeros((NBLK * piece - mine.shape[0], columns), mine.dtype)], 0
-    ).reshape(NBLK, piece, columns)
     destinations = jnp.arange(seq_count, dtype=jnp.int32)
     dest_block = jnp.sum(
         jnp.where(
@@ -133,7 +130,8 @@
         ),
         1,
     )
-    send = jnp.take(mine, dest_block, axis=0, mode="clip")
+    rows = dest_block[:, None] * piece + jnp.arange(piece, dtype=jnp.int32)[None, :]
+    send = jnp.take(mine, rows, axis=0, mode="clip")
     received = lax.all_to_all(send, "seq", 0, 0, tiled=False)
     main_block = received.reshape(BLOCK, columns)
     tail_block = jnp.concatenate(

time: 298 us -> 302 us (1.013)
  local copies, waits for them, and re-layouts: 29.3 us -> 33.4 us
    gather x1, local copies, waits for them, and re-layouts: 2 us -> 7.19 us  [owned_block(): send = jnp.take(mine, rows, axis=0, mode='clip')]
where the time goes in v12:
time: 302 us; the launch traced here: 301 us
  waiting for transfers between devices  152 us (50%)
  local copies, waits for them, and re-layouts  33.4 us (11%)
  other arithmetic  29.8 us (10%)
  Pallas kernels  27.4 us (9%)
  matrix products  25.7 us (9%)
  starting transfers between devices  16.5 us (5%)
  between operations  15.1 us (5%)
    reduce_scatter x1, waiting for transfers between devices, per_device(): lax.psum_scatter(summed, 'seq', scatter_dimension=0, tiled=True, axis_ind...  65.1 us
    ppermute x1, waiting for transfers between devices, per_device(): lax.ppermute(local, 'head', [(src, (src + lane_count) % head_count) for s...  30.2 us
    all_gather x1, waiting for transfers between devices, per_device(): lax.all_gather(pair, 'head', axis=0, tiled=False, axis_index_groups=lanes)  28.7 us
    pallas_call x1, Pallas kernels, attention_backward(): pl.pallas_call(attention_kernel, grid=(KV_DEV,), out_shape=(jax.ShapeDtyp...  27.4 us
    all_to_all x1, waiting for transfers between devices, owned_block(): received = lax.all_to_all(send, 'seq', 0, 0, tiled=False)  27.3 us
    dot_general x1, matrix products, per_device(): lax.dot_general(gathered[:, :half], column_grads, (((0,), (0,)), ((), ())...  8.87 us
    ppermute x4, starting transfers between devices, shifted(): lax.ppermute(value, axis, [(source, source + steps) for source in range(i...  8.27 us
    dot_general x1, matrix products, per_device(): lax.dot_general(gathered[:, half:], column_grads, (((0,), (0,)), ((), ())...  7.99 us
  transfers between devices with their start and end apart: 9, of which 5 were waited for; matrix products, arithmetic and copies ran while one was open for 17% of the time, Pallas kernels for 9%

profile of v12, /device:TPU:0, one launch (start us, length us, event | category | flops | bytes accessed | tf_op | source)
XLA Modules:
  0.0 300.9 jit_solution(17426658921561195680)
XLA Ops:
  7.2 1.2 slice-done
  8.5 0.8 copy.44
  9.7 4.1 %collective-permute-start = (bf16[128,5376]{0,1:T(8,128)(2,1)S(1)}, bf16[128,5376]{0,1:T(8,128)(2,1)S(1)}, u32[]{:S(2)}, u32[]{:S(2)}) collective-permute-start(bf16[128,5376]{0,1:T(8,128)(2,1)S(1)} %bitcast.50), channel_id=1, source_target_pairs={{0,4},{1,5},{2,6},{3,7},{4,0},{5,1},{6,2},{7,3},{8,12},{9,13},{10,... | collective-permute-start | bytes 4128776 | tf_op jit(solution)/shard_map/ppermute | solution.py:195
  13.8 30.2 %collective-permute-done = bf16[128,5376]{0,1:T(8,128)(2,1)S(1)} collective-permute-done((bf16[128,5376]{0,1:T(8,128)(2,1)S(1)}, bf16[128,5376]{0,1:T(8,128)(2,1)S(1)}, u32[]{:S(2)}, u32[]{:S(2)}) %collective-permute-start) | collective-permute-done | bytes 1376288 | tf_op jit(solution)/shard_map/ppermute | solution.py:195
  44.2 2.7 copy.37
  47.0 1.0 copy-done.7
  48.0 1.3 collective-permute-start.1
  49.3 4.2 %collective-permute-start.2 = (bf16[1024,256]{1,0:T(8,128)(2,1)S(1)}, bf16[1024,256]{1,0:T(8,128)(2,1)S(1)}, u32[]{:S(2)}, u32[]{:S(2)}) collective-permute-start(bf16[1024,256]{1,0:T(8,128)(2,1)S(1)} %copy-done.8), channel_id=1, source_target_pairs={{0,8},{8,16},{16,24},{24,32},{32,40},{40,48},{48,56},{56,64},{64,7... | collective-permute-start | bytes 1572872 | tf_op jit(solution)/shard_map/ppermute | solution.py:87
  53.6 1.0 copy.38.band_ref
  54.6 1.9 multiply_cosine_fusion
  56.5 1.3 pad_maximum_fusion.5
  57.8 1.1 pad_maximum_fusion.3.k_ref
  58.9 1.0 pad_maximum_fusion.4.v_ref
  60.0 27.4 %shard_map.90 = (f32[1024,512]{1,0:T(8,128)}, f32[2048,256]{1,0:T(8,128)}, f32[2048,256]{1,0:T(8,128)}) custom-call(s32[1024,1]{1,0:T(8,128)} %copy.38.band_ref, bf16[1024,512]{1,0:T(8,128)(2,1)} %q_ref.1, bf16[1024,512]{1,0:T(8,128)(2,1)} %do_ref.1, bf16[2048,256]{1,0:T(8,128)(2,1)} %pad_maximum_fusion.3.k_ref, bf16[2048,256]{1,0:T(8,128)(2,1)} %pad_maximum_fusion.4.v_ref), custom_call_target="tpu_custom_call" | custom-call | tf_op jit(solution)/shard_map/pallas_call | solution.py:71
  87.4 2.5 slice.56
  89.9 2.2 slice.84
  92.1 1.1 slice.61
  93.2 0.9 slice.83
  94.1 1.7 reshape.110
  95.8 1.8 slice.57
  97.5 2.0 convert_element_type.43
  99.5 1.3 collective-permute-start.3
  100.8 2.7 slice.62
  103.5 2.0 convert_element_type.45
  105.5 1.5 collective-permute-start.4
  107.0 2.2 broadcast_multiply_fusion
  109.2 1.2 slice_negate_fusion
  110.4 1.1 pad_maximum_fusion.1
  112.0 1.6 fusion.7
  113.6 1.8 fusion.13
  115.3 1.1 slice_negate_fusion.1
  116.5 3.6 %fusion.8 = bf16[1024,2,128]{2,1,0:T(2,128)(2,1)} fusion(f32[1024,2,64]{2,1,0:T(2,128)S(1)} %get-tuple-element.60, f32[1024,2,64]{2,1,0:T(2,128)S(1)} %get-tuple-element.59, f32[1024,2,128]{2,1,0:T(2,128)S(1)} %slice.57, bf16[1024,2,128]{2,1,0:T(2,128)(2,1)} %collective-permute-done.3, f32[1024,128]{1,0:T(8,128)S(1)} %copy-done.1), kind=kLoop, calls=%fused_computation.38 | loop fusion | flops 1572864 | bytes 3670016 | tf_op jit(solution)/shard_map/convert.4
  120.1 1.5 concatenate.60
  121.6 1.6 add_convert_fusion.1
  123.5 1.7 fusion.4
  125.4 28.7 %all-gather.3.cloned.1.call-done = bf16[8,128,5376]{2,1,0:T(8,128)(2,1)} async-done(((bf16[2,128,5376]{2,1,0:T(8,128)(2,1)}), bf16[8,128,5376]{2,1,0:T(8,128)(2,1)}) %all-gather.3.cloned.1.call-update) | async-done | bytes 11010064 | tf_op jit(solution)/shard_map/all_gather | solution.py:201
  154.1 8.9 %convolution_convert_fusion = bf16[2688,1024]{1,0:T(8,128)(2,1)S(1)} fusion(bf16[1024,1024]{1,0:T(8,128)(2,1)S(1)} %bitcast.56, bf16[1024,5376]{1,0:T(8,128)(2,1)} %bitcast.61), kind=kOutput, calls=%fused_computation.6 | convolution fusion | flops 5639897088 | bytes 13107200 | tf_op jit(solution)/shard_map/dot_general | solution.py:207
  163.1 8.0 %convolution_convert_fusion.1 = bf16[2688,1024]{1,0:T(8,128)(2,1)S(1)} fusion(bf16[1024,1024]{1,0:T(8,128)(2,1)} %bitcast.57, bf16[1024,5376]{1,0:T(8,128)(2,1)S(1)} %bitcast.62), kind=kOutput, calls=%fused_computation.7 | convolution fusion | flops 5639897088 | bytes 13107200 | tf_op jit(solution)/shard_map/dot_general | solution.py:212
  171.1 1.0 collective-permute-done.5
  172.1 5.2 %add_convert_fusion = bf16[2688,1024]{1,0:T(8,128)(2,1)} fusion(bf16[2688,1024]{1,0:T(8,128)(2,1)S(1)} %collective-permute-done.5, bf16[2688,1024]{1,0:T(8,128)(2,1)S(1)} %convolution_convert_fusion.1), kind=kLoop, calls=%fused_computation.5 | loop fusion | flops 11010048 | bytes 16515072 | tf_op jit(solution)/shard_map/convert_element_type | solution.py:217
  177.3 1.3 fusion.15
  178.9 65.1 %reduce-scatter.2.cloned.1.call-done = bf16[336,1024]{1,0:T(8,128)(2,1)} async-done(((bf16[2688,1024]{1,0:T(8,128)(2,1)}), bf16[336,1024]{1,0:T(8,128)(2,1)}) %reduce-scatter.2.cloned.1.call-update) | async-done | bytes 688144 | tf_op jit(solution)/shard_map/reduce_scatter | solution.py:219
  244.0 7.2 %gather_fusion = bf16[1024,1024]{1,0:T(8,128)(2,1)} fusion(bf16[336,1024]{1,0:T(8,128)(2,1)} %reduce-scatter.2.cloned.1.call-done, s32[1024]{0:T(1024)S(1)} %broadcast_clamp_fusion), kind=kCustom, calls=%fused_computation | custom fusion | bytes 4198400 | tf_op jit(solution)/shard_map/jit(_take)/gather | solution.py:134
  251.2 4.0 %all-to-all-start = ((bf16[16,64,1024]{2,1,0:T(8,128)(2,1)}), bf16[16,64,1024]{2,1,0:T(8,128)(2,1)S(1)}, u32[]{:S(2)}, u32[]{:S(2)}) async-start(bf16[16,64,1024]{2,1,0:T(8,128)(2,1)} %bitcast.49), calls=%async_computation.1 | async-start | bytes 4194304 | tf_op jit(solution)/shard_map/all_to_all | solution.py:135
  255.8 27.3 %all-to-all-done = bf16[16,64,1024]{2,1,0:T(8,128)(2,1)S(1)} async-done(((bf16[16,64,1024]{2,1,0:T(8,128)(2,1)}), bf16[16,64,1024]{2,1,0:T(8,128)(2,1)S(1)}, u32[]{:S(2)}, u32[]{:S(2)}) %all-to-all-start) | async-done | bytes 2097184 | tf_op jit(solution)/shard_map/all_to_all | solution.py:135
  283.1 10.9 %conditional.1 = (f32[1,1,1024,1024]{3,2,1,0:T(8,128)}, f32[1,1,1024,1024]{3,2,1,0:T(8,128)}) conditional(s32[]{:T(128)} %convert_element_type.41, () %tuple.33, (pred[6]{0:T(512)(128)(4,1)S(1)}, s32[6]{0:T(128)S(1)}, bf16[16,64,1024]{2,1,0:T(8,128)(2,1)S(1)}) %tuple.35), branch_computations={%region_3.4_spmd, %region_4.6_spmd} | conditional | flops 4298113024 | bytes 18350140 | solution.py:247
  285.2 4.4 %multiply_bitcast_fusion.1 = f32[1,1,1024,1024]{3,2,1,0:T(8,128)} fusion(bf16[1024,1024]{1,0:T(8,128)(2,1)S(1)} %bitcast_select_fusion), kind=kOutput, calls=%fused_computation.2 | convolution fusion | flops 2148532224 | bytes 6291456 | tf_op jit(solution)/shard_map/cond/branch_1_fun/dot_general | solution.py:228
  289.6 4.4 %multiply_bitcast_fusion = f32[1,1,1024,1024]{3,2,1,0:T(8,128)} fusion(bf16[1024,1024]{1,0:T(8,128)(2,1)S(1)} %bitcast_select_fusion), kind=kOutput, calls=%fused_computation.1 | convolution fusion | flops 2148532224 | bytes 6291456 | tf_op jit(solution)/shard_map/cond/branch_1_fun/dot_general | solution.py:234
  (53 shorter events, 3.5 us)
Async XLA Ops:
  7.2 1.3 slice-start
  7.2 146.9 %all-gather.3.cloned.1.call-start = ((), (), s32[]{:S(2)}) async-start(), calls=%async_computation.3 | async-start | bytes 13762560 | tf_op jit(solution)/shard_map/all_gather | solution.py:201
  8.5 0.9 slice-start.1
  9.7 34.2 %collective-permute-start = (bf16[128,5376]{0,1:T(8,128)(2,1)S(1)}, bf16[128,5376]{0,1:T(8,128)(2,1)S(1)}, u32[]{:S(2)}, u32[]{:S(2)}) collective-permute-start(bf16[128,5376]{0,1:T(8,128)(2,1)S(1)} %bitcast.50), channel_id=1, source_target_pairs={{0,4},{1,5},{2,6},{3,7},{4,0},{5,1},{6,2},{7,3},{8,12},{9,13},{10,... | collective-permute-start | bytes 4128776 | tf_op jit(solution)/shard_map/ppermute | solution.py:195
  46.9 1.0 copy-start.7
  46.9 2.4 copy-start.8
  46.9 6.6 %copy-start.9 = (s32[1024]{0:T(1024)S(1)}, s32[1024]{0:T(1024)}, u32[]{:S(2)}) copy-start(s32[1024]{0:T(1024)} %param.14) | copy-start | bytes 12292
  47.0 197.0 %reduce-scatter.2.cloned.1.call-start = ((), (), s32[]{:S(2)}) async-start(), calls=%async_computation.2 | async-start | bytes 6193152 | tf_op jit(solution)/shard_map/reduce_scatter | solution.py:219
  48.0 9.9 %collective-permute-start.1 = (bf16[1024,256]{1,0:T(8,128)(2,1)S(1)}, bf16[1024,256]{1,0:T(8,128)(2,1)S(1)}, u32[]{:S(2)}, u32[]{:S(2)}) collective-permute-start(bf16[1024,256]{1,0:T(8,128)(2,1)S(1)} %copy-done.7), channel_id=1, source_target_pairs={{0,8},{8,16},{16,24},{24,32},{32,40},{40,48},{48,56},{56,64},{64,7... | collective-permute-start | bytes 1572872 | tf_op jit(solution)/shard_map/ppermute | solution.py:87
  49.3 9.6 %collective-permute-start.2 = (bf16[1024,256]{1,0:T(8,128)(2,1)S(1)}, bf16[1024,256]{1,0:T(8,128)(2,1)S(1)}, u32[]{:S(2)}, u32[]{:S(2)}) collective-permute-start(bf16[1024,256]{1,0:T(8,128)(2,1)S(1)} %copy-done.8), channel_id=1, source_target_pairs={{0,8},{8,16},{16,24},{24,32},{32,40},{40,48},{48,56},{56,64},{64,7... | collective-permute-start | bytes 1572872 | tf_op jit(solution)/shard_map/ppermute | solution.py:87
  87.4 4.7 %copy-start.6 = (f32[2048,256]{1,0:T(8,128)S(1)}, f32[2048,256]{1,0:T(8,128)}, u32[]{:S(2)}) copy-start(f32[2048,256]{1,0:T(8,128)} %get-tuple-element.47) | copy-start | bytes 6291460
  89.9 4.2 %copy-start = (f32[1024,512]{1,0:T(8,128)S(1)}, f32[1024,512]{1,0:T(8,128)}, u32[]{:S(2)}) copy-start(f32[1024,512]{1,0:T(8,128)} %get-tuple-element.45) | copy-start | bytes 6291460
  99.5 14.0 %collective-permute-start.3 = (bf16[1024,2,128]{2,1,0:T(2,128)(2,1)}, bf16[1024,2,128]{2,1,0:T(2,128)(2,1)}, u32[]{:S(2)}, u32[]{:S(2)}) collective-permute-start(bf16[1024,2,128]{2,1,0:T(2,128)(2,1)} %convert_element_type.43), channel_id=1, source_target_pairs={{8,0},{16,8},{24,16},{32,24},{40,32},{48,40},{56,48},{64,56},{72,6... | collective-permute-start | bytes 1572872 | tf_op jit(solution)/shard_map/ppermute | solution.py:87
  105.5 16.1 %collective-permute-start.4 = (bf16[1024,2,128]{2,1,0:T(2,128)(2,1)}, bf16[1024,2,128]{2,1,0:T(2,128)(2,1)}, u32[]{:S(2)}, u32[]{:S(2)}) collective-permute-start(bf16[1024,2,128]{2,1,0:T(2,128)(2,1)} %convert_element_type.45), channel_id=1, source_target_pairs={{8,0},{16,8},{24,16},{32,24},{40,32},{48,40},{56,48},{64,56},{72,6... | collective-permute-start | bytes 1572872 | tf_op jit(solution)/shard_map/ppermute | solution.py:87
  110.4 1.2 copy-start.1
  111.9 1.6 copy-start.2
  116.5 5.1 %copy-start.4 = (f32[1024,2,128]{2,1,0:T(2,128)S(1)}, f32[1024,2,128]{2,1,0:T(2,128)}, u32[]{:S(2)}) copy-start(f32[1024,2,128]{2,1,0:T(2,128)} %slice.62) | copy-start | bytes 3145732
  120.1 3.4 %copy-start.3 = (bf16[1024,512]{1,0:T(8,128)(2,1)S(1)}, bf16[1024,512]{1,0:T(8,128)(2,1)}, u32[]{:S(2)}) copy-start(bf16[1024,512]{1,0:T(8,128)(2,1)} %fusion.7) | copy-start | bytes 3145732
  125.4 37.6 %copy-start.5 = (bf16[2,4,128,1024]{3,2,0,1:T(8,128)(2,1)}, bf16[2,4,128,1024]{3,2,0,1:T(8,128)(2,1)S(1)}, u32[]{:S(2)}) copy-start(bf16[2,4,128,1024]{3,2,0,1:T(8,128)(2,1)S(1)} %copy.46) | copy-start | bytes 6291460
  154.1 9.0 %copy-start.10 = (bf16[8,128,5376]{2,1,0:T(8,128)(2,1)S(1)}, bf16[8,128,5376]{2,1,0:T(8,128)(2,1)}, u32[]{:S(2)}) copy-start(bf16[8,128,5376]{2,1,0:T(8,128)(2,1)} %all-gather.3.cloned.1.call-done) | copy-start | bytes 33030148
  163.0 9.1 %collective-permute-start.5 = (bf16[2688,1024]{1,0:T(8,128)(2,1)S(1)}, bf16[2688,1024]{1,0:T(8,128)(2,1)S(1)}, u32[]{:S(2)}, u32[]{:S(2)}) collective-permute-start(bf16[2688,1024]{1,0:T(8,128)(2,1)S(1)} %convolution_convert_fusion), channel_id=1, source_target_pairs={{0,8},{8,0},{16,24},{24,16},{32,40},{40,32},{48,56},{56,48},{64,72... | collective-permute-start | bytes 16515080 | tf_op jit(solution)/shard_map/ppermute | solution.py:211
  251.2 31.9 %all-to-all-start = ((bf16[16,64,1024]{2,1,0:T(8,128)(2,1)}), bf16[16,64,1024]{2,1,0:T(8,128)(2,1)S(1)}, u32[]{:S(2)}, u32[]{:S(2)}) async-start(bf16[16,64,1024]{2,1,0:T(8,128)(2,1)} %bitcast.49), calls=%async_computation.1 | async-start | bytes 4194304 | tf_op jit(solution)/shard_map/all_to_all | solution.py:135
Sparse Core Ops, SparseCore 0:
  47.1 106.9 all-gather.2
  177.4 66.5 reduce-scatter.1
